TPU v7x, 128 devices: a whole 4x4x4 slice. The times are simulated.
128 devices in a mesh: tok: 16 (over x, z), row: 4 (over y), col: 2 (over core).
Axes of the slice: x: 4, y: 4, z: 4, core: 2. Of those that a mesh axis runs over, the one named last changes fastest.
Arguments:
- block_input_rows: bfloat16 [8192, 4096], P(('tok', 'row'), 'col'), may hold values from -18 to 18
- input_norm_scale: bfloat16 [4096], P('col'), may hold values from 0.6 to 10, as said below
- query_key_value_weight: bfloat16 [4096, 16, 3, 128], P('col', 'row'), may hold values from -0.09375 to 0.09375
- adapter_down_weight: bfloat16 [4096, 128], P('col'), may hold values from -0.09375 to 0.09375
- adapter_up_weight: bfloat16 [128, 16, 3, 128], P(None, 'row'), may hold values from -0.5 to 0.5
- output_projection_weight: bfloat16 [2048, 2048], P(('row', 'col')), may hold values from -0.125 to 0.125
- prompt_segment_index: int32 [8192], replicated, may hold values from 0 to 3, never falling along the last dimension, each value on 1 to 4352 neighbouring positions
- cache_owner_index: int32 [8192, 1], P('tok'), may hold values from 0 to 15; in each aligned block of 512 rows (0 to 511, 512 to 1023, ...) at most 64 rows name the same one
Outputs:
- block_output: bfloat16 [8192, 2048], P(('tok', 'row', 'col'))
- kv_cache: bfloat16 [16384, 16, 2, 128], P('tok', ('row', 'col'))
Inputs may be any that keep to these rules, and one draw needn't show every extreme that they name: `prompt_segment_index`: never falls along the tokens; every prompt holds 1 to 4352 tokens and one holds exactly 4352. `cache_owner_index`: in each aligned block of 512 tokens no owner is named by more than 64 tokens; some owner is named exactly 64 times in some block. `input_norm_scale`: positive gains.
All inputs are finite; a program needn't handle non-finite values.
Results may differ from a plain program's by a relative error of at most 0.015.
The roundings to bfloat16 on the way count: a program that leaves them out, or rounds other values in their place, can miss the bound.
Values may be sent and summed in bfloat16 or wider, within the bound.
No kernel may reach another device: no remote copies, remote signals or barrier semaphores. Data moves between devices by JAX's collectives and lax.ppermute only.
A program may use at most 192 MiB of HBM per device.

v0:
```python
import jax
import jax.numpy as jnp
from jax import lax
from jax.sharding import PartitionSpec as P

INPUT_WIDTH = 4096
HEAD_SIZE = 128
ADAPTER_RANK = 128


def fold_piece(carry, piece, query, own_seg, own_start, prompt_segment_index, scale):
    top_old, total_old, acc_old = carry
    count = piece.shape[0]
    key_pos = jnp.arange(count, dtype=jnp.int32)
    query_pos = own_start + jnp.arange(query.shape[1], dtype=jnp.int32)
    allowed = (
        (own_seg[:, None] == prompt_segment_index[None, :])
        & (key_pos[None, :] <= query_pos[:, None])
        & (key_pos[None, :] >= 0)
    )
    score = (
        jnp.einsum("htd,shd->hts", query, piece[:, :, 0], preferred_element_type=jnp.float32)
        * scale
    )
    masked = jnp.where(allowed[None], score, -1e30)
    top_new = jnp.maximum(top_old, jnp.max(masked, axis=2))
    weights = jnp.where(allowed[None], jnp.exp(score - top_new[:, :, None]), 0.0).astype(
        jnp.bfloat16
    )
    total_new = jnp.sum(weights.astype(jnp.float32), axis=2)
    acc_new = jnp.einsum(
        "hts,shd->htd", weights, piece[:, :, 1], preferred_element_type=jnp.float32
    )
    return (top_new, total_new, acc_new)


def shards(
    block_input_rows,
    input_norm_scale,
    query_key_value_weight,
    adapter_down_weight,
    adapter_up_weight,
    output_projection_weight,
    prompt_segment_index,
    cache_owner_index,
):
    gathered = lax.all_gather(block_input_rows, "row", axis=0, tiled=True)
    wide = gathered.astype(jnp.float32)
    partial_sq = jnp.sum(wide * wide, axis=1)
    total_sq = lax.psum(partial_sq, "col")
    inverse = lax.rsqrt(total_sq / INPUT_WIDTH + 1e-06)
    normalized_input = (
        wide * inverse[:, None] * input_norm_scale.astype(jnp.float32)[None, :]
    ).astype(jnp.bfloat16)
    adapter_hidden = jnp.dot(
        normalized_input, adapter_down_weight, preferred_element_type=jnp.float32
    )
    tok_dev = gathered.shape[0]
    local_head_count = query_key_value_weight.shape[1]
    flat_weight = query_key_value_weight.reshape(
        query_key_value_weight.shape[0], local_head_count, 3 * HEAD_SIZE
    )
    flattened_up_weight = adapter_up_weight.reshape(ADAPTER_RANK, local_head_count, 3 * HEAD_SIZE)
    heads_dev = local_head_count // lax.axis_size("col")
    main = jnp.einsum(
        "td,dhe->hte", normalized_input, flat_weight, preferred_element_type=jnp.float32
    )
    adapter_down_output = jnp.einsum(
        "tr,rhe->hte",
        adapter_hidden,
        flattened_up_weight.astype(jnp.float32),
        precision=lax.Precision.HIGHEST,
    )
    mixed = lax.psum_scatter(main + adapter_down_output, "col", scatter_dimension=0, tiled=True)
    qkv = mixed.astype(jnp.bfloat16).reshape(heads_dev, tok_dev, 3, HEAD_SIZE)
    query = qkv[:, :, 0]
    kv_tok = jnp.transpose(qkv[:, :, 1:3], (1, 0, 2, 3))
    own_start = lax.axis_index("tok") * tok_dev
    own_seg = lax.dynamic_slice_in_dim(prompt_segment_index, own_start, tok_dev, 0)
    scale = 1.0 / HEAD_SIZE**0.5
    init = (
        jnp.full((heads_dev, tok_dev), -1e30, jnp.float32),
        jnp.zeros((heads_dev, tok_dev), jnp.float32),
        jnp.zeros((heads_dev, tok_dev, HEAD_SIZE), jnp.float32),
    )
    state = fold_piece(
        init,
        lax.all_gather(kv_tok, "tok", axis=0, tiled=True),
        query,
        own_seg,
        own_start,
        prompt_segment_index,
        scale,
    )
    attended = (state[2] / state[1][:, :, None]).astype(jnp.bfloat16)
    attended = jnp.transpose(attended, (1, 0, 2)).reshape(tok_dev, heads_dev * HEAD_SIZE)
    block_output = lax.psum_scatter(
        jnp.dot(attended, output_projection_weight, preferred_element_type=jnp.float32).astype(
            jnp.bfloat16
        ),
        ("row", "col"),
        scatter_dimension=0,
        tiled=True,
    )
    count_tok = lax.axis_size("tok")
    capacity = max(2, 2 * tok_dev // count_tok)
    owner = cache_owner_index[:, 0]
    onehot = (owner[:, None] == jnp.arange(count_tok, dtype=jnp.int32)[None, :]).astype(jnp.int32)
    before = jnp.cumsum(onehot, axis=0) - onehot
    rank = jnp.sum(before * onehot, axis=1)
    slot = owner * capacity + rank
    selector = (jnp.arange(count_tok * capacity, dtype=jnp.int32)[:, None] == slot[None, :]).astype(
        jnp.bfloat16
    )
    outgoing = jnp.dot(
        selector,
        kv_tok.reshape(tok_dev, heads_dev * 2 * HEAD_SIZE),
        preferred_element_type=jnp.float32,
    ).astype(jnp.bfloat16)
    received = lax.all_to_all(outgoing, "tok", split_axis=0, concat_axis=0, tiled=True)
    kv_cache = received.reshape(count_tok * capacity, heads_dev, 2, HEAD_SIZE)
    return (block_output, kv_cache)


def solution(mesh):
    placed = (
        P(("tok", "row"), "col"),
        P("col"),
        P("col", "row", None, None),
        P("col", None),
        P(None, "row", None, None),
        P(("row", "col"), None),
        P(),
        P("tok", None),
    )
    return jax.shard_map(
        shards,
        mesh=mesh,
        in_specs=placed,
        out_specs=(P(("tok", "row", "col"), None), P("tok", ("row", "col"), None, None)),
        check_vma=False,
    )
```

profile of v0, /device:TPU:0, one launch (start us, length us, event | category | flops | bytes accessed | tf_op | source)
XLA Modules:
  0.0 240.3 jit_solution(15088219014091748765)
XLA Ops:
  7.2 0.0 copy-start
  7.2 0.0 all-gather.3.cloned.1.call-start
  7.2 0.7 all-gather.3.cloned.1.call-update
  7.9 0.0 reduce-scatter.3.cloned.1.call-start
  8.0 0.7 convert_element_type.38
  8.7 0.0 copy-start.3
  8.7 10.7 %copy.13 = bf16[2048,4,3,128]{0,3,2,1:T(8,128)(2,1)} copy(bf16[2048,4,3,128]{3,1,2,0:T(4,128)(2,1)} %param.10) | data formatting | bytes 12582912 | tf_op args[2]
  19.4 0.0 copy-done.3
  19.4 0.3 copy.15
  19.7 23.3 %all-gather.3.cloned.1.call-done = bf16[512,2048]{1,0:T(8,128)(2,1)} async-done(((bf16[128,2048]{1,0:T(8,128)(2,1)}), bf16[512,2048]{1,0:T(8,128)(2,1)}) %all-gather.3.cloned.1.call-update) | async-done | bytes 2097168 | tf_op jit(solution)/shard_map/all_gather | solution.py:47
  43.0 2.1 fusion.1
  45.0 2.5 %psum.7 = f32[512]{0:T(512)S(1)} all-reduce(f32[512]{0:T(512)S(1)} %fusion.1), channel_id=1, replica_groups=mesh['tok'=16,'row'=4,'col'=2] {'col'}, use_global_device_ids=true, to_apply=%region_1.0 | all-reduce | flops 512 | bytes 4096 | tf_op jit(solution)/shard_map/psum | solution.py:50
  47.5 0.0 copy-start.2
  47.5 0.0 copy-start.6
  47.5 6.4 %fusion.6 = f32[512,4,384]{2,0,1:T(8,128)S(1)} fusion(bf16[2048,4,384]{0,2,1:T(8,128)(2,1)} %bitcast.71, bf16[512,2048]{1,0:T(8,128)(2,1)} %all-gather.3.cloned.1.call-done, f32[2048]{0:T(1024)S(1)} %convert_element_type.38, f32[512]{0:T(512)S(1)} %add_rsqrt_fusion), kind=kOutput, calls=%fused_computation.16 | convolution fusion | flops 3225419776 | bytes 11544576 | tf_op jit(solution)/shard_map/td,dhe->hte/dot_general | solution.py:65
  53.9 0.0 copy-done.2
  53.9 0.0 copy-done.6
  53.9 0.8 convolution_bitcast_fusion
  54.7 3.2 %add_bitcast_fusion = f32[4,512,384]{2,1,0:T(8,128)} fusion(f32[512,4,384]{2,0,1:T(8,128)S(1)} %fusion.6, f32[512,128,1]{1,0,2:T(8,128)S(1)} %convolution_bitcast_fusion, bf16[128,4,384]{0,2,1:T(8,128)(2,1)S(1)} %bitcast.76), kind=kOutput, calls=%fused_computation.14 | convolution fusion | flops 1208745984 | bytes 6946816 | tf_op jit(solution)/shard_map/tr,rhe->hte/dot_general | solution.py:68
  57.9 0.0 copy-start.4
  57.9 0.0 reduce-scatter.3.cloned.1.call-update
  57.9 0.0 all-gather.5.cloned.1.call-start
  58.0 14.1 %reduce-scatter.3.cloned.1.call-done = f32[2,512,384]{2,1,0:T(8,128)} async-done(((f32[4,512,384]{2,1,0:T(8,128)}), f32[2,512,384]{2,1,0:T(8,128)}) %reduce-scatter.3.cloned.1.call-update) | async-done | bytes 1572880 | tf_op jit(solution)/shard_map/reduce_scatter | solution.py:74
  72.0 1.5 convert_element_type.40
  73.5 0.3 copy.17
  73.9 1.0 copy.27
  74.9 0.0 all-gather.5.cloned.1.call-update
  74.9 0.2 reduce-scatter.5.cloned.1.call-start
  75.1 0.0 copy-done.4
  75.1 0.1 dynamic_slice.3
  75.2 4.8 %fusion = pred[512,8192]{1,0:T(8,128)(4,1)} fusion(s32[512]{0:T(512)S(1)} %iota_add_fusion, s32[8192]{0:T(1024)S(1)} %copy-done.4, s32[512]{0:T(512)S(1)} %dynamic_slice.3), kind=kLoop, calls=%fused_computation.4 | loop fusion | flops 12582912 | bytes 4231168 | tf_op jit(solution)/shard_map/and | solution.py:17
  80.1 67.3 %all-gather.5.cloned.1.call-done = bf16[8192,2,2,128]{3,0,1,2:T(8,128)(2,1)} async-done(((bf16[512,2,2,128]{3,0,1,2:T(8,128)(2,1)}), bf16[8192,2,2,128]{3,0,1,2:T(8,128)(2,1)}) %all-gather.5.cloned.1.call-update) | async-done | bytes 8388624 | tf_op jit(solution)/shard_map/all_gather | solution.py:88
  147.4 17.6 %select_reduce_fusion = (f32[2,512]{1,0:T(2,128)S(1)}, f32[2,512,8192]{2,1,0:T(8,128)}) fusion(pred[512,8192]{1,0:T(8,128)(4,1)} %fusion, bf16[8192,2,2,128]{3,0,1,2:T(8,128)(2,1)} %all-gather.5.cloned.1.call-done, bf16[2,512,3,128]{1,3,2,0:T(8,128)(2,1)S(1)} %bitcast.73), kind=kOutput, calls=%fused_computation.2 | convolution fusion | flops 2172648448 | bytes 42209280 | tf_op jit(solution)/shard_map/htd,shd->hts/dot_general | solution.py:22
  164.9 0.0 copy-start.1
  164.9 16.2 %convert_reduce_fusion = f32[2,512]{1,0:T(2,128)S(1)} fusion(f32[2,512]{1,0:T(2,128)S(1)} %broadcast_maximum_fusion, f32[2,512,8192]{2,1,0:T(8,128)} %get-tuple-element.3, pred[512,8192]{1,0:T(8,128)(4,1)} %fusion), kind=kLoop, calls=%fused_computation | loop fusion | flops 50330624 | bytes 37756928 | tf_op jit(solution)/shard_map/reduce_sum | solution.py:30
  181.1 0.0 copy-done.1
  181.1 16.5 %fusion.12 = bf16[512,2,128]{0,2,1:T(8,128)(2,1)S(1)} fusion(bf16[8192,2,2,128]{3,0,1,2:T(8,128)(2,1)} %all-gather.5.cloned.1.call-done, f32[512,2]{0,1:T(2,128)S(1)} %bitcast.82, f32[2,512,8192]{2,1,0:T(8,128)} %get-tuple-element.3, f32[2,512]{1,0:T(2,128)S(1)} %broadcast_maximum_fusion, pred[512,8192]{1,0:T(8,128)(4,1)S(1)} %copy-done.1), kind=kOutput, calls=%fused_computation.23 | convolution fusion | flops 2181300224 | bytes 42213376 | tf_op jit(solution)/shard_map/hts,shd->htd/dot_general | solution.py:31
  197.6 0.0 copy-start.5
  197.7 0.0 copy-done
  197.7 2.1 convolution_convert_fusion
  199.7 0.0 reduce-scatter.5.cloned.1.call-update
  199.8 0.0 copy-done.5
  199.8 1.2 reduce-window.6
  201.0 0.2 slice_reduce_fusion
  201.2 0.1 fusion.18
  201.3 0.7 fusion.9
  202.1 22.0 %all_to_all.9 = bf16[16,64,512]{2,1,0:T(8,128)(2,1)S(1)} all-to-all(bf16[16,64,512]{2,1,0:T(8,128)(2,1)S(1)} %bitcast.77), channel_id=1, replica_groups=mesh['tok'=16,'row'=4,'col'=2] {'tok'}, dimensions={0} | all-to-all | bytes 2097152 | tf_op jit(solution)/shard_map/all_to_all | solution.py:120
  224.1 1.1 reshape.115
  225.2 8.6 %reduce-scatter.5.cloned.1.call-done = bf16[64,2048]{1,0:T(8,128)(2,1)} async-done(((bf16[512,2048]{1,0:T(8,128)(2,1)}), bf16[64,2048]{1,0:T(8,128)(2,1)}) %reduce-scatter.5.cloned.1.call-update) | async-done | bytes 262160 | tf_op jit(solution)/shard_map/reduce_scatter | solution.py:97
  (8 shorter events, 0.1 us)
Async XLA Ops:
  7.2 190.5 %copy-start = (bf16[256,2048]{1,0:T(8,128)(2,1)S(1)}, bf16[256,2048]{1,0:T(8,128)(2,1)}, u32[]{:S(2)}) copy-start(bf16[256,2048]{1,0:T(8,128)(2,1)} %param.13) | copy-start | bytes 3145732
  7.2 35.8 %all-gather.3.cloned.1.call-start = ((), (), s32[]{:S(2)}) async-start(), calls=%async_computation.3 | async-start | bytes 2621440 | tf_op jit(solution)/shard_map/all_gather | solution.py:47
  7.9 64.1 %reduce-scatter.3.cloned.1.call-start = ((), (), s32[]{:S(2)}) async-start(), calls=%async_computation.4 | async-start | bytes 4718592 | tf_op jit(solution)/shard_map/reduce_scatter | solution.py:74
  8.7 10.7 %copy-start.3 = (bf16[128,4,3,128]{3,1,2,0:T(4,128)(2,1)S(1)}, bf16[128,4,3,128]{3,1,2,0:T(4,128)(2,1)}, u32[]{:S(2)}) copy-start(bf16[128,4,3,128]{3,1,2,0:T(4,128)(2,1)} %param.12) | copy-start | bytes 1179652
  47.5 6.4 %copy-start.2 = (bf16[512,2048]{1,0:T(8,128)(2,1)S(1)}, bf16[512,2048]{1,0:T(8,128)(2,1)}, u32[]{:S(2)}) copy-start(bf16[512,2048]{1,0:T(8,128)(2,1)} %all-gather.3.cloned.1.call-done) | copy-start | bytes 6291460
  47.5 6.4 %copy-start.6 = (bf16[2048,128]{1,0:T(8,128)(2,1)S(1)}, bf16[2048,128]{1,0:T(8,128)(2,1)}, u32[]{:S(2)}) copy-start(bf16[2048,128]{1,0:T(8,128)(2,1)} %param.11) | copy-start | bytes 1572868
  57.9 17.2 %copy-start.4 = (s32[8192]{0:T(1024)S(1)}, s32[8192]{0:T(1024)}, u32[]{:S(2)}) copy-start(s32[8192]{0:T(1024)} %param.14) | copy-start | bytes 98308
  57.9 89.4 %all-gather.5.cloned.1.call-start = ((), (), s32[]{:S(2)}) async-start(), calls=%async_computation.5 | async-start | bytes 8912896 | tf_op jit(solution)/shard_map/all_gather | solution.py:88
  74.9 158.9 %reduce-scatter.5.cloned.1.call-start = ((), (), s32[]{:S(2)}) async-start(), calls=%async_computation.6 | async-start | bytes 2359296 | tf_op jit(solution)/shard_map/reduce_scatter | solution.py:97
  164.9 16.2 %copy-start.1 = (pred[512,8192]{1,0:T(8,128)(4,1)S(1)}, pred[512,8192]{1,0:T(8,128)(4,1)}, u32[]{:S(2)}) copy-start(pred[512,8192]{1,0:T(8,128)(4,1)} %fusion) | copy-start | bytes 12582916
  197.6 2.1 copy-start.5
Sparse Core Ops, SparseCore 0:
  9.6 33.2 all-gather.2
  58.0 13.9 reduce-scatter.2
  75.0 72.3 all-gather.4
  199.9 33.8 reduce-scatter.4
where the time goes:
time: 241 us; the launch traced here: 240 us
  waiting for transfers between devices  114 us (47%)
  matrix products  47.2 us (20%)
  other arithmetic  26.6 us (11%)
  blocking collectives  24.5 us (10%)
  between operations  13.9 us (6%)
  local copies, waits for them, and re-layouts  13.8 us (6%)
    all_gather x1, waiting for transfers between devices, shards(): lax.all_gather(kv_tok, 'tok', axis=0, tiled=True)  67.3 us
    all_gather x1, waiting for transfers between devices, shards(): gathered = lax.all_gather(block_input_rows, 'row', axis=0, tiled=True)  23.3 us
    all_to_all x1, blocking collectives, shards(): lax.all_to_all(outgoing, 'tok', split_axis=0, concat_axis=0, tiled=True)  22 us
    dot_general x1, matrix products, fold_piece(): jnp.einsum('htd,shd->hts', query, piece[:, :, 0], preferred_element_type=...  17.6 us
    dot_general x1, matrix products, fold_piece(): jnp.einsum('hts,shd->htd', weights, piece[:, :, 1], preferred_element_typ...  16.5 us
    reduce_sum x1, other arithmetic, fold_piece(): total_new = jnp.sum(weights.astype(jnp.float32), axis=2)  16.2 us
    reduce_scatter x1, waiting for transfers between devices, shards(): lax.psum_scatter(main + adapter_down_output, 'col', scatter_dimension=0,...  14.1 us
    unnamed x17, local copies, waits for them, and re-layouts  12.1 us
  transfers between devices with their start and end apart: 4, of which 4 were waited for; matrix products, arithmetic and copies ran while one was open for 8% of the time, Pallas kernels for 0%

commit v1 on v0

--- a/solution.py
+++ b/solution.py
@@ -3,13 +3,15 @@
 from jax import lax
 from jax.sharding import PartitionSpec as P
 
+
 INPUT_WIDTH = 4096
 HEAD_SIZE = 128
 ADAPTER_RANK = 128
+MAXLEN = 4352
 
 
 def fold_piece(carry, piece, query, own_seg, own_start, prompt_segment_index, scale):
-    top_old, total_old, acc_old = carry
+    top_old, _, _ = carry
     count = piece.shape[0]
     key_pos = jnp.arange(count, dtype=jnp.int32)
     query_pos = own_start + jnp.arange(query.shape[1], dtype=jnp.int32)
@@ -34,7 +36,7 @@
     return (top_new, total_new, acc_new)
 
 
-def shards(
+def shards_body(
     block_input_rows,
     input_norm_scale,
     query_key_value_weight,
@@ -75,23 +77,23 @@
     qkv = mixed.astype(jnp.bfloat16).reshape(heads_dev, tok_dev, 3, HEAD_SIZE)
     query = qkv[:, :, 0]
     kv_tok = jnp.transpose(qkv[:, :, 1:3], (1, 0, 2, 3))
-    own_start = lax.axis_index("tok") * tok_dev
+    count_tok = lax.axis_size("tok")
+    me = lax.axis_index("tok")
+    own_start = me * tok_dev
     own_seg = lax.dynamic_slice_in_dim(prompt_segment_index, own_start, tok_dev, 0)
     scale = 1.0 / HEAD_SIZE**0.5
+    back = min(count_tok - 1, -(-(MAXLEN - 1) // tok_dev))
+    window = (back + 1) * tok_dev
+    first = jnp.clip(me - back, 0, count_tok - 1 - back) * tok_dev
+    gathered_kv = lax.all_gather(kv_tok, "tok", axis=0, tiled=True)
+    piece = lax.dynamic_slice_in_dim(gathered_kv, first, window, 0)
+    key_seg = lax.dynamic_slice_in_dim(prompt_segment_index, first, window, 0)
     init = (
         jnp.full((heads_dev, tok_dev), -1e30, jnp.float32),
         jnp.zeros((heads_dev, tok_dev), jnp.float32),
         jnp.zeros((heads_dev, tok_dev, HEAD_SIZE), jnp.float32),
     )
-    state = fold_piece(
-        init,
-        lax.all_gather(kv_tok, "tok", axis=0, tiled=True),
-        query,
-        own_seg,
-        own_start,
-        prompt_segment_index,
-        scale,
-    )
+    state = fold_piece(init, piece, query, own_seg, own_start - first, key_seg, scale)
     attended = (state[2] / state[1][:, :, None]).astype(jnp.bfloat16)
     attended = jnp.transpose(attended, (1, 0, 2)).reshape(tok_dev, heads_dev * HEAD_SIZE)
     block_output = lax.psum_scatter(
@@ -102,13 +104,12 @@
         scatter_dimension=0,
         tiled=True,
     )
-    count_tok = lax.axis_size("tok")
     capacity = max(2, 2 * tok_dev // count_tok)
     owner = cache_owner_index[:, 0]
     onehot = (owner[:, None] == jnp.arange(count_tok, dtype=jnp.int32)[None, :]).astype(jnp.int32)
     before = jnp.cumsum(onehot, axis=0) - onehot
     rank = jnp.sum(before * onehot, axis=1)
-    slot = owner * capacity + rank
+    slot = ((owner - me) % count_tok) * capacity + rank
     selector = (jnp.arange(count_tok * capacity, dtype=jnp.int32)[:, None] == slot[None, :]).astype(
         jnp.bfloat16
     )
@@ -116,8 +117,13 @@
         selector,
         kv_tok.reshape(tok_dev, heads_dev * 2 * HEAD_SIZE),
         preferred_element_type=jnp.float32,
-    ).astype(jnp.bfloat16)
-    received = lax.all_to_all(outgoing, "tok", split_axis=0, concat_axis=0, tiled=True)
+    ).astype(jnp.bfloat16).reshape(count_tok, capacity, heads_dev * 2 * HEAD_SIZE)
+    chunks = [outgoing[0]]
+    for shift in range(1, count_tok):
+        pairs = [(j, (j + shift) % count_tok) for j in range(count_tok)]
+        chunks.append(lax.ppermute(outgoing[shift], "tok", pairs))
+    arrived = jnp.stack(chunks)
+    received = jnp.take(arrived, (me - jnp.arange(count_tok)) % count_tok, axis=0)
     kv_cache = received.reshape(count_tok * capacity, heads_dev, 2, HEAD_SIZE)
     return (block_output, kv_cache)
 
@@ -134,7 +140,7 @@
         P("tok", None),
     )
     return jax.shard_map(
-        shards,
+        shards_body,
         mesh=mesh,
         in_specs=placed,
         out_specs=(P(("tok", "row", "col"), None), P("tok", ("row", "col"), None, None)),

time: 241 us -> 228 us (0.946)
  starting transfers between devices: 0.34 us -> 30.5 us
  blocking collectives: 24.5 us -> 2.47 us
  matrix products: 47.2 us -> 36.5 us
  waiting for transfers between devices: 114 us -> 105 us
    ppermute x0 -> x15, starting transfers between devices: none -> 30.1 us  [shards_body(): chunks.append(lax.ppermute(outgoing[shift], 'tok', pairs))]
    all_to_all x1 -> x0, blocking collectives: 22 us -> none  [shards(): lax.all_to_all(outgoing, 'tok', split_axis=0, concat_axis=0, tiled=True)]
    reduce_scatter x2, waiting for transfers between devices: 22.6 us -> 14.1 us  [the longest x1 14.1 us: shards_body(): lax.psum_scatter(main + adapter_down_output, 'col', scatter_dimension=0,...]
    dot_general x1, matrix products: 16.5 us -> 10.5 us  [fold_piece(): jnp.einsum('hts,shd->htd', weights, piece[:, :, 1], preferred_element_typ...]
    dot_general x1, matrix products: 17.6 us -> 11.9 us  [fold_piece(): jnp.einsum('htd,shd->hts', query, piece[:, :, 0], preferred_element_type=...]
    reduce_sum x1, other arithmetic: 16.2 us -> 10.7 us  [fold_piece(): total_new = jnp.sum(weights.astype(jnp.float32), axis=2)]
    select_n x0 -> x2, other arithmetic: none -> 4.43 us  [shards_body(): jnp.take(arrived, (me - jnp.arange(count_tok)) % count_tok, axis=0)]
    all_gather x2, waiting for transfers between devices: 90.6 us -> 87.4 us  [the longest x1 63.5 us: shards_body(): gathered_kv = lax.all_gather(kv_tok, 'tok', axis=0, tiled=True)]
  transfers between devices with their start and end apart: 4 -> 19, of which waited for: 4 -> 6; matrix products, arithmetic and copies ran while one was open for 8% -> 11% of each run, Pallas kernels for 0% -> 0%
where the time goes in v1:
time: 228 us
  waiting for transfers between devices  105 us (46%)
  matrix products  36.5 us (16%)
  starting transfers between devices  30.5 us (13%)
  other arithmetic  25.2 us (11%)
  between operations  14.1 us (6%)
  local copies, waits for them, and re-layouts  14 us (6%)
  blocking collectives  2.47 us (1%)
    all_gather x1, waiting for transfers between devices, shards_body(): gathered_kv = lax.all_gather(kv_tok, 'tok', axis=0, tiled=True)  63.5 us
    ppermute x15, starting transfers between devices, shards_body(): chunks.append(lax.ppermute(outgoing[shift], 'tok', pairs))  30.1 us
    all_gather x1, waiting for transfers between devices, shards_body(): gathered = lax.all_gather(block_input_rows, 'row', axis=0, tiled=True)  24 us
    reduce_scatter x1, waiting for transfers between devices, shards_body(): lax.psum_scatter(main + adapter_down_output, 'col', scatter_dimension=0,...  14.1 us
    unnamed x36, local copies, waits for them, and re-layouts  12.1 us
    dot_general x1, matrix products, fold_piece(): jnp.einsum('htd,shd->hts', query, piece[:, :, 0], preferred_element_type=...  11.9 us
    reduce_sum x1, other arithmetic, fold_piece(): total_new = jnp.sum(weights.astype(jnp.float32), axis=2)  10.7 us
    dot_general x1, matrix products, fold_piece(): jnp.einsum('hts,shd->htd', weights, piece[:, :, 1], preferred_element_typ...  10.5 us
  transfers between devices with their start and end apart: 19, of which 6 were waited for; matrix products, arithmetic and copies ran while one was open for 11% of the time, Pallas kernels for 0%

profile of v1, /device:TPU:0, one launch (start us, length us, event | category | flops | bytes accessed | tf_op | source)
XLA Modules:
  0.0 227.7 jit_solution(6471377655335773641)
XLA Ops:
  7.2 0.0 copy-start
  7.2 0.0 all-gather.3.cloned.1.call-start
  7.2 0.7 all-gather.3.cloned.1.call-update
  7.9 0.0 reduce-scatter.3.cloned.1.call-start
  8.0 10.7 %copy.13 = bf16[2048,4,3,128]{0,3,2,1:T(8,128)(2,1)} copy(bf16[2048,4,3,128]{3,1,2,0:T(4,128)(2,1)} %param.10) | data formatting | bytes 12582912 | tf_op args[2]
  18.7 0.3 copy.15
  19.0 24.0 %all-gather.3.cloned.1.call-done = bf16[512,2048]{1,0:T(8,128)(2,1)} async-done(((bf16[128,2048]{1,0:T(8,128)(2,1)}), bf16[512,2048]{1,0:T(8,128)(2,1)}) %all-gather.3.cloned.1.call-update) | async-done | bytes 2097168 | tf_op jit(solution)/shard_map/all_gather | solution.py:49
  43.0 2.1 fusion.1
  45.0 2.5 %psum.7 = f32[512]{0:T(512)S(1)} all-reduce(f32[512]{0:T(512)S(1)} %fusion.1), channel_id=1, replica_groups=mesh['tok'=16,'row'=4,'col'=2] {'col'}, use_global_device_ids=true, to_apply=%region_1.0 | all-reduce | flops 512 | bytes 4096 | tf_op jit(solution)/shard_map/psum | solution.py:52
  47.5 6.4 %fusion.6 = f32[512,4,384]{2,0,1:T(8,128)S(1)} fusion(bf16[2048,4,384]{0,2,1:T(8,128)(2,1)} %bitcast.106, bf16[512,2048]{1,0:T(8,128)(2,1)} %all-gather.3.cloned.1.call-done, f32[2048]{0:T(1024)S(1)} %convert_element_type.38, f32[512]{0:T(512)S(1)} %add_rsqrt_fusion), kind=kOutput, calls=%fused_computation.17 | convolution fusion | flops 3225419776 | bytes 11544576 | tf_op jit(solution)/shard_map/td,dhe->hte/dot_general | solution.py:67
  54.0 0.8 convolution_bitcast_fusion
  54.7 3.1 %add_bitcast_fusion = f32[4,512,384]{2,1,0:T(8,128)} fusion(f32[512,4,384]{2,0,1:T(8,128)S(1)} %fusion.6, f32[512,128,1]{1,0,2:T(8,128)S(1)} %convolution_bitcast_fusion, bf16[128,4,384]{0,2,1:T(8,128)(2,1)S(1)} %bitcast.111), kind=kOutput, calls=%fused_computation.11 | convolution fusion | flops 1208745984 | bytes 6946816 | tf_op jit(solution)/shard_map/tr,rhe->hte/dot_general | solution.py:70
  57.9 0.0 reduce-scatter.3.cloned.1.call-update
  57.9 0.0 all-gather.5.cloned.1.call-start
  57.9 14.1 %reduce-scatter.3.cloned.1.call-done = f32[2,512,384]{2,1,0:T(8,128)} async-done(((f32[4,512,384]{2,1,0:T(8,128)}), f32[2,512,384]{2,1,0:T(8,128)}) %reduce-scatter.3.cloned.1.call-update) | async-done | bytes 1572880 | tf_op jit(solution)/shard_map/reduce_scatter | solution.py:76
  72.0 1.5 convert_element_type.40
  73.5 0.3 copy.17
  73.8 1.0 copy.27
  74.9 0.0 all-gather.5.cloned.1.call-update
  74.9 0.2 reduce-scatter.5.cloned.1.call-start
  75.1 0.1 dynamic_slice.10
  75.2 0.1 dynamic_slice.9
  75.3 1.2 reduce-window.6
  76.5 0.2 slice_reduce_fusion
  76.7 0.1 broadcast_in_dim.53
  76.8 0.1 broadcast_in_dim.54
  76.9 0.1 fusion.19
  77.0 5.1 %fusion = pred[512,5120]{1,0:T(8,128)(4,1)} fusion(s32[512]{0:T(512)S(1)} %iota_add_fusion, s32[5120]{0:T(1024)S(1)} %dynamic_slice.10, s32[512]{0:T(512)S(1)} %dynamic_slice.9), kind=kLoop, calls=%fused_computation.5 | loop fusion | flops 7864320 | bytes 2646016 | tf_op jit(solution)/shard_map/and | solution.py:19
  82.2 1.7 fusion.9
  83.9 63.5 %all-gather.5.cloned.1.call-done = bf16[8192,2,2,128]{3,0,1,2:T(8,128)(2,1)} async-done(((bf16[512,2,2,128]{3,0,1,2:T(8,128)(2,1)}), bf16[8192,2,2,128]{3,0,1,2:T(8,128)(2,1)}) %all-gather.5.cloned.1.call-update) | async-done | bytes 8388624 | tf_op jit(solution)/shard_map/all_gather | solution.py:88
  147.3 11.9 %select_reduce_fusion = (f32[2,512]{1,0:T(2,128)S(1)}, f32[2,512,5120]{2,1,0:T(8,128)}) fusion(pred[512,5120]{1,0:T(8,128)(4,1)} %fusion, bf16[8192,2,2,128]{3,0,1,2:T(8,128)(2,1)} %all-gather.5.cloned.1.call-done, s32[]{:T(128)S(6)} %select_n.64, bf16[2,512,3,128]{1,3,2,0:T(8,128)(2,1)S(1)} %bitcast.108), kind=kOutput, calls=%fused_computation.3 | convolution fusion | flops 1357904896 | bytes 26480644 | tf_op jit(solution)/shard_map/htd,shd->hts/dot_general | solution.py:24
  159.3 10.7 %convert_reduce_fusion = f32[2,512]{1,0:T(2,128)S(1)} fusion(f32[2,512]{1,0:T(2,128)S(1)} %broadcast_maximum_fusion, f32[2,512,5120]{2,1,0:T(8,128)} %get-tuple-element.18, pred[512,5120]{1,0:T(8,128)(4,1)S(1)} %copy-done.1), kind=kLoop, calls=%fused_computation.1 | loop fusion | flops 31456256 | bytes 23601152 | tf_op jit(solution)/shard_map/reduce_sum | solution.py:32
  170.0 10.5 %fusion.12 = bf16[512,2,128]{0,2,1:T(8,128)(2,1)S(1)} fusion(bf16[8192,2,2,128]{3,0,1,2:T(8,128)(2,1)} %all-gather.5.cloned.1.call-done, s32[]{:T(128)S(6)} %select_n.64, s32[]{:T(128)S(6)} %add.100, f32[512,2]{0,1:T(2,128)S(1)} %bitcast.116, f32[2,512,5120]{2,1,0:T(8,128)} %get-tuple-element.18, f32[2,512]{1,0:T(2,128)S(1)} %broadcast_maximum_fusion, ...), kind=kOutput, calls=%fused_computation.25 | convolution fusion | flops 1363410944 | bytes 26484744 | tf_op jit(solution)/shard_map/hts,shd->htd/dot_general | solution.py:33
  180.5 0.0 copy-start.3
  180.5 2.1 convolution_convert_fusion
  182.6 0.0 reduce-scatter.5.cloned.1.call-update
  182.6 0.1 fusion.29
  182.7 1.4 collective-permute-start
  184.1 2.9 %collective-permute-start.1 = (bf16[64,512]{1,0:T(8,128)(2,1)S(1)}, bf16[64,512]{1,0:T(8,128)(2,1)S(1)}, u32[]{:S(2)}, u32[]{:S(2)}) collective-permute-start(bf16[64,512]{1,0:T(8,128)(2,1)S(1)} %get-tuple-element.15), channel_id=1, source_target_pairs={{0,16},{8,24},{16,32},{24,40},{32,48},{40,56},{48,64},{56,72},{64,... | collective-permute-start | bytes 196616 | tf_op jit(solution)/shard_map/ppermute | solution.py:124
  187.0 1.1 collective-permute-start.2
  188.0 1.3 collective-permute-start.3
  189.3 0.9 collective-permute-start.4
  190.1 0.9 collective-permute-done
  191.1 1.7 collective-permute-start.5
  192.8 4.3 %collective-permute-start.6 = (bf16[64,512]{1,0:T(8,128)(2,1)S(1)}, bf16[64,512]{1,0:T(8,128)(2,1)S(1)}, u32[]{:S(2)}, u32[]{:S(2)}) collective-permute-start(bf16[64,512]{1,0:T(8,128)(2,1)S(1)} %get-tuple-element.10), channel_id=1, source_target_pairs={{0,56},{8,64},{16,72},{24,80},{32,88},{40,96},{48,104},{56,112},{6... | collective-permute-start | bytes 196616 | tf_op jit(solution)/shard_map/ppermute | solution.py:124
  197.1 0.0 collective-permute-done.2
  197.1 2.1 collective-permute-start.7
  199.2 0.0 collective-permute-done.3
  199.2 0.5 collective-permute-start.8
  199.8 0.0 collective-permute-done.4
  199.8 4.0 %collective-permute-start.9 = (bf16[64,512]{1,0:T(8,128)(2,1)S(1)}, bf16[64,512]{1,0:T(8,128)(2,1)S(1)}, u32[]{:S(2)}, u32[]{:S(2)}) collective-permute-start(bf16[64,512]{1,0:T(8,128)(2,1)S(1)} %get-tuple-element.7), channel_id=1, source_target_pairs={{0,80},{8,88},{16,96},{24,104},{32,112},{40,120},{48,0},{56,8},{64... | collective-permute-start | bytes 196616 | tf_op jit(solution)/shard_map/ppermute | solution.py:124
  203.8 0.0 collective-permute-done.5
  203.8 4.2 %collective-permute-start.10 = (bf16[64,512]{1,0:T(8,128)(2,1)S(1)}, bf16[64,512]{1,0:T(8,128)(2,1)S(1)}, u32[]{:S(2)}, u32[]{:S(2)}) collective-permute-start(bf16[64,512]{1,0:T(8,128)(2,1)S(1)} %get-tuple-element.6), channel_id=1, source_target_pairs={{0,88},{8,96},{16,104},{24,112},{32,120},{40,0},{48,8},{56,16},{64... | collective-permute-start | bytes 196616 | tf_op jit(solution)/shard_map/ppermute | solution.py:124
  208.0 0.7 collective-permute-start.11
  208.7 0.1 collective-permute-start.12
  208.9 1.4 collective-permute-start.13
  210.3 0.0 collective-permute-done.9
  210.3 3.7 %collective-permute-start.14 = (bf16[64,512]{1,0:T(8,128)(2,1)S(1)}, bf16[64,512]{1,0:T(8,128)(2,1)S(1)}, u32[]{:S(2)}, u32[]{:S(2)}) collective-permute-start(bf16[64,512]{1,0:T(8,128)(2,1)S(1)} %get-tuple-element.2), channel_id=1, source_target_pairs={{0,120},{8,0},{16,8},{24,16},{32,24},{40,32},{48,40},{56,48},{64,5... | collective-permute-start | bytes 196616 | tf_op jit(solution)/shard_map/ppermute | solution.py:124
  214.0 0.0 collective-permute-done.11
  214.0 1.0 collective-permute-done.12
  215.0 0.9 collective-permute-done.14
  215.9 0.6 gather_fusion
  216.5 0.3 gather.7
  216.8 4.4 %broadcast_select_fusion = bf16[1024,2,2,128]{3,2,1,0:T(2,128)(2,1)} fusion(bf16[1024,2,2,128]{3,2,1,0:T(2,128)(2,1)S(1)} %gather.7, pred[1024]{0:T(1024)(128)(4,1)S(1)} %broadcast_in_dim.54), kind=kLoop, calls=%fused_computation.20 | loop fusion | flops 524288 | bytes 2098176 | tf_op jit(solution)/shard_map/jit(_take)/select_n | solution.py:126
  (51 shorter events, 0.3 us)
Async XLA Ops:
  7.2 173.4 %copy-start = (bf16[256,2048]{1,0:T(8,128)(2,1)S(1)}, bf16[256,2048]{1,0:T(8,128)(2,1)}, u32[]{:S(2)}) copy-start(bf16[256,2048]{1,0:T(8,128)(2,1)} %param.13) | copy-start | bytes 3145732
  7.2 35.8 %all-gather.3.cloned.1.call-start = ((), (), s32[]{:S(2)}) async-start(), calls=%async_computation.2 | async-start | bytes 2621440 | tf_op jit(solution)/shard_map/all_gather | solution.py:49
  7.9 10.8 %copy-start.7 = (bf16[2048]{0:T(1024)(128)(2,1)S(1)}, bf16[2048]{0:T(1024)(128)(2,1)}, u32[]{:S(2)}) copy-start(bf16[2048]{0:T(1024)(128)(2,1)} %param.9) | copy-start | bytes 12292
  7.9 10.8 %copy-start.4 = (bf16[128,4,3,128]{3,1,2,0:T(4,128)(2,1)S(1)}, bf16[128,4,3,128]{3,1,2,0:T(4,128)(2,1)}, u32[]{:S(2)}) copy-start(bf16[128,4,3,128]{3,1,2,0:T(4,128)(2,1)} %param.12) | copy-start | bytes 1179652
  7.9 64.1 %reduce-scatter.3.cloned.1.call-start = ((), (), s32[]{:S(2)}) async-start(), calls=%async_computation.3 | async-start | bytes 4718592 | tf_op jit(solution)/shard_map/reduce_scatter | solution.py:76
  47.5 6.4 %copy-start.2 = (bf16[512,2048]{1,0:T(8,128)(2,1)S(1)}, bf16[512,2048]{1,0:T(8,128)(2,1)}, u32[]{:S(2)}) copy-start(bf16[512,2048]{1,0:T(8,128)(2,1)} %all-gather.3.cloned.1.call-done) | copy-start | bytes 6291460
  47.5 6.4 %copy-start.8 = (bf16[2048,128]{1,0:T(8,128)(2,1)S(1)}, bf16[2048,128]{1,0:T(8,128)(2,1)}, u32[]{:S(2)}) copy-start(bf16[2048,128]{1,0:T(8,128)(2,1)} %param.11) | copy-start | bytes 1572868
  57.9 17.3 %copy-start.6 = (s32[8192]{0:T(1024)S(1)}, s32[8192]{0:T(1024)}, u32[]{:S(2)}) copy-start(s32[8192]{0:T(1024)} %param.14) | copy-start | bytes 98308
  57.9 17.4 %copy-start.5 = (s32[512,1]{0,1:T(1,128)S(1)}, s32[512,1]{0,1:T(1,128)}, u32[]{:S(2)}) copy-start(s32[512,1]{0,1:T(1,128)} %param.15) | copy-start | bytes 6148
  57.9 89.5 %all-gather.5.cloned.1.call-start = ((), (), s32[]{:S(2)}) async-start(), calls=%async_computation.4 | async-start | bytes 8912896 | tf_op jit(solution)/shard_map/all_gather | solution.py:88
  74.9 146.3 %reduce-scatter.5.cloned.1.call-start = ((), (), s32[]{:S(2)}) async-start(), calls=%async_computation.5 | async-start | bytes 2359296 | tf_op jit(solution)/shard_map/reduce_scatter | solution.py:99
  147.3 11.9 %copy-start.1 = (pred[512,5120]{1,0:T(8,128)(4,1)S(1)}, pred[512,5120]{1,0:T(8,128)(4,1)}, u32[]{:S(2)}) copy-start(pred[512,5120]{1,0:T(8,128)(4,1)} %fusion) | copy-start | bytes 7864324
  180.5 2.1 copy-start.3
  182.7 8.3 %collective-permute-start = (bf16[64,512]{1,0:T(8,128)(2,1)S(1)}, bf16[64,512]{1,0:T(8,128)(2,1)S(1)}, u32[]{:S(2)}, u32[]{:S(2)}) collective-permute-start(bf16[64,512]{1,0:T(8,128)(2,1)S(1)} %get-tuple-element.16), channel_id=1, source_target_pairs={{0,8},{8,16},{16,24},{24,32},{32,40},{40,48},{48,56},{56,64},{64,7... | collective-permute-start | bytes 196616 | tf_op jit(solution)/shard_map/ppermute | solution.py:124
  184.1 8.7 %collective-permute-start.1 = (bf16[64,512]{1,0:T(8,128)(2,1)S(1)}, bf16[64,512]{1,0:T(8,128)(2,1)S(1)}, u32[]{:S(2)}, u32[]{:S(2)}) collective-permute-start(bf16[64,512]{1,0:T(8,128)(2,1)S(1)} %get-tuple-element.15), channel_id=1, source_target_pairs={{0,16},{8,24},{16,32},{24,40},{32,48},{40,56},{48,64},{56,72},{64,... | collective-permute-start | bytes 196616 | tf_op jit(solution)/shard_map/ppermute | solution.py:124
  187.0 10.1 %collective-permute-start.2 = (bf16[64,512]{1,0:T(8,128)(2,1)S(1)}, bf16[64,512]{1,0:T(8,128)(2,1)S(1)}, u32[]{:S(2)}, u32[]{:S(2)}) collective-permute-start(bf16[64,512]{1,0:T(8,128)(2,1)S(1)} %get-tuple-element.14), channel_id=1, source_target_pairs={{0,24},{8,32},{16,40},{24,48},{32,56},{40,64},{48,72},{56,80},{64,... | collective-permute-start | bytes 196616 | tf_op jit(solution)/shard_map/ppermute | solution.py:124
  188.0 11.2 %collective-permute-start.3 = (bf16[64,512]{1,0:T(8,128)(2,1)S(1)}, bf16[64,512]{1,0:T(8,128)(2,1)S(1)}, u32[]{:S(2)}, u32[]{:S(2)}) collective-permute-start(bf16[64,512]{1,0:T(8,128)(2,1)S(1)} %get-tuple-element.13), channel_id=1, source_target_pairs={{0,32},{8,40},{16,48},{24,56},{32,64},{40,72},{48,80},{56,88},{64,... | collective-permute-start | bytes 196616 | tf_op jit(solution)/shard_map/ppermute | solution.py:124
  189.3 10.5 %collective-permute-start.4 = (bf16[64,512]{1,0:T(8,128)(2,1)S(1)}, bf16[64,512]{1,0:T(8,128)(2,1)S(1)}, u32[]{:S(2)}, u32[]{:S(2)}) collective-permute-start(bf16[64,512]{1,0:T(8,128)(2,1)S(1)} %get-tuple-element.12), channel_id=1, source_target_pairs={{0,40},{8,48},{16,56},{24,64},{32,72},{40,80},{48,88},{56,96},{64,... | collective-permute-start | bytes 196616 | tf_op jit(solution)/shard_map/ppermute | solution.py:124
  191.1 12.7 %collective-permute-start.5 = (bf16[64,512]{1,0:T(8,128)(2,1)S(1)}, bf16[64,512]{1,0:T(8,128)(2,1)S(1)}, u32[]{:S(2)}, u32[]{:S(2)}) collective-permute-start(bf16[64,512]{1,0:T(8,128)(2,1)S(1)} %get-tuple-element.11), channel_id=1, source_target_pairs={{0,48},{8,56},{16,64},{24,72},{32,80},{40,88},{48,96},{56,104},{64... | collective-permute-start | bytes 196616 | tf_op jit(solution)/shard_map/ppermute | solution.py:124
  192.8 15.2 %collective-permute-start.6 = (bf16[64,512]{1,0:T(8,128)(2,1)S(1)}, bf16[64,512]{1,0:T(8,128)(2,1)S(1)}, u32[]{:S(2)}, u32[]{:S(2)}) collective-permute-start(bf16[64,512]{1,0:T(8,128)(2,1)S(1)} %get-tuple-element.10), channel_id=1, source_target_pairs={{0,56},{8,64},{16,72},{24,80},{32,88},{40,96},{48,104},{56,112},{6... | collective-permute-start | bytes 196616 | tf_op jit(solution)/shard_map/ppermute | solution.py:124
  197.1 11.6 %collective-permute-start.7 = (bf16[64,512]{1,0:T(8,128)(2,1)S(1)}, bf16[64,512]{1,0:T(8,128)(2,1)S(1)}, u32[]{:S(2)}, u32[]{:S(2)}) collective-permute-start(bf16[64,512]{1,0:T(8,128)(2,1)S(1)} %get-tuple-element.9), channel_id=1, source_target_pairs={{0,64},{8,72},{16,80},{24,88},{32,96},{40,104},{48,112},{56,120},{... | collective-permute-start | bytes 196616 | tf_op jit(solution)/shard_map/ppermute | solution.py:124
  199.2 9.6 %collective-permute-start.8 = (bf16[64,512]{1,0:T(8,128)(2,1)S(1)}, bf16[64,512]{1,0:T(8,128)(2,1)S(1)}, u32[]{:S(2)}, u32[]{:S(2)}) collective-permute-start(bf16[64,512]{1,0:T(8,128)(2,1)S(1)} %get-tuple-element.8), channel_id=1, source_target_pairs={{0,72},{8,80},{16,88},{24,96},{32,104},{40,112},{48,120},{56,0},{6... | collective-permute-start | bytes 196616 | tf_op jit(solution)/shard_map/ppermute | solution.py:124
  199.8 10.5 %collective-permute-start.9 = (bf16[64,512]{1,0:T(8,128)(2,1)S(1)}, bf16[64,512]{1,0:T(8,128)(2,1)S(1)}, u32[]{:S(2)}, u32[]{:S(2)}) collective-permute-start(bf16[64,512]{1,0:T(8,128)(2,1)S(1)} %get-tuple-element.7), channel_id=1, source_target_pairs={{0,80},{8,88},{16,96},{24,104},{32,112},{40,120},{48,0},{56,8},{64... | collective-permute-start | bytes 196616 | tf_op jit(solution)/shard_map/ppermute | solution.py:124
  203.8 10.2 %collective-permute-start.10 = (bf16[64,512]{1,0:T(8,128)(2,1)S(1)}, bf16[64,512]{1,0:T(8,128)(2,1)S(1)}, u32[]{:S(2)}, u32[]{:S(2)}) collective-permute-start(bf16[64,512]{1,0:T(8,128)(2,1)S(1)} %get-tuple-element.6), channel_id=1, source_target_pairs={{0,88},{8,96},{16,104},{24,112},{32,120},{40,0},{48,8},{56,16},{64... | collective-permute-start | bytes 196616 | tf_op jit(solution)/shard_map/ppermute | solution.py:124
  208.0 6.0 %collective-permute-start.11 = (bf16[64,512]{1,0:T(8,128)(2,1)S(1)}, bf16[64,512]{1,0:T(8,128)(2,1)S(1)}, u32[]{:S(2)}, u32[]{:S(2)}) collective-permute-start(bf16[64,512]{1,0:T(8,128)(2,1)S(1)} %get-tuple-element.5), channel_id=1, source_target_pairs={{0,96},{8,104},{16,112},{24,120},{32,0},{40,8},{48,16},{56,24},{64... | collective-permute-start | bytes 196616 | tf_op jit(solution)/shard_map/ppermute | solution.py:124
  208.7 6.2 %collective-permute-start.12 = (bf16[64,512]{1,0:T(8,128)(2,1)S(1)}, bf16[64,512]{1,0:T(8,128)(2,1)S(1)}, u32[]{:S(2)}, u32[]{:S(2)}) collective-permute-start(bf16[64,512]{1,0:T(8,128)(2,1)S(1)} %get-tuple-element.4), channel_id=1, source_target_pairs={{0,104},{8,112},{16,120},{24,0},{32,8},{40,16},{48,24},{56,32},{64... | collective-permute-start | bytes 196616 | tf_op jit(solution)/shard_map/ppermute | solution.py:124
  208.9 6.1 %collective-permute-start.13 = (bf16[64,512]{1,0:T(8,128)(2,1)S(1)}, bf16[64,512]{1,0:T(8,128)(2,1)S(1)}, u32[]{:S(2)}, u32[]{:S(2)}) collective-permute-start(bf16[64,512]{1,0:T(8,128)(2,1)S(1)} %get-tuple-element.3), channel_id=1, source_target_pairs={{0,112},{8,120},{16,0},{24,8},{32,16},{40,24},{48,32},{56,40},{64,... | collective-permute-start | bytes 196616 | tf_op jit(solution)/shard_map/ppermute | solution.py:124
  210.3 5.6 %collective-permute-start.14 = (bf16[64,512]{1,0:T(8,128)(2,1)S(1)}, bf16[64,512]{1,0:T(8,128)(2,1)S(1)}, u32[]{:S(2)}, u32[]{:S(2)}) collective-permute-start(bf16[64,512]{1,0:T(8,128)(2,1)S(1)} %get-tuple-element.2), channel_id=1, source_target_pairs={{0,120},{8,0},{16,8},{24,16},{32,24},{40,32},{48,40},{56,48},{64,5... | collective-permute-start | bytes 196616 | tf_op jit(solution)/shard_map/ppermute | solution.py:124
Sparse Core Ops, SparseCore 0:
  9.7 33.2 all-gather.2
  58.0 13.9 reduce-scatter.2
  75.0 72.3 all-gather.4
  182.8 33.6 reduce-scatter.4

commit v2 on v1

--- a/solution.py
+++ b/solution.py
@@ -8,7 +8,6 @@
 HEAD_SIZE = 128
 ADAPTER_RANK = 128
 MAXLEN = 4352
-
 
 def fold_piece(carry, piece, query, own_seg, own_start, prompt_segment_index, scale):
     top_old, _, _ = carry
@@ -34,7 +33,6 @@
         "hts,shd->htd", weights, piece[:, :, 1], preferred_element_type=jnp.float32
     )
     return (top_new, total_new, acc_new)
-
 
 def shards_body(
     block_input_rows,
@@ -85,15 +83,43 @@
     back = min(count_tok - 1, -(-(MAXLEN - 1) // tok_dev))
     window = (back + 1) * tok_dev
     first = jnp.clip(me - back, 0, count_tok - 1 - back) * tok_dev
-    gathered_kv = lax.all_gather(kv_tok, "tok", axis=0, tiled=True)
-    piece = lax.dynamic_slice_in_dim(gathered_kv, first, window, 0)
     key_seg = lax.dynamic_slice_in_dim(prompt_segment_index, first, window, 0)
     init = (
-        jnp.full((heads_dev, tok_dev), -1e30, jnp.float32),
-        jnp.zeros((heads_dev, tok_dev), jnp.float32),
-        jnp.zeros((heads_dev, tok_dev, HEAD_SIZE), jnp.float32),
+        jnp.full((1, tok_dev), -1e30, jnp.float32),
+        jnp.zeros((1, tok_dev), jnp.float32),
+        jnp.zeros((1, tok_dev, HEAD_SIZE), jnp.float32),
     )
-    state = fold_piece(init, piece, query, own_seg, own_start - first, key_seg, scale)
+    capacity = max(2, 2 * tok_dev // count_tok)
+    owner = cache_owner_index[:, 0]
+    onehot = (owner[:, None] == jnp.arange(count_tok, dtype=jnp.int32)[None, :]).astype(jnp.int32)
+    before = jnp.cumsum(onehot, axis=0) - onehot
+    rank = jnp.sum(before * onehot, axis=1)
+    slot = owner * capacity + rank
+    selector = (jnp.arange(count_tok * capacity, dtype=jnp.int32)[:, None] == slot[None, :]).astype(
+        jnp.bfloat16
+    )
+    outgoing = jnp.dot(
+        selector,
+        kv_tok.reshape(tok_dev, heads_dev * 2 * HEAD_SIZE),
+        preferred_element_type=jnp.float32,
+    ).astype(jnp.bfloat16).reshape(count_tok, capacity, heads_dev * 2 * HEAD_SIZE)
+    gathered = []
+    for head in range(heads_dev):
+        gathered.append(lax.all_gather(kv_tok[:, head : head + 1], "tok", axis=0, tiled=True))
+    received = lax.all_to_all(outgoing, "tok", split_axis=0, concat_axis=0, tiled=True)
+    received, gathered[0] = lax.optimization_barrier((received, gathered[0]))
+    states = []
+    for head in range(heads_dev):
+        gathered_kv = gathered[head]
+        if head > 0:
+            gathered_kv, _ = lax.optimization_barrier((gathered_kv, states[-1]))
+        piece = lax.dynamic_slice_in_dim(gathered_kv, first, window, 0)
+        states.append(
+            fold_piece(
+                init, piece, query[head : head + 1], own_seg, own_start - first, key_seg, scale
+            )
+        )
+    state = tuple(jnp.concatenate(parts, axis=0) for parts in zip(*states))
     attended = (state[2] / state[1][:, :, None]).astype(jnp.bfloat16)
     attended = jnp.transpose(attended, (1, 0, 2)).reshape(tok_dev, heads_dev * HEAD_SIZE)
     block_output = lax.psum_scatter(
@@ -104,29 +130,8 @@
         scatter_dimension=0,
         tiled=True,
     )
-    capacity = max(2, 2 * tok_dev // count_tok)
-    owner = cache_owner_index[:, 0]
-    onehot = (owner[:, None] == jnp.arange(count_tok, dtype=jnp.int32)[None, :]).astype(jnp.int32)
-    before = jnp.cumsum(onehot, axis=0) - onehot
-    rank = jnp.sum(before * onehot, axis=1)
-    slot = ((owner - me) % count_tok) * capacity + rank
-    selector = (jnp.arange(count_tok * capacity, dtype=jnp.int32)[:, None] == slot[None, :]).astype(
-        jnp.bfloat16
-    )
-    outgoing = jnp.dot(
-        selector,
-        kv_tok.reshape(tok_dev, heads_dev * 2 * HEAD_SIZE),
-        preferred_element_type=jnp.float32,
-    ).astype(jnp.bfloat16).reshape(count_tok, capacity, heads_dev * 2 * HEAD_SIZE)
-    chunks = [outgoing[0]]
-    for shift in range(1, count_tok):
-        pairs = [(j, (j + shift) % count_tok) for j in range(count_tok)]
-        chunks.append(lax.ppermute(outgoing[shift], "tok", pairs))
-    arrived = jnp.stack(chunks)
-    received = jnp.take(arrived, (me - jnp.arange(count_tok)) % count_tok, axis=0)
     kv_cache = received.reshape(count_tok * capacity, heads_dev, 2, HEAD_SIZE)
     return (block_output, kv_cache)
-
 
 def solution(mesh):
     placed = (

time: 228 us -> 255 us (1.12)
  waiting for transfers between devices: 105 us -> 173 us
  starting transfers between devices: 30.5 us -> 7.42 us
  other arithmetic: 25.2 us -> 14.1 us
  matrix products: 36.5 us -> 29.8 us
    reduce_scatter x1, waiting for transfers between devices: 0.01 us -> 32.2 us  [shards_body(): lax.psum_scatter(jnp.dot(attended, output_projection_weight, preferred_el...]
    ppermute x15 -> x0, starting transfers between devices: 30.1 us -> none  [shards_body(): chunks.append(lax.ppermute(outgoing[shift], 'tok', pairs))]
    all_to_all x0 -> x1, waiting for transfers between devices: none -> 21 us  [shards_body(): lax.all_to_all(outgoing, 'tok', split_axis=0, concat_axis=0, tiled=True)]
    all_gather x1 -> x2, waiting for transfers between devices: 63.5 us -> 81.2 us  [shards_body(): lax.all_gather(kv_tok[:, head:head + 1], 'tok', axis=0, tiled=True)]
    all_to_all x0 -> x1, starting transfers between devices: none -> 7.04 us  [shards_body(): lax.all_to_all(outgoing, 'tok', split_axis=0, concat_axis=0, tiled=True)]
    and x2 -> x0, other arithmetic: 5.14 us -> none  [the longest x1 5.13 us: fold_piece(): (own_seg[:, None] == prompt_segment_index[None, :]) & (key_pos[None, :] <...]
    select_n x2 -> x0, other arithmetic: 4.43 us -> none  [shards_body(): jnp.take(arrived, (me - jnp.arange(count_tok)) % count_tok, axis=0)]
    dot_general x1 -> x2, matrix products: 10.5 us -> 6.39 us  [fold_piece(): jnp.einsum('hts,shd->htd', weights, piece[:, :, 1], preferred_element_typ...]
  transfers between devices with their start and end apart: 19 -> 6, of which waited for: 6 -> 6; matrix products, arithmetic and copies ran while one was open for 11% -> 11% of each run, Pallas kernels for 0% -> 0%
where the time goes in v2:
time: 255 us; the launch traced here: 254 us
  waiting for transfers between devices  173 us (68%)
  matrix products  29.8 us (12%)
  other arithmetic  14.1 us (6%)
  between operations  14 us (5%)
  local copies, waits for them, and re-layouts  13.8 us (5%)
  starting transfers between devices  7.42 us (3%)
    all_gather x2, waiting for transfers between devices, shards_body(): lax.all_gather(kv_tok[:, head:head + 1], 'tok', axis=0, tiled=True)  81.2 us
    reduce_scatter x1, waiting for transfers between devices, shards_body(): lax.psum_scatter(jnp.dot(attended, output_projection_weight, preferred_el...  32.2 us
    all_gather x1, waiting for transfers between devices, shards_body(): gathered = lax.all_gather(block_input_rows, 'row', axis=0, tiled=True)  23.3 us
    all_to_all x1, waiting for transfers between devices, shards_body(): lax.all_to_all(outgoing, 'tok', split_axis=0, concat_axis=0, tiled=True)  21 us
    reduce_scatter x1, waiting for transfers between devices, shards_body(): lax.psum_scatter(main + adapter_down_output, 'col', scatter_dimension=0,...  14.1 us
    unnamed x14, local copies, waits for them, and re-layouts  11.1 us
    dot_general x2, matrix products, fold_piece(): jnp.einsum('htd,shd->hts', query, piece[:, :, 0], preferred_element_type=...  9.27 us
    reduce_sum x2, other arithmetic, fold_piece(): total_new = jnp.sum(weights.astype(jnp.float32), axis=2)  8.41 us
  transfers between devices with their start and end apart: 6, of which 6 were waited for; matrix products, arithmetic and copies ran while one was open for 11% of the time, Pallas kernels for 0%

profile of v2, /device:TPU:0, one launch (start us, length us, event | category | flops | bytes accessed | tf_op | source)
XLA Modules:
  0.0 254.5 jit_solution(18077239002666291057)
XLA Ops:
  7.2 0.0 copy-start
  7.2 0.0 all-gather.4.cloned.1.call-start
  7.2 0.7 all-gather.4.cloned.1.call-update
  7.9 0.0 reduce-scatter.3.cloned.1.call-start
  8.0 0.7 convert_element_type.47
  8.7 0.0 copy-start.2
  8.7 10.7 %copy.10 = bf16[2048,4,3,128]{0,3,2,1:T(8,128)(2,1)} copy(bf16[2048,4,3,128]{3,1,2,0:T(4,128)(2,1)} %param.10) | data formatting | bytes 12582912 | tf_op args[2]
  19.4 0.0 copy-done.2
  19.4 0.3 copy.12
  19.7 23.3 %all-gather.4.cloned.1.call-done = bf16[512,2048]{1,0:T(8,128)(2,1)} async-done(((bf16[128,2048]{1,0:T(8,128)(2,1)}), bf16[512,2048]{1,0:T(8,128)(2,1)}) %all-gather.4.cloned.1.call-update) | async-done | bytes 2097168 | tf_op jit(solution)/shard_map/all_gather | solution.py:47
  43.0 2.1 fusion.1
  45.0 2.5 psum.7
  47.5 0.0 copy-start.1
  47.5 0.0 copy-start.5
  47.5 6.4 %fusion.4 = f32[512,4,384]{2,0,1:T(8,128)S(1)} fusion(bf16[2048,4,384]{0,2,1:T(8,128)(2,1)} %bitcast.90, bf16[512,2048]{1,0:T(8,128)(2,1)} %all-gather.4.cloned.1.call-done, f32[2048]{0:T(1024)S(1)} %convert_element_type.47, f32[512]{0:T(512)S(1)} %add_rsqrt_fusion), kind=kOutput, calls=%fused_computation.15 | convolution fusion | flops 3225419776 | bytes 11544576 | tf_op jit(solution)/shard_map/td,dhe->hte/dot_general | solution.py:65
  53.9 0.0 copy-done.1
  53.9 0.0 copy-done.5
  54.0 0.8 convolution_bitcast_fusion
  54.7 3.2 %add_bitcast_fusion = f32[4,512,384]{2,1,0:T(8,128)} fusion(f32[512,4,384]{2,0,1:T(8,128)S(1)} %fusion.4, f32[512,128,1]{1,0,2:T(8,128)S(1)} %convolution_bitcast_fusion, bf16[128,4,384]{0,2,1:T(8,128)(2,1)S(1)} %bitcast.95), kind=kOutput, calls=%fused_computation.13 | convolution fusion | flops 1208745984 | bytes 6946816 | tf_op jit(solution)/shard_map/tr,rhe->hte/dot_general | solution.py:68
  57.9 0.0 reduce-scatter.3.cloned.1.call-update
  57.9 0.0 copy-start.3
  57.9 0.0 all-gather.6.cloned.1.call-start
  58.0 14.1 %reduce-scatter.3.cloned.1.call-done = f32[2,512,384]{2,1,0:T(8,128)} async-done(((f32[4,512,384]{2,1,0:T(8,128)}), f32[2,512,384]{2,1,0:T(8,128)}) %reduce-scatter.3.cloned.1.call-update) | async-done | bytes 1572880 | tf_op jit(solution)/shard_map/reduce_scatter | solution.py:74
  72.0 1.5 convert_element_type.49
  73.5 0.3 copy.14
  73.8 0.0 copy-start.4
  73.9 0.1 fusion.26
  73.9 0.8 fusion.27
  74.8 0.0 all-gather.6.cloned.1.call-update
  74.8 0.0 all-gather.8.cloned.1.call-start
  74.9 0.5 all-gather.8.cloned.1.call-update
  75.4 0.0 copy-done.3
  75.4 1.2 reduce-window.6
  76.6 0.2 slice_reduce_fusion
  76.8 0.1 fusion.20
  76.9 1.7 fusion.7
  78.6 7.0 %all-to-all-start = ((bf16[16,64,512]{2,1,0:T(8,128)(2,1)}), bf16[16,64,512]{2,1,0:T(8,128)(2,1)S(1)}, u32[]{:S(2)}, u32[]{:S(2)}) async-start(bf16[16,64,512]{2,1,0:T(8,128)(2,1)} %bitcast.96), calls=%async_computation.1 | async-start | bytes 2097152 | tf_op jit(solution)/shard_map/all_to_all | solution.py:109
  85.7 0.2 reduce-scatter.5.cloned.1.call-start
  85.9 0.0 copy-done.4
  85.9 0.1 dynamic_slice.13
  86.0 0.1 dynamic_slice.12
  86.1 21.0 %all-to-all-done = bf16[16,64,512]{2,1,0:T(8,128)(2,1)S(1)} async-done(((bf16[16,64,512]{2,1,0:T(8,128)(2,1)}), bf16[16,64,512]{2,1,0:T(8,128)(2,1)S(1)}, u32[]{:S(2)}, u32[]{:S(2)}) %all-to-all-start) | async-done | bytes 1048608 | tf_op jit(solution)/shard_map/all_to_all | solution.py:109
  107.1 35.0 %all-gather.6.cloned.1.call-done = bf16[8192,1,2,128]{0,3,2,1:T(8,128)(2,1)} async-done(((bf16[512,1,2,128]{0,3,2,1:T(8,128)(2,1)}), bf16[8192,1,2,128]{0,3,2,1:T(8,128)(2,1)}) %all-gather.6.cloned.1.call-update) | async-done | bytes 4194320 | tf_op jit(solution)/shard_map/all_gather | solution.py:108
  142.1 4.6 %select_reduce_fusion.1 = (f32[512]{0:T(512)S(1)}, f32[512,5120]{1,0:T(8,128)S(1)}) fusion(s32[512]{0:T(512)S(1)} %iota_add_fusion, s32[5120]{0:T(1024)S(1)} %dynamic_slice.13, s32[512]{0:T(512)S(1)} %dynamic_slice.12, bf16[8192,1,2,128]{0,3,2,1:T(8,128)(2,1)} %all-gather.6.cloned.1.call-done, s32[]{:T(128)S(6)} %select_n.26, ...), kind=kOutput, calls=%fused_computation.5 | convolution fusion | flops 686816768 | bytes 11954180 | tf_op jit(solution)/shard_map/htd,shd->hts/dot_general | solution.py:23
  146.8 4.2 %convert_reduce_fusion.1 = (f32[512]{0:T(512)S(1)}, bf16[512,5120]{1,0:T(8,128)(2,1)S(1)}) fusion(f32[512]{0:T(512)S(1)} %broadcast_maximum_fusion.1, f32[512,5120]{1,0:T(8,128)S(1)} %get-tuple-element.17, s32[512]{0:T(512)S(1)} %iota_add_fusion, s32[5120]{0:T(1024)S(1)} %dynamic_slice.13, s32[512]{0:T(512)S(1)} %dynamic_slice.12), kind=kLoop, calls=%fused_computation.3 | loop fusion | flops 23592448 | bytes 15757312 | tf_op jit(solution)/shard_map/reduce_sum | solution.py:31
  151.0 3.2 %fusion.12 = f32[1,512,128]{1,2,0:T(8,128)S(1)} fusion(bf16[512,5120]{1,0:T(8,128)(2,1)S(1)} %get-tuple-element.11, bf16[8192,1,2,128]{0,3,2,1:T(8,128)(2,1)} %all-gather.6.cloned.1.call-done, s32[]{:T(128)S(6)} %select_n.26, s32[]{:T(128)S(6)} %add.56), kind=kOutput, calls=%fused_computation.28 | convolution fusion | flops 671088640 | bytes 6815752 | tf_op jit(solution)/shard_map/hts,shd->htd/dot_general | solution.py:32
  154.2 46.1 %all-gather.8.cloned.1.call-done = bf16[8192,1,2,128]{0,3,2,1:T(8,128)(2,1)} async-done(((bf16[512,1,2,128]{0,3,2,1:T(8,128)(2,1)}), bf16[8192,1,2,128]{0,3,2,1:T(8,128)(2,1)}) %all-gather.8.cloned.1.call-update) | async-done | bytes 4194320 | tf_op jit(solution)/shard_map/all_gather | solution.py:108
  200.4 4.6 %select_reduce_fusion = (f32[512]{0:T(512)S(1)}, f32[512,5120]{1,0:T(8,128)S(1)}) fusion(s32[512]{0:T(512)S(1)} %iota_add_fusion, s32[5120]{0:T(1024)S(1)} %dynamic_slice.13, s32[512]{0:T(512)S(1)} %dynamic_slice.12, bf16[8192,1,2,128]{0,3,2,1:T(8,128)(2,1)} %all-gather.8.cloned.1.call-done, s32[]{:T(128)S(6)} %select_n.26, ...), kind=kOutput, calls=%fused_computation.2 | convolution fusion | flops 686816768 | bytes 11954180 | tf_op jit(solution)/shard_map/htd,shd->hts/dot_general | solution.py:23
  205.0 4.2 %convert_reduce_fusion = (f32[512]{0:T(512)S(1)}, bf16[512,5120]{1,0:T(8,128)(2,1)S(1)}) fusion(f32[512]{0:T(512)S(1)} %broadcast_maximum_fusion, f32[512,5120]{1,0:T(8,128)S(1)} %get-tuple-element.19, s32[512]{0:T(512)S(1)} %iota_add_fusion, s32[5120]{0:T(1024)S(1)} %dynamic_slice.13, s32[512]{0:T(512)S(1)} %dynamic_slice.12), kind=kLoop, calls=%fused_computation | loop fusion | flops 23592448 | bytes 15757312 | tf_op jit(solution)/shard_map/reduce_sum | solution.py:31
  209.2 3.2 %fusion.13 = f32[1,512,128]{1,2,0:T(8,128)S(1)} fusion(bf16[512,5120]{1,0:T(8,128)(2,1)S(1)} %get-tuple-element.9, bf16[8192,1,2,128]{0,3,2,1:T(8,128)(2,1)} %all-gather.8.cloned.1.call-done, s32[]{:T(128)S(6)} %select_n.26, s32[]{:T(128)S(6)} %add.56), kind=kOutput, calls=%fused_computation.29 | convolution fusion | flops 671088640 | bytes 6815752 | tf_op jit(solution)/shard_map/hts,shd->htd/dot_general | solution.py:32
  212.4 0.1 fusion.17
  212.5 0.0 copy-done
  212.5 2.1 convolution_convert_fusion
  214.6 0.0 reduce-scatter.5.cloned.1.call-update
  214.6 1.1 reshape.139
  215.7 32.2 %reduce-scatter.5.cloned.1.call-done = bf16[64,2048]{1,0:T(8,128)(2,1)} async-done(((bf16[512,2048]{1,0:T(8,128)(2,1)}), bf16[64,2048]{1,0:T(8,128)(2,1)}) %reduce-scatter.5.cloned.1.call-update) | async-done | bytes 262160 | tf_op jit(solution)/shard_map/reduce_scatter | solution.py:125
  (9 shorter events, 0.1 us)
Async XLA Ops:
  7.2 205.3 %copy-start = (bf16[256,2048]{1,0:T(8,128)(2,1)S(1)}, bf16[256,2048]{1,0:T(8,128)(2,1)}, u32[]{:S(2)}) copy-start(bf16[256,2048]{1,0:T(8,128)(2,1)} %param.13) | copy-start | bytes 3145732
  7.2 35.8 %all-gather.4.cloned.1.call-start = ((), (), s32[]{:S(2)}) async-start(), calls=%async_computation.3 | async-start | bytes 2621440 | tf_op jit(solution)/shard_map/all_gather | solution.py:47
  7.9 64.1 %reduce-scatter.3.cloned.1.call-start = ((), (), s32[]{:S(2)}) async-start(), calls=%async_computation.4 | async-start | bytes 4718592 | tf_op jit(solution)/shard_map/reduce_scatter | solution.py:74
  8.7 10.7 %copy-start.2 = (bf16[128,4,3,128]{3,1,2,0:T(4,128)(2,1)S(1)}, bf16[128,4,3,128]{3,1,2,0:T(4,128)(2,1)}, u32[]{:S(2)}) copy-start(bf16[128,4,3,128]{3,1,2,0:T(4,128)(2,1)} %param.12) | copy-start | bytes 1179652
  47.5 6.4 %copy-start.1 = (bf16[512,2048]{1,0:T(8,128)(2,1)S(1)}, bf16[512,2048]{1,0:T(8,128)(2,1)}, u32[]{:S(2)}) copy-start(bf16[512,2048]{1,0:T(8,128)(2,1)} %all-gather.4.cloned.1.call-done) | copy-start | bytes 6291460
  47.5 6.4 %copy-start.5 = (bf16[2048,128]{1,0:T(8,128)(2,1)S(1)}, bf16[2048,128]{1,0:T(8,128)(2,1)}, u32[]{:S(2)}) copy-start(bf16[2048,128]{1,0:T(8,128)(2,1)} %param.11) | copy-start | bytes 1572868
  57.9 17.5 %copy-start.3 = (s32[512,1]{0,1:T(1,128)S(1)}, s32[512,1]{0,1:T(1,128)}, u32[]{:S(2)}) copy-start(s32[512,1]{0,1:T(1,128)} %param.15) | copy-start | bytes 6148
  57.9 84.2 %all-gather.6.cloned.1.call-start = ((), (), s32[]{:S(2)}) async-start(), calls=%async_computation.5 | async-start | bytes 4456448 | tf_op jit(solution)/shard_map/all_gather | solution.py:108
  73.8 12.1 %copy-start.4 = (s32[8192]{0:T(1024)S(1)}, s32[8192]{0:T(1024)}, u32[]{:S(2)}) copy-start(s32[8192]{0:T(1024)} %param.14) | copy-start | bytes 98308
  74.8 125.6 %all-gather.8.cloned.1.call-start = ((), (), s32[]{:S(2)}) async-start(), calls=%async_computation.6 | async-start | bytes 4456448 | tf_op jit(solution)/shard_map/all_gather | solution.py:108
  78.6 28.5 %all-to-all-start = ((bf16[16,64,512]{2,1,0:T(8,128)(2,1)}), bf16[16,64,512]{2,1,0:T(8,128)(2,1)S(1)}, u32[]{:S(2)}, u32[]{:S(2)}) async-start(bf16[16,64,512]{2,1,0:T(8,128)(2,1)} %bitcast.96), calls=%async_computation.1 | async-start | bytes 2097152 | tf_op jit(solution)/shard_map/all_to_all | solution.py:109
  85.7 162.3 %reduce-scatter.5.cloned.1.call-start = ((), (), s32[]{:S(2)}) async-start(), calls=%async_computation.7 | async-start | bytes 2359296 | tf_op jit(solution)/shard_map/reduce_scatter | solution.py:125
Sparse Core Ops, SparseCore 0:
  9.6 33.2 all-gather.3
  58.0 13.9 reduce-scatter.2
  74.9 67.1 all-gather.5
  144.1 56.1 all-gather.7
  214.7 33.1 reduce-scatter.4

commit v3 on v2

--- a/solution.py
+++ b/solution.py
@@ -8,6 +8,7 @@
 HEAD_SIZE = 128
 ADAPTER_RANK = 128
 MAXLEN = 4352
+
 
 def fold_piece(carry, piece, query, own_seg, own_start, prompt_segment_index, scale):
     top_old, _, _ = carry
@@ -82,8 +83,10 @@
     scale = 1.0 / HEAD_SIZE**0.5
     back = min(count_tok - 1, -(-(MAXLEN - 1) // tok_dev))
     window = (back + 1) * tok_dev
-    first = jnp.clip(me - back, 0, count_tok - 1 - back) * tok_dev
-    key_seg = lax.dynamic_slice_in_dim(prompt_segment_index, first, window, 0)
+    padded_seg = jnp.concatenate(
+        [jnp.full((back * tok_dev,), -1, jnp.int32), prompt_segment_index]
+    )
+    key_seg = lax.dynamic_slice_in_dim(padded_seg, own_start, window, 0)
     init = (
         jnp.full((1, tok_dev), -1e30, jnp.float32),
         jnp.zeros((1, tok_dev), jnp.float32),
@@ -103,21 +106,21 @@
         kv_tok.reshape(tok_dev, heads_dev * 2 * HEAD_SIZE),
         preferred_element_type=jnp.float32,
     ).astype(jnp.bfloat16).reshape(count_tok, capacity, heads_dev * 2 * HEAD_SIZE)
-    gathered = []
-    for head in range(heads_dev):
-        gathered.append(lax.all_gather(kv_tok[:, head : head + 1], "tok", axis=0, tiled=True))
+    blocks = [kv_tok]
+    for shift in range(1, back + 1):
+        pairs = [(j, j + shift) for j in range(count_tok - shift)]
+        blocks.append(lax.ppermute(kv_tok, "tok", pairs))
+    gathered_all = jnp.concatenate(blocks[::-1], axis=0)
     received = lax.all_to_all(outgoing, "tok", split_axis=0, concat_axis=0, tiled=True)
-    received, gathered[0] = lax.optimization_barrier((received, gathered[0]))
+    received, gathered_all = lax.optimization_barrier((received, gathered_all))
     states = []
     for head in range(heads_dev):
-        gathered_kv = gathered[head]
+        gathered_kv = gathered_all[:, head : head + 1]
         if head > 0:
             gathered_kv, _ = lax.optimization_barrier((gathered_kv, states[-1]))
-        piece = lax.dynamic_slice_in_dim(gathered_kv, first, window, 0)
+        piece = gathered_kv
         states.append(
-            fold_piece(
-                init, piece, query[head : head + 1], own_seg, own_start - first, key_seg, scale
-            )
+            fold_piece(init, piece, query[head : head + 1], own_seg, back * tok_dev, key_seg, scale)
         )
     state = tuple(jnp.concatenate(parts, axis=0) for parts in zip(*states))
     attended = (state[2] / state[1][:, :, None]).astype(jnp.bfloat16)

time: 255 us -> 286 us (1.12)
  starting transfers between devices: 7.42 us -> 81.3 us
  waiting for transfers between devices: 173 us -> 116 us
  local copies, waits for them, and re-layouts: 13.8 us -> 28.9 us
    all_gather x2 -> x0, waiting for transfers between devices: 81.2 us -> none  [shards_body(): lax.all_gather(kv_tok[:, head:head + 1], 'tok', axis=0, tiled=True)]
    ppermute x0 -> x9, starting transfers between devices: none -> 77.6 us  [shards_body(): blocks.append(lax.ppermute(kv_tok, 'tok', pairs))]
    reduce_scatter x1, waiting for transfers between devices: 32.2 us -> 79.3 us  [shards_body(): lax.psum_scatter(jnp.dot(attended, output_projection_weight, preferred_el...]
    all_to_all x1, waiting for transfers between devices: 21 us -> 0.01 us  [shards_body(): lax.all_to_all(outgoing, 'tok', split_axis=0, concat_axis=0, tiled=True)]
    unnamed x14 -> x23, local copies, waits for them, and re-layouts: 11.1 us -> 24.3 us
    all_to_all x1, starting transfers between devices: 7.04 us -> 3.66 us  [shards_body(): lax.all_to_all(outgoing, 'tok', split_axis=0, concat_axis=0, tiled=True)]
  transfers between devices with their start and end apart: 6 -> 13, of which waited for: 6 -> 4; matrix products, arithmetic and copies ran while one was open for 11% -> 11% of each run, Pallas kernels for 0% -> 0%
where the time goes in v3:
time: 286 us; the launch traced here: 285 us
  waiting for transfers between devices  116 us (41%)
  starting transfers between devices  81.3 us (28%)
  local copies, waits for them, and re-layouts  28.9 us (10%)
  matrix products  27.2 us (10%)
  other arithmetic  14.3 us (5%)
  between operations  14 us (5%)
    reduce_scatter x1, waiting for transfers between devices, shards_body(): lax.psum_scatter(jnp.dot(attended, output_projection_weight, preferred_el...  79.3 us
    ppermute x9, starting transfers between devices, shards_body(): blocks.append(lax.ppermute(kv_tok, 'tok', pairs))  77.6 us
    unnamed x23, local copies, waits for them, and re-layouts  24.3 us
    all_gather x1, waiting for transfers between devices, shards_body(): gathered = lax.all_gather(block_input_rows, 'row', axis=0, tiled=True)  23.3 us
    reduce_scatter x1, waiting for transfers between devices, shards_body(): lax.psum_scatter(main + adapter_down_output, 'col', scatter_dimension=0,...  12.6 us
    reduce_sum x2, other arithmetic, fold_piece(): total_new = jnp.sum(weights.astype(jnp.float32), axis=2)  8.61 us
    dot_general x2, matrix products, fold_piece(): jnp.einsum('htd,shd->hts', query, piece[:, :, 0], preferred_element_type=...  7.98 us
    dot_general x1, matrix products, shards_body(): jnp.einsum('td,dhe->hte', normalized_input, flat_weight, preferred_elemen...  6.4 us
  transfers between devices with their start and end apart: 13, of which 4 were waited for; matrix products, arithmetic and copies ran while one was open for 11% of the time, Pallas kernels for 0%

profile of v3, /device:TPU:0, one launch (start us, length us, event | category | flops | bytes accessed | tf_op | source)
XLA Modules:
  0.0 284.5 jit_solution(1550495616392718038)
XLA Ops:
  7.2 0.0 copy-start
  7.2 0.0 all-gather.2.cloned.1.call-start
  7.2 0.7 all-gather.2.cloned.1.call-update
  7.9 0.0 reduce-scatter.3.cloned.1.call-start
  8.0 0.7 convert_element_type.47
  8.7 10.7 %copy.10 = bf16[2048,4,3,128]{0,3,2,1:T(8,128)(2,1)} copy(bf16[2048,4,3,128]{3,1,2,0:T(4,128)(2,1)} %param.10) | data formatting | bytes 12582912 | tf_op args[2]
  19.4 0.3 copy.12
  19.7 23.3 %all-gather.2.cloned.1.call-done = bf16[512,2048]{1,0:T(8,128)(2,1)} async-done(((bf16[128,2048]{1,0:T(8,128)(2,1)}), bf16[512,2048]{1,0:T(8,128)(2,1)}) %all-gather.2.cloned.1.call-update) | async-done | bytes 2097168 | tf_op jit(solution)/shard_map/all_gather | solution.py:48
  43.0 2.1 fusion.1
  45.0 2.5 psum.7
  47.5 6.4 %fusion.4 = f32[512,4,384]{2,0,1:T(8,128)S(1)} fusion(bf16[2048,4,384]{0,2,1:T(8,128)(2,1)} %bitcast.91, bf16[512,2048]{1,0:T(8,128)(2,1)} %all-gather.2.cloned.1.call-done, f32[2048]{0:T(1024)S(1)} %convert_element_type.47, f32[512]{0:T(512)S(1)} %add_rsqrt_fusion), kind=kOutput, calls=%fused_computation.15 | convolution fusion | flops 3225419776 | bytes 11544576 | tf_op jit(solution)/shard_map/td,dhe->hte/dot_general | solution.py:66
  53.9 0.8 convolution_bitcast_fusion
  54.7 0.0 copy-start.4
  54.7 3.2 %add_bitcast_fusion = f32[4,512,384]{2,1,0:T(8,128)} fusion(f32[512,4,384]{2,0,1:T(8,128)S(1)} %fusion.4, f32[512,128,1]{1,0,2:T(8,128)S(1)} %convolution_bitcast_fusion, bf16[128,4,384]{0,2,1:T(8,128)(2,1)S(1)} %bitcast.97), kind=kOutput, calls=%fused_computation.13 | convolution fusion | flops 1208745984 | bytes 6946816 | tf_op jit(solution)/shard_map/tr,rhe->hte/dot_general | solution.py:69
  57.9 0.0 reduce-scatter.3.cloned.1.call-update
  57.9 1.2 reduce-window.6
  59.1 0.2 slice_reduce_fusion
  59.4 0.1 fusion.32
  59.5 12.6 %reduce-scatter.3.cloned.1.call-done = f32[2,512,384]{2,1,0:T(8,128)} async-done(((f32[4,512,384]{2,1,0:T(8,128)}), f32[2,512,384]{2,1,0:T(8,128)}) %reduce-scatter.3.cloned.1.call-update) | async-done | bytes 1572880 | tf_op jit(solution)/shard_map/reduce_scatter | solution.py:75
  72.0 1.5 convert_element_type.49
  73.5 0.3 copy.14
  73.8 0.1 slice_bitcast_fusion.4
  73.9 6.8 %collective-permute-start = (bf16[512,2,2,128]{0,3,2,1:T(8,128)(2,1)S(1)}, bf16[512,2,2,128]{0,3,2,1:T(8,128)(2,1)}, u32[]{:S(2)}, u32[]{:S(2)}) collective-permute-start(bf16[512,2,2,128]{0,3,2,1:T(8,128)(2,1)S(1)} %get-tuple-element.12), channel_id=1, source_target_pairs={{0,72},{8,80},{16,88},{24,96},{32,104},{40,112},{48,120},{1,73},{9... | collective-permute-start | bytes 1572872 | tf_op jit(solution)/shard_map/ppermute | solution.py:112
  80.7 2.1 collective-permute-start.1
  82.8 0.1 pad_dynamic-slice_fusion
  82.9 3.9 %collective-permute-start.2 = (bf16[512,2,2,128]{0,3,2,1:T(8,128)(2,1)S(1)}, bf16[512,2,2,128]{0,3,2,1:T(8,128)(2,1)}, u32[]{:S(2)}, u32[]{:S(2)}) collective-permute-start(bf16[512,2,2,128]{0,3,2,1:T(8,128)(2,1)S(1)} %get-tuple-element.12), channel_id=1, source_target_pairs={{0,56},{8,64},{16,72},{24,80},{32,88},{40,96},{48,104},{56,112},{6... | collective-permute-start | bytes 1572872 | tf_op jit(solution)/shard_map/ppermute | solution.py:112
  86.8 0.1 dynamic_slice.6
  86.9 3.8 %collective-permute-start.3 = (bf16[512,2,2,128]{0,3,2,1:T(8,128)(2,1)S(1)}, bf16[512,2,2,128]{0,3,2,1:T(8,128)(2,1)}, u32[]{:S(2)}, u32[]{:S(2)}) collective-permute-start(bf16[512,2,2,128]{0,3,2,1:T(8,128)(2,1)S(1)} %get-tuple-element.12), channel_id=1, source_target_pairs={{0,48},{8,56},{16,64},{24,72},{32,80},{40,88},{48,96},{56,104},{64... | collective-permute-start | bytes 1572872 | tf_op jit(solution)/shard_map/ppermute | solution.py:112
  90.7 2.1 collective-permute-start.4
  92.8 1.7 fusion.7
  94.5 3.7 %all-to-all-start = ((bf16[16,64,512]{2,1,0:T(8,128)(2,1)}), bf16[16,64,512]{2,1,0:T(8,128)(2,1)S(1)}, u32[]{:S(2)}, u32[]{:S(2)}) async-start(bf16[16,64,512]{2,1,0:T(8,128)(2,1)} %bitcast.98), calls=%async_computation.1 | async-start | bytes 2097152 | tf_op jit(solution)/shard_map/all_to_all | solution.py:114
  98.1 0.0 reduce-scatter.5.cloned.1.call-start
  98.2 3.8 %collective-permute-start.5 = (bf16[512,2,2,128]{0,3,2,1:T(8,128)(2,1)S(1)}, bf16[512,2,2,128]{0,3,2,1:T(8,128)(2,1)S(1)}, u32[]{:S(2)}, u32[]{:S(2)}) collective-permute-start(bf16[512,2,2,128]{0,3,2,1:T(8,128)(2,1)S(1)} %get-tuple-element.12), channel_id=1, source_target_pairs={{0,32},{8,40},{16,48},{24,56},{32,64},{40,72},{48,80},{56,88},{64,... | collective-permute-start | bytes 1572872 | tf_op jit(solution)/shard_map/ppermute | solution.py:112
  102.0 2.0 constant_dynamic-update-slice_fusion.9
  103.9 50.5 %collective-permute-start.6 = (bf16[512,2,2,128]{0,3,2,1:T(8,128)(2,1)S(1)}, bf16[512,2,2,128]{0,3,2,1:T(8,128)(2,1)S(1)}, u32[]{:S(2)}, u32[]{:S(2)}) collective-permute-start(bf16[512,2,2,128]{0,3,2,1:T(8,128)(2,1)S(1)} %get-tuple-element.12), channel_id=1, source_target_pairs={{0,24},{8,32},{16,40},{24,48},{32,56},{40,64},{48,72},{56,80},{64,... | collective-permute-start | bytes 1572872 | tf_op jit(solution)/shard_map/ppermute | solution.py:112
  154.4 2.0 constant_dynamic-update-slice_fusion.8
  156.4 1.3 collective-permute-start.7
  157.7 1.9 constant_dynamic-update-slice_fusion.7
  159.6 0.0 collective-permute-done.3
  159.6 3.4 %collective-permute-start.8 = (bf16[512,2,2,128]{0,3,2,1:T(8,128)(2,1)S(1)}, bf16[512,2,2,128]{0,3,2,1:T(8,128)(2,1)S(1)}, u32[]{:S(2)}, u32[]{:S(2)}) collective-permute-start(bf16[512,2,2,128]{0,3,2,1:T(8,128)(2,1)S(1)} %get-tuple-element.12), channel_id=1, source_target_pairs={{0,8},{8,16},{16,24},{24,32},{32,40},{40,48},{48,56},{56,64},{64,7... | collective-permute-start | bytes 1572872 | tf_op jit(solution)/shard_map/ppermute | solution.py:112
  163.0 1.9 constant_dynamic-update-slice_fusion.6
  164.9 0.0 collective-permute-done.4
  164.9 1.9 constant_dynamic-update-slice_fusion.5
  166.8 0.0 collective-permute-done.5
  166.8 0.9 constant_dynamic-update-slice_fusion.4
  167.7 0.0 collective-permute-done.6
  167.7 0.9 constant_dynamic-update-slice_fusion.3
  168.6 0.0 collective-permute-done.7
  168.6 0.9 constant_dynamic-update-slice_fusion.2
  169.4 0.6 collective-permute-done.8
  170.0 0.9 constant_dynamic-update-slice_fusion.1
  170.9 0.9 constant_dynamic-update-slice_fusion
  171.8 1.9 slice.45
  173.7 4.6 %select_reduce_fusion.1 = (f32[512]{0:T(512)S(1)}, f32[512,5120]{1,0:T(8,128)S(1)}) fusion(s32[512]{0:T(512)S(1)} %iota_add_fusion, s32[5120]{0:T(1024)S(1)} %pad_dynamic-slice_fusion, s32[512]{0:T(512)S(1)} %dynamic_slice.6, bf16[5120,2,2,128]{0,3,2,1:T(8,128)(2,1)} %constant_dynamic-update-slice_fusion, bf16[2,512,3,128]{1,3,2,0:T(8,128)(2,1)S(1)} %bitcast.94), kind=kOutput, calls=%fused_computation.5 | convolution fusion | flops 686816768 | bytes 11954176 | tf_op jit(solution)/shard_map/htd,shd->hts/dot_general | solution.py:24
  178.4 4.4 %convert_reduce_fusion.1 = (f32[512]{0:T(512)S(1)}, bf16[512,5120]{1,0:T(8,128)(2,1)S(1)}) fusion(f32[512]{0:T(512)S(1)} %broadcast_maximum_fusion.1, f32[512,5120]{1,0:T(8,128)S(1)} %get-tuple-element.15, s32[512]{0:T(512)S(1)} %iota_add_fusion, s32[5120]{0:T(1024)S(1)} %pad_dynamic-slice_fusion, s32[512]{0:T(512)S(1)} %dynamic_slice.6), kind=kLoop, calls=%fused_computation.3 | loop fusion | flops 23592448 | bytes 15757312 | tf_op jit(solution)/shard_map/reduce_sum | solution.py:32
  182.8 3.2 %fusion.20 = f32[1,512,128]{1,2,0:T(8,128)S(1)} fusion(bf16[512,5120]{1,0:T(8,128)(2,1)S(1)} %get-tuple-element.11, bf16[5120,2,2,128]{0,3,2,1:T(8,128)(2,1)} %constant_dynamic-update-slice_fusion), kind=kOutput, calls=%fused_computation.33 | convolution fusion | flops 671088640 | bytes 6815744 | tf_op jit(solution)/shard_map/hts,shd->htd/dot_general | solution.py:33
  186.0 3.3 %select_reduce_fusion = (f32[512]{0:T(512)S(1)}, f32[512,5120]{1,0:T(8,128)S(1)}) fusion(s32[512]{0:T(512)S(1)} %iota_add_fusion, s32[5120]{0:T(1024)S(1)} %pad_dynamic-slice_fusion, s32[512]{0:T(512)S(1)} %dynamic_slice.6, bf16[5120,1,2,128]{0,3,2,1:T(8,128)(2,1)S(1)} %slice.45, bf16[2,512,3,128]{1,3,2,0:T(8,128)(2,1)S(1)} %bitcast.95), kind=kOutput, calls=%fused_computation.2 | convolution fusion | flops 686816768 | bytes 11954176 | tf_op jit(solution)/shard_map/htd,shd->hts/dot_general | solution.py:24
  189.3 4.2 %convert_reduce_fusion = (f32[512]{0:T(512)S(1)}, bf16[512,5120]{1,0:T(8,128)(2,1)S(1)}) fusion(f32[512]{0:T(512)S(1)} %broadcast_maximum_fusion, f32[512,5120]{1,0:T(8,128)S(1)} %get-tuple-element.17, s32[512]{0:T(512)S(1)} %iota_add_fusion, s32[5120]{0:T(1024)S(1)} %pad_dynamic-slice_fusion, s32[512]{0:T(512)S(1)} %dynamic_slice.6), kind=kLoop, calls=%fused_computation | loop fusion | flops 23592448 | bytes 15757312 | tf_op jit(solution)/shard_map/reduce_sum | solution.py:32
  193.6 1.9 fusion.23
  195.5 0.1 fusion.29
  195.5 2.1 convolution_convert_fusion
  197.6 0.0 reduce-scatter.5.cloned.1.call-update
  197.7 1.1 reshape.139
  198.8 79.3 %reduce-scatter.5.cloned.1.call-done = bf16[64,2048]{1,0:T(8,128)(2,1)} async-done(((bf16[512,2048]{1,0:T(8,128)(2,1)}), bf16[64,2048]{1,0:T(8,128)(2,1)}) %reduce-scatter.5.cloned.1.call-update) | async-done | bytes 262160 | tf_op jit(solution)/shard_map/reduce_scatter | solution.py:128
  (23 shorter events, 0.1 us)
Async XLA Ops:
  7.2 188.4 %copy-start = (bf16[256,2048]{1,0:T(8,128)(2,1)S(1)}, bf16[256,2048]{1,0:T(8,128)(2,1)}, u32[]{:S(2)}) copy-start(bf16[256,2048]{1,0:T(8,128)(2,1)} %param.13) | copy-start | bytes 3145732
  7.2 35.8 %all-gather.2.cloned.1.call-start = ((), (), s32[]{:S(2)}) async-start(), calls=%async_computation.3 | async-start | bytes 2621440 | tf_op jit(solution)/shard_map/all_gather | solution.py:48
  7.9 64.1 %reduce-scatter.3.cloned.1.call-start = ((), (), s32[]{:S(2)}) async-start(), calls=%async_computation.4 | async-start | bytes 4718592 | tf_op jit(solution)/shard_map/reduce_scatter | solution.py:75
  8.7 10.7 %copy-start.2 = (bf16[128,4,3,128]{3,1,2,0:T(4,128)(2,1)S(1)}, bf16[128,4,3,128]{3,1,2,0:T(4,128)(2,1)}, u32[]{:S(2)}) copy-start(bf16[128,4,3,128]{3,1,2,0:T(4,128)(2,1)} %param.12) | copy-start | bytes 1179652
  47.5 6.4 %copy-start.1 = (bf16[512,2048]{1,0:T(8,128)(2,1)S(1)}, bf16[512,2048]{1,0:T(8,128)(2,1)}, u32[]{:S(2)}) copy-start(bf16[512,2048]{1,0:T(8,128)(2,1)} %all-gather.2.cloned.1.call-done) | copy-start | bytes 6291460
  47.5 6.4 %copy-start.5 = (bf16[2048,128]{1,0:T(8,128)(2,1)S(1)}, bf16[2048,128]{1,0:T(8,128)(2,1)}, u32[]{:S(2)}) copy-start(bf16[2048,128]{1,0:T(8,128)(2,1)} %param.11) | copy-start | bytes 1572868
  54.7 3.2 %copy-start.4 = (s32[512,1]{0,1:T(1,128)S(1)}, s32[512,1]{0,1:T(1,128)}, u32[]{:S(2)}) copy-start(s32[512,1]{0,1:T(1,128)} %param.15) | copy-start | bytes 6148
  57.9 24.9 %copy-start.3 = (s32[8192]{0:T(1024)S(1)}, s32[8192]{0:T(1024)}, u32[]{:S(2)}) copy-start(s32[8192]{0:T(1024)} %param.14) | copy-start | bytes 98308
  73.9 24.3 %collective-permute-start = (bf16[512,2,2,128]{0,3,2,1:T(8,128)(2,1)S(1)}, bf16[512,2,2,128]{0,3,2,1:T(8,128)(2,1)}, u32[]{:S(2)}, u32[]{:S(2)}) collective-permute-start(bf16[512,2,2,128]{0,3,2,1:T(8,128)(2,1)S(1)} %get-tuple-element.12), channel_id=1, source_target_pairs={{0,72},{8,80},{16,88},{24,96},{32,104},{40,112},{48,120},{1,73},{9... | collective-permute-start | bytes 1572872 | tf_op jit(solution)/shard_map/ppermute | solution.py:112
  80.7 23.2 %collective-permute-start.1 = (bf16[512,2,2,128]{0,3,2,1:T(8,128)(2,1)S(1)}, bf16[512,2,2,128]{0,3,2,1:T(8,128)(2,1)}, u32[]{:S(2)}, u32[]{:S(2)}) collective-permute-start(bf16[512,2,2,128]{0,3,2,1:T(8,128)(2,1)S(1)} %get-tuple-element.12), channel_id=1, source_target_pairs={{0,64},{8,72},{16,80},{24,88},{32,96},{40,104},{48,112},{56,120},{... | collective-permute-start | bytes 1572872 | tf_op jit(solution)/shard_map/ppermute | solution.py:112
  82.9 73.5 %collective-permute-start.2 = (bf16[512,2,2,128]{0,3,2,1:T(8,128)(2,1)S(1)}, bf16[512,2,2,128]{0,3,2,1:T(8,128)(2,1)}, u32[]{:S(2)}, u32[]{:S(2)}) collective-permute-start(bf16[512,2,2,128]{0,3,2,1:T(8,128)(2,1)S(1)} %get-tuple-element.12), channel_id=1, source_target_pairs={{0,56},{8,64},{16,72},{24,80},{32,88},{40,96},{48,104},{56,112},{6... | collective-permute-start | bytes 1572872 | tf_op jit(solution)/shard_map/ppermute | solution.py:112
  86.9 72.7 %collective-permute-start.3 = (bf16[512,2,2,128]{0,3,2,1:T(8,128)(2,1)S(1)}, bf16[512,2,2,128]{0,3,2,1:T(8,128)(2,1)}, u32[]{:S(2)}, u32[]{:S(2)}) collective-permute-start(bf16[512,2,2,128]{0,3,2,1:T(8,128)(2,1)S(1)} %get-tuple-element.12), channel_id=1, source_target_pairs={{0,48},{8,56},{16,64},{24,72},{32,80},{40,88},{48,96},{56,104},{64... | collective-permute-start | bytes 1572872 | tf_op jit(solution)/shard_map/ppermute | solution.py:112
  90.7 74.2 %collective-permute-start.4 = (bf16[512,2,2,128]{0,3,2,1:T(8,128)(2,1)S(1)}, bf16[512,2,2,128]{0,3,2,1:T(8,128)(2,1)}, u32[]{:S(2)}, u32[]{:S(2)}) collective-permute-start(bf16[512,2,2,128]{0,3,2,1:T(8,128)(2,1)S(1)} %get-tuple-element.12), channel_id=1, source_target_pairs={{0,40},{8,48},{16,56},{24,64},{32,72},{40,80},{48,88},{56,96},{64,... | collective-permute-start | bytes 1572872 | tf_op jit(solution)/shard_map/ppermute | solution.py:112
  94.5 77.3 %all-to-all-start = ((bf16[16,64,512]{2,1,0:T(8,128)(2,1)}), bf16[16,64,512]{2,1,0:T(8,128)(2,1)S(1)}, u32[]{:S(2)}, u32[]{:S(2)}) async-start(bf16[16,64,512]{2,1,0:T(8,128)(2,1)} %bitcast.98), calls=%async_computation.1 | async-start | bytes 2097152 | tf_op jit(solution)/shard_map/all_to_all | solution.py:114
  98.1 179.9 %reduce-scatter.5.cloned.1.call-start = ((), (), s32[]{:S(2)}) async-start(), calls=%async_computation.5 | async-start | bytes 2359296 | tf_op jit(solution)/shard_map/reduce_scatter | solution.py:128
  98.2 68.6 %collective-permute-start.5 = (bf16[512,2,2,128]{0,3,2,1:T(8,128)(2,1)S(1)}, bf16[512,2,2,128]{0,3,2,1:T(8,128)(2,1)S(1)}, u32[]{:S(2)}, u32[]{:S(2)}) collective-permute-start(bf16[512,2,2,128]{0,3,2,1:T(8,128)(2,1)S(1)} %get-tuple-element.12), channel_id=1, source_target_pairs={{0,32},{8,40},{16,48},{24,56},{32,64},{40,72},{48,80},{56,88},{64,... | collective-permute-start | bytes 1572872 | tf_op jit(solution)/shard_map/ppermute | solution.py:112
  103.9 63.8 %collective-permute-start.6 = (bf16[512,2,2,128]{0,3,2,1:T(8,128)(2,1)S(1)}, bf16[512,2,2,128]{0,3,2,1:T(8,128)(2,1)S(1)}, u32[]{:S(2)}, u32[]{:S(2)}) collective-permute-start(bf16[512,2,2,128]{0,3,2,1:T(8,128)(2,1)S(1)} %get-tuple-element.12), channel_id=1, source_target_pairs={{0,24},{8,32},{16,40},{24,48},{32,56},{40,64},{48,72},{56,80},{64,... | collective-permute-start | bytes 1572872 | tf_op jit(solution)/shard_map/ppermute | solution.py:112
  156.4 12.2 %collective-permute-start.7 = (bf16[512,2,2,128]{0,3,2,1:T(8,128)(2,1)S(1)}, bf16[512,2,2,128]{0,3,2,1:T(8,128)(2,1)S(1)}, u32[]{:S(2)}, u32[]{:S(2)}) collective-permute-start(bf16[512,2,2,128]{0,3,2,1:T(8,128)(2,1)S(1)} %get-tuple-element.12), channel_id=1, source_target_pairs={{0,16},{8,24},{16,32},{24,40},{32,48},{40,56},{48,64},{56,72},{64,... | collective-permute-start | bytes 1572872 | tf_op jit(solution)/shard_map/ppermute | solution.py:112
  159.6 10.4 %collective-permute-start.8 = (bf16[512,2,2,128]{0,3,2,1:T(8,128)(2,1)S(1)}, bf16[512,2,2,128]{0,3,2,1:T(8,128)(2,1)S(1)}, u32[]{:S(2)}, u32[]{:S(2)}) collective-permute-start(bf16[512,2,2,128]{0,3,2,1:T(8,128)(2,1)S(1)} %get-tuple-element.12), channel_id=1, source_target_pairs={{0,8},{8,16},{16,24},{24,32},{32,40},{40,48},{48,56},{56,64},{64,7... | collective-permute-start | bytes 1572872 | tf_op jit(solution)/shard_map/ppermute | solution.py:112
Sparse Core Ops, SparseCore 0:
  9.6 33.2 all-gather.1
  58.0 13.9 reduce-scatter.2
  197.8 80.1 reduce-scatter.4

commit v4 on v2

--- a/solution.py
+++ b/solution.py
@@ -103,14 +103,10 @@
         kv_tok.reshape(tok_dev, heads_dev * 2 * HEAD_SIZE),
         preferred_element_type=jnp.float32,
     ).astype(jnp.bfloat16).reshape(count_tok, capacity, heads_dev * 2 * HEAD_SIZE)
-    gathered = []
-    for head in range(heads_dev):
-        gathered.append(lax.all_gather(kv_tok[:, head : head + 1], "tok", axis=0, tiled=True))
-    received = lax.all_to_all(outgoing, "tok", split_axis=0, concat_axis=0, tiled=True)
-    received, gathered[0] = lax.optimization_barrier((received, gathered[0]))
+    gathered_all = lax.all_gather(kv_tok, "tok", axis=0, tiled=True)
     states = []
     for head in range(heads_dev):
-        gathered_kv = gathered[head]
+        gathered_kv = gathered_all[:, head : head + 1]
         if head > 0:
             gathered_kv, _ = lax.optimization_barrier((gathered_kv, states[-1]))
         piece = lax.dynamic_slice_in_dim(gathered_kv, first, window, 0)
@@ -120,6 +116,8 @@
             )
         )
     state = tuple(jnp.concatenate(parts, axis=0) for parts in zip(*states))
+    outgoing, _ = lax.optimization_barrier((outgoing, states[-1]))
+    received = lax.all_to_all(outgoing, "tok", split_axis=0, concat_axis=0, tiled=True)
     attended = (state[2] / state[1][:, :, None]).astype(jnp.bfloat16)
     attended = jnp.transpose(attended, (1, 0, 2)).reshape(tok_dev, heads_dev * HEAD_SIZE)
     block_output = lax.psum_scatter(

time: 255 us -> 219 us (0.86)
  waiting for transfers between devices: 173 us -> 127 us
  blocking collectives: 2.47 us -> 22.9 us
  starting transfers between devices: 7.42 us -> 0.34 us
  matrix products: 29.8 us -> 23.7 us
  local copies, waits for them, and re-layouts: 13.8 us -> 17.6 us
    reduce_scatter x1, waiting for transfers between devices: 32.2 us -> 9.77 us  [shards_body(): lax.psum_scatter(jnp.dot(attended, output_projection_weight, preferred_el...]
    all_to_all x1 -> x0, waiting for transfers between devices: 21 us -> none  [shards_body(): lax.all_to_all(outgoing, 'tok', split_axis=0, concat_axis=0, tiled=True)]
    all_to_all x0 -> x1, blocking collectives: none -> 20.4 us  [shards_body(): lax.all_to_all(outgoing, 'tok', split_axis=0, concat_axis=0, tiled=True)]
    all_to_all x1 -> x0, starting transfers between devices: 7.04 us -> none  [shards_body(): lax.all_to_all(outgoing, 'tok', split_axis=0, concat_axis=0, tiled=True)]
    slice x2, local copies, waits for them, and re-layouts: 1.05 us -> 4.11 us  [the longest x1 3.89 us: shards_body(): gathered_kv = gathered_all[:, head:head + 1]]
    all_gather x2 -> x1, waiting for transfers between devices: 81.2 us -> 78.5 us  [shards_body(): gathered_all = lax.all_gather(kv_tok, 'tok', axis=0, tiled=True)]
    dot_general x2, matrix products: 9.27 us -> 6.61 us  [fold_piece(): jnp.einsum('htd,shd->hts', query, piece[:, :, 0], preferred_element_type=...]
    unnamed x14 -> x16, local copies, waits for them, and re-layouts: 11.1 us -> 11.1 us
  transfers between devices with their start and end apart: 6 -> 4, of which waited for: 6 -> 4; matrix products, arithmetic and copies ran while one was open for 11% -> 7% of each run, Pallas kernels for 0% -> 0%
where the time goes in v4:
time: 219 us
  waiting for transfers between devices  127 us (58%)
  matrix products  23.7 us (11%)
  blocking collectives  22.9 us (10%)
  local copies, waits for them, and re-layouts  17.6 us (8%)
  between operations  14 us (6%)
  other arithmetic  13.4 us (6%)
    all_gather x1, waiting for transfers between devices, shards_body(): gathered_all = lax.all_gather(kv_tok, 'tok', axis=0, tiled=True)  78.5 us
    all_gather x1, waiting for transfers between devices, shards_body(): gathered = lax.all_gather(block_input_rows, 'row', axis=0, tiled=True)  23.9 us
    all_to_all x1, blocking collectives, shards_body(): lax.all_to_all(outgoing, 'tok', split_axis=0, concat_axis=0, tiled=True)  20.4 us
    reduce_scatter x1, waiting for transfers between devices, shards_body(): lax.psum_scatter(main + adapter_down_output, 'col', scatter_dimension=0,...  14.1 us
    unnamed x16, local copies, waits for them, and re-layouts  11.1 us
    reduce_scatter x1, waiting for transfers between devices, shards_body(): lax.psum_scatter(jnp.dot(attended, output_projection_weight, preferred_el...  9.77 us
    reduce_sum x2, other arithmetic, fold_piece(): total_new = jnp.sum(weights.astype(jnp.float32), axis=2)  8.42 us
    dot_general x2, matrix products, fold_piece(): jnp.einsum('htd,shd->hts', query, piece[:, :, 0], preferred_element_type=...  6.61 us
  transfers between devices with their start and end apart: 4, of which 4 were waited for; matrix products, arithmetic and copies ran while one was open for 7% of the time, Pallas kernels for 0%

profile of v4, /device:TPU:0, one launch (start us, length us, event | category | flops | bytes accessed | tf_op | source)
XLA Modules:
  0.0 218.9 jit_solution(9330202867210430927)
XLA Ops:
  7.2 0.0 copy-start
  7.2 0.0 all-gather.3.cloned.1.call-start
  7.2 0.7 all-gather.3.cloned.1.call-update
  7.9 0.0 copy-start.5
  7.9 0.0 copy-start.2
  7.9 0.0 reduce-scatter.3.cloned.1.call-start
  8.0 10.7 %copy.10 = bf16[2048,4,3,128]{0,3,2,1:T(8,128)(2,1)} copy(bf16[2048,4,3,128]{3,1,2,0:T(4,128)(2,1)} %param.10) | data formatting | bytes 12582912 | tf_op args[2]
  18.7 0.0 copy-done.5
  18.7 0.0 copy-done.2
  18.7 0.3 copy.12
  19.0 23.9 %all-gather.3.cloned.1.call-done = bf16[512,2048]{1,0:T(8,128)(2,1)} async-done(((bf16[128,2048]{1,0:T(8,128)(2,1)}), bf16[512,2048]{1,0:T(8,128)(2,1)}) %all-gather.3.cloned.1.call-update) | async-done | bytes 2097168 | tf_op jit(solution)/shard_map/all_gather | solution.py:47
  43.0 2.1 fusion.1
  45.0 2.5 %psum.7 = f32[512]{0:T(512)S(1)} all-reduce(f32[512]{0:T(512)S(1)} %fusion.1), channel_id=1, replica_groups=mesh['tok'=16,'row'=4,'col'=2] {'col'}, use_global_device_ids=true, to_apply=%region_1.0 | all-reduce | flops 512 | bytes 4096 | tf_op jit(solution)/shard_map/psum | solution.py:50
  47.5 0.0 copy-start.1
  47.5 0.0 copy-start.6
  47.5 6.4 %fusion.4 = f32[512,4,384]{2,0,1:T(8,128)S(1)} fusion(bf16[2048,4,384]{0,2,1:T(8,128)(2,1)} %bitcast.90, bf16[512,2048]{1,0:T(8,128)(2,1)} %all-gather.3.cloned.1.call-done, f32[2048]{0:T(1024)S(1)} %convert_element_type.47, f32[512]{0:T(512)S(1)} %add_rsqrt_fusion), kind=kOutput, calls=%fused_computation.15 | convolution fusion | flops 3225419776 | bytes 11544576 | tf_op jit(solution)/shard_map/td,dhe->hte/dot_general | solution.py:65
  53.9 0.0 copy-done.1
  53.9 0.0 copy-done.6
  54.0 0.8 convolution_bitcast_fusion
  54.7 3.2 %add_bitcast_fusion = f32[4,512,384]{2,1,0:T(8,128)} fusion(f32[512,4,384]{2,0,1:T(8,128)S(1)} %fusion.4, f32[512,128,1]{1,0,2:T(8,128)S(1)} %convolution_bitcast_fusion, bf16[128,4,384]{0,2,1:T(8,128)(2,1)S(1)} %bitcast.95), kind=kOutput, calls=%fused_computation.13 | convolution fusion | flops 1208745984 | bytes 6946816 | tf_op jit(solution)/shard_map/tr,rhe->hte/dot_general | solution.py:68
  57.9 0.0 copy-start.4
  57.9 0.0 reduce-scatter.3.cloned.1.call-update
  57.9 0.0 all-gather.5.cloned.1.call-start
  58.0 14.1 %reduce-scatter.3.cloned.1.call-done = f32[2,512,384]{2,1,0:T(8,128)} async-done(((f32[4,512,384]{2,1,0:T(8,128)}), f32[2,512,384]{2,1,0:T(8,128)}) %reduce-scatter.3.cloned.1.call-update) | async-done | bytes 1572880 | tf_op jit(solution)/shard_map/reduce_scatter | solution.py:74
  72.0 1.5 convert_element_type.49
  73.5 0.3 copy.14
  73.8 0.9 fusion.27
  74.7 0.0 all-gather.5.cloned.1.call-update
  74.7 0.2 reduce-scatter.5.cloned.1.call-start
  75.0 0.0 copy-done.4
  75.0 0.1 dynamic_slice.13
  75.1 0.1 dynamic_slice.12
  75.1 78.5 %all-gather.5.cloned.1.call-done = bf16[8192,2,2,128]{0,3,2,1:T(8,128)(2,1)} async-done(((bf16[512,2,2,128]{0,3,2,1:T(8,128)(2,1)}), bf16[8192,2,2,128]{0,3,2,1:T(8,128)(2,1)}) %all-gather.5.cloned.1.call-update) | async-done | bytes 8388624 | tf_op jit(solution)/shard_map/all_gather | solution.py:106
  153.6 3.9 %fusion.26 = (bf16[8192,1,2,128]{0,3,2,1:T(8,128)(2,1)S(1)}, bf16[8192,1,2,128]{0,3,2,1:T(8,128)(2,1)S(1)}) fusion(bf16[8192,2,2,128]{0,3,2,1:T(8,128)(2,1)} %all-gather.5.cloned.1.call-done), kind=kLoop, calls=%fused_computation.56 | loop fusion | bytes 16777216 | tf_op jit(solution)/shard_map/slice | solution.py:109
  157.5 3.3 %select_reduce_fusion.1 = (f32[512]{0:T(512)S(1)}, f32[512,5120]{1,0:T(8,128)S(1)}) fusion(s32[512]{0:T(512)S(1)} %iota_add_fusion, s32[5120]{0:T(1024)S(1)} %dynamic_slice.13, s32[512]{0:T(512)S(1)} %dynamic_slice.12, bf16[8192,1,2,128]{0,3,2,1:T(8,128)(2,1)S(1)} %get-tuple-element.10, s32[]{:T(128)S(6)} %select_n.26, bf16[2,512,3,128]{1,3,2,0:T(8,128)(2,1)S(1)} %bitcast.92), kind=kOutput, calls=%fused_computation.5 | convolution fusion | flops 686816768 | bytes 11954180 | tf_op jit(solution)/shard_map/htd,shd->hts/dot_general | solution.py:23
  160.8 4.2 %convert_reduce_fusion.1 = (f32[512]{0:T(512)S(1)}, bf16[512,5120]{1,0:T(8,128)(2,1)S(1)}) fusion(f32[512]{0:T(512)S(1)} %broadcast_maximum_fusion.1, f32[512,5120]{1,0:T(8,128)S(1)} %get-tuple-element.15, s32[512]{0:T(512)S(1)} %iota_add_fusion, s32[5120]{0:T(1024)S(1)} %dynamic_slice.13, s32[512]{0:T(512)S(1)} %dynamic_slice.12), kind=kLoop, calls=%fused_computation.3 | loop fusion | flops 23592448 | bytes 15757312 | tf_op jit(solution)/shard_map/reduce_sum | solution.py:31
  165.0 1.9 fusion.12
  167.0 3.3 %select_reduce_fusion = (f32[512]{0:T(512)S(1)}, f32[512,5120]{1,0:T(8,128)S(1)}) fusion(s32[512]{0:T(512)S(1)} %iota_add_fusion, s32[5120]{0:T(1024)S(1)} %dynamic_slice.13, s32[512]{0:T(512)S(1)} %dynamic_slice.12, bf16[8192,1,2,128]{0,3,2,1:T(8,128)(2,1)S(1)} %get-tuple-element.4, s32[]{:T(128)S(6)} %select_n.26, bf16[2,512,3,128]{1,3,2,0:T(8,128)(2,1)S(1)} %bitcast.93), kind=kOutput, calls=%fused_computation.2 | convolution fusion | flops 686816768 | bytes 11954180 | tf_op jit(solution)/shard_map/htd,shd->hts/dot_general | solution.py:23
  170.3 4.2 %convert_reduce_fusion = (f32[512]{0:T(512)S(1)}, bf16[512,5120]{1,0:T(8,128)(2,1)S(1)}) fusion(f32[512]{0:T(512)S(1)} %broadcast_maximum_fusion, f32[512,5120]{1,0:T(8,128)S(1)} %get-tuple-element.17, s32[512]{0:T(512)S(1)} %iota_add_fusion, s32[5120]{0:T(1024)S(1)} %dynamic_slice.13, s32[512]{0:T(512)S(1)} %dynamic_slice.12), kind=kLoop, calls=%fused_computation | loop fusion | flops 23592448 | bytes 15757312 | tf_op jit(solution)/shard_map/reduce_sum | solution.py:31
  174.5 1.9 fusion.13
  176.5 0.0 copy-start.3
  176.5 0.1 fusion.17
  176.6 0.0 copy-done
  176.6 2.1 convolution_convert_fusion
  178.7 0.0 reduce-scatter.5.cloned.1.call-update
  178.7 0.0 copy-done.3
  178.7 1.2 reduce-window.6
  179.9 0.2 slice_reduce_fusion
  180.1 0.1 fusion.20
  180.3 0.8 fusion.7
  181.0 20.4 %all_to_all.5 = bf16[16,64,512]{2,1,0:T(8,128)(2,1)S(1)} all-to-all(bf16[16,64,512]{2,1,0:T(8,128)(2,1)S(1)} %bitcast.96), channel_id=1, replica_groups=mesh['tok'=16,'row'=4,'col'=2] {'tok'}, dimensions={0} | all-to-all | bytes 2097152 | tf_op jit(solution)/shard_map/all_to_all | solution.py:120
  201.5 1.1 reshape.139
  202.6 9.8 %reduce-scatter.5.cloned.1.call-done = bf16[64,2048]{1,0:T(8,128)(2,1)} async-done(((bf16[512,2048]{1,0:T(8,128)(2,1)}), bf16[64,2048]{1,0:T(8,128)(2,1)}) %reduce-scatter.5.cloned.1.call-update) | async-done | bytes 262160 | tf_op jit(solution)/shard_map/reduce_scatter | solution.py:123
  (10 shorter events, 0.1 us)
Async XLA Ops:
  7.2 169.4 %copy-start = (bf16[256,2048]{1,0:T(8,128)(2,1)S(1)}, bf16[256,2048]{1,0:T(8,128)(2,1)}, u32[]{:S(2)}) copy-start(bf16[256,2048]{1,0:T(8,128)(2,1)} %param.13) | copy-start | bytes 3145732
  7.2 35.8 %all-gather.3.cloned.1.call-start = ((), (), s32[]{:S(2)}) async-start(), calls=%async_computation.3 | async-start | bytes 2621440 | tf_op jit(solution)/shard_map/all_gather | solution.py:47
  7.9 10.8 %copy-start.5 = (bf16[2048]{0:T(1024)(128)(2,1)S(1)}, bf16[2048]{0:T(1024)(128)(2,1)}, u32[]{:S(2)}) copy-start(bf16[2048]{0:T(1024)(128)(2,1)} %param.9) | copy-start | bytes 12292
  7.9 10.8 %copy-start.2 = (bf16[128,4,3,128]{3,1,2,0:T(4,128)(2,1)S(1)}, bf16[128,4,3,128]{3,1,2,0:T(4,128)(2,1)}, u32[]{:S(2)}) copy-start(bf16[128,4,3,128]{3,1,2,0:T(4,128)(2,1)} %param.12) | copy-start | bytes 1179652
  7.9 64.1 %reduce-scatter.3.cloned.1.call-start = ((), (), s32[]{:S(2)}) async-start(), calls=%async_computation.4 | async-start | bytes 4718592 | tf_op jit(solution)/shard_map/reduce_scatter | solution.py:74
  47.5 6.4 %copy-start.1 = (bf16[512,2048]{1,0:T(8,128)(2,1)S(1)}, bf16[512,2048]{1,0:T(8,128)(2,1)}, u32[]{:S(2)}) copy-start(bf16[512,2048]{1,0:T(8,128)(2,1)} %all-gather.3.cloned.1.call-done) | copy-start | bytes 6291460
  47.5 6.4 %copy-start.6 = (bf16[2048,128]{1,0:T(8,128)(2,1)S(1)}, bf16[2048,128]{1,0:T(8,128)(2,1)}, u32[]{:S(2)}) copy-start(bf16[2048,128]{1,0:T(8,128)(2,1)} %param.11) | copy-start | bytes 1572868
  57.9 17.1 %copy-start.4 = (s32[8192]{0:T(1024)S(1)}, s32[8192]{0:T(1024)}, u32[]{:S(2)}) copy-start(s32[8192]{0:T(1024)} %param.14) | copy-start | bytes 98308
  57.9 95.7 %all-gather.5.cloned.1.call-start = ((), (), s32[]{:S(2)}) async-start(), calls=%async_computation.5 | async-start | bytes 8912896 | tf_op jit(solution)/shard_map/all_gather | solution.py:106
  74.7 137.6 %reduce-scatter.5.cloned.1.call-start = ((), (), s32[]{:S(2)}) async-start(), calls=%async_computation.6 | async-start | bytes 2359296 | tf_op jit(solution)/shard_map/reduce_scatter | solution.py:123
  176.5 2.2 %copy-start.3 = (s32[512,1]{0,1:T(1,128)S(1)}, s32[512,1]{0,1:T(1,128)}, u32[]{:S(2)}) copy-start(s32[512,1]{0,1:T(1,128)} %param.15) | copy-start | bytes 6148
Sparse Core Ops, SparseCore 0:
  9.7 33.2 all-gather.2
  58.0 13.9 reduce-scatter.2
  74.9 78.7 all-gather.4
  178.8 33.4 reduce-scatter.4

commit v5 on v4

--- a/solution.py
+++ b/solution.py
@@ -9,30 +9,19 @@
 ADAPTER_RANK = 128
 MAXLEN = 4352
 
-def fold_piece(carry, piece, query, own_seg, own_start, prompt_segment_index, scale):
-    top_old, _, _ = carry
-    count = piece.shape[0]
+def attend_head(query, keys, values, own_seg, own_start, key_seg, scale):
+    count = keys.shape[0]
     key_pos = jnp.arange(count, dtype=jnp.int32)
-    query_pos = own_start + jnp.arange(query.shape[1], dtype=jnp.int32)
-    allowed = (
-        (own_seg[:, None] == prompt_segment_index[None, :])
-        & (key_pos[None, :] <= query_pos[:, None])
-        & (key_pos[None, :] >= 0)
-    )
-    score = (
-        jnp.einsum("htd,shd->hts", query, piece[:, :, 0], preferred_element_type=jnp.float32)
-        * scale
-    )
-    masked = jnp.where(allowed[None], score, -1e30)
-    top_new = jnp.maximum(top_old, jnp.max(masked, axis=2))
-    weights = jnp.where(allowed[None], jnp.exp(score - top_new[:, :, None]), 0.0).astype(
-        jnp.bfloat16
-    )
-    total_new = jnp.sum(weights.astype(jnp.float32), axis=2)
-    acc_new = jnp.einsum(
-        "hts,shd->htd", weights, piece[:, :, 1], preferred_element_type=jnp.float32
-    )
-    return (top_new, total_new, acc_new)
+    query_pos = own_start + jnp.arange(query.shape[0], dtype=jnp.int32)
+    allowed = (own_seg[:, None] == key_seg[None, :]) & (key_pos[None, :] <= query_pos[:, None])
+    score = jnp.dot(query, keys.T, preferred_element_type=jnp.float32) * scale
+    masked = jnp.where(allowed, score, -1e30)
+    top = jnp.max(masked, axis=1)
+    weights = jnp.where(allowed, jnp.exp(score - top[:, None]), 0.0).astype(jnp.bfloat16)
+    total = jnp.sum(weights.astype(jnp.float32), axis=1)
+    summed = jnp.dot(weights, values, preferred_element_type=jnp.float32)
+    return total, summed
+
 
 def shards_body(
     block_input_rows,
@@ -75,6 +64,7 @@
     qkv = mixed.astype(jnp.bfloat16).reshape(heads_dev, tok_dev, 3, HEAD_SIZE)
     query = qkv[:, :, 0]
     kv_tok = jnp.transpose(qkv[:, :, 1:3], (1, 0, 2, 3))
+    kv_flat = kv_tok.reshape(tok_dev, heads_dev * 2 * HEAD_SIZE)
     count_tok = lax.axis_size("tok")
     me = lax.axis_index("tok")
     own_start = me * tok_dev
@@ -84,11 +74,6 @@
     window = (back + 1) * tok_dev
     first = jnp.clip(me - back, 0, count_tok - 1 - back) * tok_dev
     key_seg = lax.dynamic_slice_in_dim(prompt_segment_index, first, window, 0)
-    init = (
-        jnp.full((1, tok_dev), -1e30, jnp.float32),
-        jnp.zeros((1, tok_dev), jnp.float32),
-        jnp.zeros((1, tok_dev, HEAD_SIZE), jnp.float32),
-    )
     capacity = max(2, 2 * tok_dev // count_tok)
     owner = cache_owner_index[:, 0]
     onehot = (owner[:, None] == jnp.arange(count_tok, dtype=jnp.int32)[None, :]).astype(jnp.int32)
@@ -100,25 +85,32 @@
     )
     outgoing = jnp.dot(
         selector,
-        kv_tok.reshape(tok_dev, heads_dev * 2 * HEAD_SIZE),
+        kv_flat,
         preferred_element_type=jnp.float32,
     ).astype(jnp.bfloat16).reshape(count_tok, capacity, heads_dev * 2 * HEAD_SIZE)
-    gathered_all = lax.all_gather(kv_tok, "tok", axis=0, tiled=True)
+    gathered_all = lax.all_gather(kv_flat, "tok", axis=0, tiled=True)
+    window_kv = lax.dynamic_slice_in_dim(gathered_all, first, window, 0)
     states = []
     for head in range(heads_dev):
-        gathered_kv = gathered_all[:, head : head + 1]
+        head_kv = window_kv[:, head * 2 * HEAD_SIZE : (head + 1) * 2 * HEAD_SIZE]
         if head > 0:
-            gathered_kv, _ = lax.optimization_barrier((gathered_kv, states[-1]))
-        piece = lax.dynamic_slice_in_dim(gathered_kv, first, window, 0)
+            head_kv, _ = lax.optimization_barrier((head_kv, states[-1]))
         states.append(
-            fold_piece(
-                init, piece, query[head : head + 1], own_seg, own_start - first, key_seg, scale
+            attend_head(
+                query[head],
+                head_kv[:, :HEAD_SIZE],
+                head_kv[:, HEAD_SIZE:],
+                own_seg,
+                own_start - first,
+                key_seg,
+                scale,
             )
         )
-    state = tuple(jnp.concatenate(parts, axis=0) for parts in zip(*states))
+    total = jnp.stack([part[0] for part in states])
+    summed = jnp.stack([part[1] for part in states])
     outgoing, _ = lax.optimization_barrier((outgoing, states[-1]))
     received = lax.all_to_all(outgoing, "tok", split_axis=0, concat_axis=0, tiled=True)
-    attended = (state[2] / state[1][:, :, None]).astype(jnp.bfloat16)
+    attended = (summed / total[:, :, None]).astype(jnp.bfloat16)
     attended = jnp.transpose(attended, (1, 0, 2)).reshape(tok_dev, heads_dev * HEAD_SIZE)
     block_output = lax.psum_scatter(
         jnp.dot(attended, output_projection_weight, preferred_element_type=jnp.float32).astype(

time: 219 us -> 220 us (level)
  matrix products: 23.7 us -> 26.2 us
    dot_general x5, matrix products: 11.3 us -> 13.8 us  [the longest x2 7.96 us: attend_head(): score = jnp.dot(query, keys.T, preferred_element_type=jnp.float32) * scale]
where the time goes in v5:
time: 220 us
  waiting for transfers between devices  126 us (57%)
  matrix products  26.2 us (12%)
  blocking collectives  23 us (10%)
  local copies, waits for them, and re-layouts  15.6 us (7%)
  other arithmetic  14.2 us (6%)
  between operations  14 us (6%)
    all_gather x1, waiting for transfers between devices, shards_body(): gathered_all = lax.all_gather(kv_flat, 'tok', axis=0, tiled=True)  78.7 us
    all_gather x1, waiting for transfers between devices, shards_body(): gathered = lax.all_gather(block_input_rows, 'row', axis=0, tiled=True)  23.3 us
    all_to_all x1, blocking collectives, shards_body(): lax.all_to_all(outgoing, 'tok', split_axis=0, concat_axis=0, tiled=True)  20.5 us
    reduce_scatter x1, waiting for transfers between devices, shards_body(): lax.psum_scatter(main + adapter_down_output, 'col', scatter_dimension=0,...  14.1 us
    unnamed x16, local copies, waits for them, and re-layouts  11.1 us
    reduce_scatter x1, waiting for transfers between devices, shards_body(): lax.psum_scatter(jnp.dot(attended, output_projection_weight, preferred_el...  9.73 us
    reduce_sum x2, other arithmetic, attend_head(): total = jnp.sum(weights.astype(jnp.float32), axis=1)  8.6 us
    dot_general x2, matrix products, attend_head(): score = jnp.dot(query, keys.T, preferred_element_type=jnp.float32) * scale  7.96 us
  transfers between devices with their start and end apart: 4, of which 4 were waited for; matrix products, arithmetic and copies ran while one was open for 7% of the time, Pallas kernels for 0%

profile of v5, /device:TPU:0, one launch (start us, length us, event | category | flops | bytes accessed | tf_op | source)
XLA Modules:
  0.0 219.5 jit_solution(8671841335216989313)
XLA Ops:
  7.2 0.0 copy-start
  7.2 0.0 all-gather.3.cloned.1.call-start
  7.2 0.7 all-gather.3.cloned.1.call-update
  7.9 0.0 reduce-scatter.3.cloned.1.call-start
  8.0 0.7 convert_element_type.43
  8.7 0.0 copy-start.3
  8.7 10.7 %copy.10 = bf16[2048,4,3,128]{0,3,2,1:T(8,128)(2,1)} copy(bf16[2048,4,3,128]{3,1,2,0:T(4,128)(2,1)} %param.10) | data formatting | bytes 12582912 | tf_op args[2]
  19.4 0.0 copy-done.3
  19.4 0.3 copy.12
  19.7 23.3 %all-gather.3.cloned.1.call-done = bf16[512,2048]{1,0:T(8,128)(2,1)} async-done(((bf16[128,2048]{1,0:T(8,128)(2,1)}), bf16[512,2048]{1,0:T(8,128)(2,1)}) %all-gather.3.cloned.1.call-update) | async-done | bytes 2097168 | tf_op jit(solution)/shard_map/all_gather | solution.py:36
  43.0 2.1 fusion.1
  45.0 2.5 %psum.7 = f32[512]{0:T(512)S(1)} all-reduce(f32[512]{0:T(512)S(1)} %fusion.1), channel_id=1, replica_groups=mesh['tok'=16,'row'=4,'col'=2] {'col'}, use_global_device_ids=true, to_apply=%region_1.0 | all-reduce | flops 512 | bytes 4096 | tf_op jit(solution)/shard_map/psum | solution.py:39
  47.5 0.0 copy-start.1
  47.5 0.0 copy-start.6
  47.5 6.4 %fusion.4 = f32[512,4,384]{2,0,1:T(8,128)S(1)} fusion(bf16[2048,4,384]{0,2,1:T(8,128)(2,1)} %bitcast.63, bf16[512,2048]{1,0:T(8,128)(2,1)} %all-gather.3.cloned.1.call-done, f32[2048]{0:T(1024)S(1)} %convert_element_type.43, f32[512]{0:T(512)S(1)} %add_rsqrt_fusion), kind=kOutput, calls=%fused_computation.15 | convolution fusion | flops 3225419776 | bytes 11544576 | tf_op jit(solution)/shard_map/td,dhe->hte/dot_general | solution.py:54
  53.9 0.0 copy-done.1
  53.9 0.0 copy-done.6
  53.9 0.8 convolution_bitcast_fusion
  54.7 3.2 %add_bitcast_fusion = f32[4,512,384]{2,1,0:T(8,128)} fusion(f32[512,4,384]{2,0,1:T(8,128)S(1)} %fusion.4, f32[512,128,1]{1,0,2:T(8,128)S(1)} %convolution_bitcast_fusion, bf16[128,4,384]{0,2,1:T(8,128)(2,1)S(1)} %bitcast.70), kind=kOutput, calls=%fused_computation.13 | convolution fusion | flops 1208745984 | bytes 6946816 | tf_op jit(solution)/shard_map/tr,rhe->hte/dot_general | solution.py:57
  57.9 0.0 copy-start.5
  57.9 0.0 reduce-scatter.3.cloned.1.call-update
  57.9 0.0 all-gather.5.cloned.1.call-start
  58.0 14.1 %reduce-scatter.3.cloned.1.call-done = f32[2,512,384]{2,1,0:T(8,128)} async-done(((f32[4,512,384]{2,1,0:T(8,128)}), f32[2,512,384]{2,1,0:T(8,128)}) %reduce-scatter.3.cloned.1.call-update) | async-done | bytes 1572880 | tf_op jit(solution)/shard_map/reduce_scatter | solution.py:63
  72.0 1.5 convert_element_type.45
  73.5 0.3 copy.14
  73.8 0.8 slice.49
  74.6 0.0 all-gather.5.cloned.1.call-update
  74.7 0.0 reduce-scatter.5.cloned.1.call-start
  74.7 0.0 copy-done.5
  74.7 0.1 dynamic_slice.10
  74.8 0.1 dynamic_slice.9
  74.9 78.7 %all-gather.5.cloned.1.call-done = bf16[8192,512]{0,1:T(8,128)(2,1)} async-done(((bf16[512,512]{0,1:T(8,128)(2,1)}), bf16[8192,512]{0,1:T(8,128)(2,1)}) %all-gather.5.cloned.1.call-update) | async-done | bytes 8388624 | tf_op jit(solution)/shard_map/all_gather | solution.py:91
  153.6 4.6 %select_reduce_fusion.1 = (f32[512]{0:T(512)S(1)}, f32[512,5120]{1,0:T(8,128)S(1)}) fusion(s32[512]{0:T(512)S(1)} %iota_add_fusion, s32[5120]{0:T(1024)S(1)} %dynamic_slice.10, s32[512]{0:T(512)S(1)} %dynamic_slice.9, bf16[8192,512]{0,1:T(8,128)(2,1)} %all-gather.5.cloned.1.call-done, s32[]{:T(128)S(6)} %select_n.21, bf16[2,512,3,128]{1,3,2,0:T(8,128)(2,1)S(1)} %bitcast.65), kind=kOutput, calls=%fused_computation.5 | convolution fusion | flops 686816768 | bytes 11954180 | tf_op jit(solution)/shard_map/dot_general | solution.py:17
  158.2 4.4 %convert_reduce_fusion.1 = (f32[512]{0:T(512)S(1)}, bf16[512,5120]{1,0:T(8,128)(2,1)S(1)}) fusion(f32[512]{0:T(512)S(1)} %get-tuple-element.10, f32[512,5120]{1,0:T(8,128)S(1)} %get-tuple-element.11, s32[512]{0:T(512)S(1)} %iota_add_fusion, s32[5120]{0:T(1024)S(1)} %dynamic_slice.10, s32[512]{0:T(512)S(1)} %dynamic_slice.9), kind=kLoop, calls=%fused_computation.3 | loop fusion | flops 23592448 | bytes 15757312 | tf_op jit(solution)/shard_map/reduce_sum | solution.py:21
  162.6 1.9 dynamic-slice.2
  164.5 3.2 %fusion.8 = f32[512,128]{0,1:T(8,128)S(1)} fusion(bf16[512,5120]{1,0:T(8,128)(2,1)S(1)} %get-tuple-element.9, bf16[8192,512]{0,1:T(8,128)(2,1)} %all-gather.5.cloned.1.call-done, s32[]{:T(128)S(6)} %select_n.21, s32[]{:T(128)S(6)} %add.55), kind=kOutput, calls=%fused_computation.20 | convolution fusion | flops 671088640 | bytes 6815752 | tf_op jit(solution)/shard_map/dot_general | solution.py:22
  167.7 3.3 %select_reduce_fusion = (f32[512]{0:T(512)S(1)}, f32[512,5120]{1,0:T(8,128)S(1)}) fusion(s32[512]{0:T(512)S(1)} %iota_add_fusion, s32[5120]{0:T(1024)S(1)} %dynamic_slice.10, s32[512]{0:T(512)S(1)} %dynamic_slice.9, bf16[5120,256]{0,1:T(8,128)(2,1)S(1)} %dynamic-slice.2, bf16[2,512,3,128]{1,3,2,0:T(8,128)(2,1)S(1)} %bitcast.66), kind=kOutput, calls=%fused_computation.2 | convolution fusion | flops 686816768 | bytes 11954176 | tf_op jit(solution)/shard_map/dot_general | solution.py:17
  171.0 4.2 %convert_reduce_fusion = (f32[512]{0:T(512)S(1)}, bf16[512,5120]{1,0:T(8,128)(2,1)S(1)}) fusion(f32[512]{0:T(512)S(1)} %get-tuple-element.12, f32[512,5120]{1,0:T(8,128)S(1)} %get-tuple-element.13, s32[512]{0:T(512)S(1)} %iota_add_fusion, s32[5120]{0:T(1024)S(1)} %dynamic_slice.10, s32[512]{0:T(512)S(1)} %dynamic_slice.9), kind=kLoop, calls=%fused_computation | loop fusion | flops 23592448 | bytes 15757312 | tf_op jit(solution)/shard_map/reduce_sum | solution.py:21
  175.3 1.9 fusion.12
  177.1 0.0 copy-start.4
  177.1 0.0 copy-start.2
  177.2 0.1 fusion.19
  177.2 0.0 copy-done
  177.3 2.1 convolution_convert_fusion
  179.4 0.0 reduce-scatter.5.cloned.1.call-update
  179.4 0.0 copy-done.4
  179.4 1.2 reduce-window.6
  180.6 0.2 slice_reduce_fusion
  180.8 0.1 fusion.22
  180.9 0.0 copy-done.2
  180.9 0.8 fusion.7
  181.7 20.5 %all_to_all.5 = bf16[16,64,512]{2,1,0:T(8,128)(2,1)S(1)} all-to-all(bf16[16,64,512]{2,1,0:T(8,128)(2,1)S(1)} %bitcast.72), channel_id=1, replica_groups=mesh['tok'=16,'row'=4,'col'=2] {'tok'}, dimensions={0} | all-to-all | bytes 2097152 | tf_op jit(solution)/shard_map/all_to_all | solution.py:112
  202.2 1.1 reshape.71
  203.3 9.7 %reduce-scatter.5.cloned.1.call-done = bf16[64,2048]{1,0:T(8,128)(2,1)} async-done(((bf16[512,2048]{1,0:T(8,128)(2,1)}), bf16[64,2048]{1,0:T(8,128)(2,1)}) %reduce-scatter.5.cloned.1.call-update) | async-done | bytes 262160 | tf_op jit(solution)/shard_map/reduce_scatter | solution.py:115
  (7 shorter events, 0.1 us)
Async XLA Ops:
  7.2 170.1 %copy-start = (bf16[256,2048]{1,0:T(8,128)(2,1)S(1)}, bf16[256,2048]{1,0:T(8,128)(2,1)}, u32[]{:S(2)}) copy-start(bf16[256,2048]{1,0:T(8,128)(2,1)} %param.13) | copy-start | bytes 3145732
  7.2 35.8 %all-gather.3.cloned.1.call-start = ((), (), s32[]{:S(2)}) async-start(), calls=%async_computation.3 | async-start | bytes 2621440 | tf_op jit(solution)/shard_map/all_gather | solution.py:36
  7.9 64.1 %reduce-scatter.3.cloned.1.call-start = ((), (), s32[]{:S(2)}) async-start(), calls=%async_computation.4 | async-start | bytes 4718592 | tf_op jit(solution)/shard_map/reduce_scatter | solution.py:63
  8.7 10.7 %copy-start.3 = (bf16[128,4,3,128]{3,1,2,0:T(4,128)(2,1)S(1)}, bf16[128,4,3,128]{3,1,2,0:T(4,128)(2,1)}, u32[]{:S(2)}) copy-start(bf16[128,4,3,128]{3,1,2,0:T(4,128)(2,1)} %param.12) | copy-start | bytes 1179652
  47.5 6.4 %copy-start.1 = (bf16[512,2048]{1,0:T(8,128)(2,1)S(1)}, bf16[512,2048]{1,0:T(8,128)(2,1)}, u32[]{:S(2)}) copy-start(bf16[512,2048]{1,0:T(8,128)(2,1)} %all-gather.3.cloned.1.call-done) | copy-start | bytes 6291460
  47.5 6.4 %copy-start.6 = (bf16[2048,128]{1,0:T(8,128)(2,1)S(1)}, bf16[2048,128]{1,0:T(8,128)(2,1)}, u32[]{:S(2)}) copy-start(bf16[2048,128]{1,0:T(8,128)(2,1)} %param.11) | copy-start | bytes 1572868
  57.9 16.8 %copy-start.5 = (s32[8192]{0:T(1024)S(1)}, s32[8192]{0:T(1024)}, u32[]{:S(2)}) copy-start(s32[8192]{0:T(1024)} %param.14) | copy-start | bytes 98308
  57.9 95.6 %all-gather.5.cloned.1.call-start = ((), (), s32[]{:S(2)}) async-start(), calls=%async_computation.5 | async-start | bytes 8912896 | tf_op jit(solution)/shard_map/all_gather | solution.py:91
  74.7 138.3 %reduce-scatter.5.cloned.1.call-start = ((), (), s32[]{:S(2)}) async-start(), calls=%async_computation.6 | async-start | bytes 2359296 | tf_op jit(solution)/shard_map/reduce_scatter | solution.py:115
  177.1 2.2 %copy-start.4 = (s32[512,1]{0,1:T(1,128)S(1)}, s32[512,1]{0,1:T(1,128)}, u32[]{:S(2)}) copy-start(s32[512,1]{0,1:T(1,128)} %param.15) | copy-start | bytes 6148
  177.1 3.8 %copy-start.2 = (bf16[2,512,2,128]{1,3,2,0:T(8,128)(2,1)S(1)}, bf16[2,512,2,128]{1,3,2,0:T(8,128)(2,1)}, u32[]{:S(2)}) copy-start(bf16[2,512,2,128]{1,3,2,0:T(8,128)(2,1)} %slice.49) | copy-start | bytes 1572868
Sparse Core Ops, SparseCore 0:
  9.6 33.2 all-gather.2
  58.0 13.9 reduce-scatter.2
  74.8 78.7 all-gather.4
  179.5 33.4 reduce-scatter.4

commit v6 on v5

--- a/solution.py
+++ b/solution.py
@@ -1,6 +1,10 @@
+import functools
+
 import jax
 import jax.numpy as jnp
 from jax import lax
+from jax.experimental import pallas as pl
+from jax.experimental.pallas import tpu as pltpu
 from jax.sharding import PartitionSpec as P
 
 
@@ -9,18 +13,47 @@
 ADAPTER_RANK = 128
 MAXLEN = 4352
 
-def attend_head(query, keys, values, own_seg, own_start, key_seg, scale):
-    count = keys.shape[0]
-    key_pos = jnp.arange(count, dtype=jnp.int32)
-    query_pos = own_start + jnp.arange(query.shape[0], dtype=jnp.int32)
-    allowed = (own_seg[:, None] == key_seg[None, :]) & (key_pos[None, :] <= query_pos[:, None])
-    score = jnp.dot(query, keys.T, preferred_element_type=jnp.float32) * scale
+def attend_kernel(offset_ref, q_ref, k_ref, v_ref, qseg_ref, kseg_ref, o_ref, *, scale, rows):
+    tile = pl.program_id(1)
+    q = q_ref[0]
+    k = k_ref[...]
+    v = v_ref[...]
+    count = k.shape[0]
+    score = lax.dot_general(q, k, (((1,), (1,)), ((), ())), preferred_element_type=jnp.float32) * scale
+    key_pos = lax.broadcasted_iota(jnp.int32, (rows, count), 1)
+    query_pos = offset_ref[0] + tile * rows + lax.broadcasted_iota(jnp.int32, (rows, count), 0)
+    allowed = (qseg_ref[...] == kseg_ref[...]) & (key_pos <= query_pos)
     masked = jnp.where(allowed, score, -1e30)
-    top = jnp.max(masked, axis=1)
-    weights = jnp.where(allowed, jnp.exp(score - top[:, None]), 0.0).astype(jnp.bfloat16)
-    total = jnp.sum(weights.astype(jnp.float32), axis=1)
-    summed = jnp.dot(weights, values, preferred_element_type=jnp.float32)
-    return total, summed
+    top = jnp.max(masked, axis=1, keepdims=True)
+    weights = jnp.where(allowed, jnp.exp(score - top), 0.0).astype(jnp.bfloat16)
+    total = jnp.sum(weights.astype(jnp.float32), axis=1, keepdims=True)
+    summed = jnp.dot(weights, v, preferred_element_type=jnp.float32)
+    o_ref[0] = (summed / total).astype(o_ref.dtype)
+
+def attend(query, window_kv, own_seg, key_seg, offset, scale, rows=128):
+    heads, tokens, _ = query.shape
+    count = window_kv.shape[0]
+    grid = (heads, tokens // rows)
+    kernel = functools.partial(attend_kernel, scale=scale, rows=rows)
+    flops = 4 * heads * tokens * count * HEAD_SIZE
+    return pl.pallas_call(
+        kernel,
+        out_shape=jax.ShapeDtypeStruct((heads, tokens, HEAD_SIZE), jnp.bfloat16),
+        grid_spec=pltpu.PrefetchScalarGridSpec(
+            num_scalar_prefetch=1,
+            grid=grid,
+            in_specs=[
+                pl.BlockSpec((1, rows, HEAD_SIZE), lambda h, i, off: (h, i, 0)),
+                pl.BlockSpec((count, HEAD_SIZE), lambda h, i, off: (0, 2 * h)),
+                pl.BlockSpec((count, HEAD_SIZE), lambda h, i, off: (0, 2 * h + 1)),
+                pl.BlockSpec((rows, 1), lambda h, i, off: (i, 0)),
+                pl.BlockSpec((1, count), lambda h, i, off: (0, 0)),
+            ],
+            out_specs=pl.BlockSpec((1, rows, HEAD_SIZE), lambda h, i, off: (h, i, 0)),
+        ),
+        compiler_params=pltpu.CompilerParams(dimension_semantics=("arbitrary", "arbitrary"), vmem_limit_bytes=48 * 1024 * 1024),
+        cost_estimate=pl.CostEstimate(flops=flops, transcendentals=heads * tokens * count, bytes_accessed=2 * count * 512 + 4 * heads * tokens * HEAD_SIZE),
+    )(offset.reshape(1).astype(jnp.int32), query, window_kv, window_kv, own_seg.reshape(tokens, 1), key_seg.reshape(1, count))
 
 
 def shards_body(
@@ -90,27 +123,9 @@
     ).astype(jnp.bfloat16).reshape(count_tok, capacity, heads_dev * 2 * HEAD_SIZE)
     gathered_all = lax.all_gather(kv_flat, "tok", axis=0, tiled=True)
     window_kv = lax.dynamic_slice_in_dim(gathered_all, first, window, 0)
-    states = []
-    for head in range(heads_dev):
-        head_kv = window_kv[:, head * 2 * HEAD_SIZE : (head + 1) * 2 * HEAD_SIZE]
-        if head > 0:
-            head_kv, _ = lax.optimization_barrier((head_kv, states[-1]))
-        states.append(
-            attend_head(
-                query[head],
-                head_kv[:, :HEAD_SIZE],
-                head_kv[:, HEAD_SIZE:],
-                own_seg,
-                own_start - first,
-                key_seg,
-                scale,
-            )
-        )
-    total = jnp.stack([part[0] for part in states])
-    summed = jnp.stack([part[1] for part in states])
-    outgoing, _ = lax.optimization_barrier((outgoing, states[-1]))
+    attended = attend(query, window_kv, own_seg, key_seg, own_start - first, scale)
+    outgoing, _ = lax.optimization_barrier((outgoing, attended))
     received = lax.all_to_all(outgoing, "tok", split_axis=0, concat_axis=0, tiled=True)
-    attended = (summed / total[:, :, None]).astype(jnp.bfloat16)
     attended = jnp.transpose(attended, (1, 0, 2)).reshape(tok_dev, heads_dev * HEAD_SIZE)
     block_output = lax.psum_scatter(
         jnp.dot(attended, output_projection_weight, preferred_element_type=jnp.float32).astype(

time: 220 us -> 211 us (0.959)
  Pallas kernels: 0 us -> 17.9 us
  matrix products: 26.2 us -> 13.2 us
  other arithmetic: 14.2 us -> 4.88 us
  waiting for transfers between devices: 126 us -> 119 us
    pallas_call x0 -> x1, Pallas kernels: none -> 17.9 us  [attend(): pl.pallas_call(kernel, out_shape=jax.ShapeDtypeStruct((heads, tokens, HEA...]
    dot_general x4 -> x0, matrix products: 13 us -> none  [the longest x2 7.96 us: attend_head(): score = jnp.dot(query, keys.T, preferred_element_type=jnp.float32) * scale]
    reduce_sum x2 -> x0, other arithmetic: 8.6 us -> none  [attend_head(): total = jnp.sum(weights.astype(jnp.float32), axis=1)]
    all_gather x1, waiting for transfers between devices: 78.7 us -> 71.9 us  [shards_body(): gathered_all = lax.all_gather(kv_flat, 'tok', axis=0, tiled=True)]
    dynamic_slice x0 -> x1, local copies, waits for them, and re-layouts: none -> 2.82 us  [shards_body(): window_kv = lax.dynamic_slice_in_dim(gathered_all, first, window, 0)]
    unnamed x16 -> x17, local copies, waits for them, and re-layouts: 11.1 us -> 11.2 us
where the time goes in v6:
time: 211 us
  waiting for transfers between devices  119 us (56%)
  blocking collectives  24.2 us (11%)
  Pallas kernels  17.9 us (8%)
  local copies, waits for them, and re-layouts  17.2 us (8%)
  between operations  14 us (7%)
  matrix products  13.2 us (6%)
  other arithmetic  4.88 us (2%)
    all_gather x1, waiting for transfers between devices, shards_body(): gathered_all = lax.all_gather(kv_flat, 'tok', axis=0, tiled=True)  71.9 us
    all_gather x1, waiting for transfers between devices, shards_body(): gathered = lax.all_gather(block_input_rows, 'row', axis=0, tiled=True)  23.9 us
    all_to_all x1, blocking collectives, shards_body(): lax.all_to_all(outgoing, 'tok', split_axis=0, concat_axis=0, tiled=True)  21.7 us
    pallas_call x1, Pallas kernels, attend(): pl.pallas_call(kernel, out_shape=jax.ShapeDtypeStruct((heads, tokens, HEA...  17.9 us
    reduce_scatter x1, waiting for transfers between devices, shards_body(): lax.psum_scatter(main + adapter_down_output, 'col', scatter_dimension=0,...  14.1 us
    unnamed x17, local copies, waits for them, and re-layouts  11.2 us
    reduce_scatter x1, waiting for transfers between devices, shards_body(): lax.psum_scatter(jnp.dot(attended, output_projection_weight, preferred_el...  8.84 us
    dot_general x1, matrix products, shards_body(): jnp.einsum('td,dhe->hte', normalized_input, flat_weight, preferred_elemen...  6.4 us
  transfers between devices with their start and end apart: 4, of which 4 were waited for; matrix products, arithmetic and copies ran while one was open for 7% of the time, Pallas kernels for 0%

profile of v6, /device:TPU:0, one launch (start us, length us, event | category | flops | bytes accessed | tf_op | source)
XLA Modules:
  0.0 210.9 jit_solution(12089385810732040360)
XLA Ops:
  7.2 0.0 copy-start
  7.2 0.0 all-gather.3.cloned.1.call-start
  7.2 0.7 all-gather.3.cloned.1.call-update
  7.9 0.0 copy-start.5
  7.9 0.0 copy-start.2
  7.9 0.0 reduce-scatter.3.cloned.1.call-start
  8.0 10.7 %copy.11 = bf16[2048,4,3,128]{0,3,2,1:T(8,128)(2,1)} copy(bf16[2048,4,3,128]{3,1,2,0:T(4,128)(2,1)} %param.10) | data formatting | bytes 12582912 | tf_op args[2]
  18.7 0.0 copy-done.5
  18.7 0.0 copy-done.2
  18.7 0.3 copy.13
  19.0 23.9 %all-gather.3.cloned.1.call-done = bf16[512,2048]{1,0:T(8,128)(2,1)} async-done(((bf16[128,2048]{1,0:T(8,128)(2,1)}), bf16[512,2048]{1,0:T(8,128)(2,1)}) %all-gather.3.cloned.1.call-update) | async-done | bytes 2097168 | tf_op jit(solution)/shard_map/all_gather | solution.py:69
  43.0 2.1 fusion
  45.0 2.5 %psum.7 = f32[512]{0:T(512)S(1)} all-reduce(f32[512]{0:T(512)S(1)} %fusion), channel_id=1, replica_groups=mesh['tok'=16,'row'=4,'col'=2] {'col'}, use_global_device_ids=true, to_apply=%region_1.0 | all-reduce | flops 512 | bytes 4096 | tf_op jit(solution)/shard_map/psum | solution.py:72
  47.5 0.0 copy-start.1
  47.5 0.0 copy-start.6
  47.5 6.4 %fusion.3 = f32[512,4,384]{2,0,1:T(8,128)S(1)} fusion(bf16[2048,4,384]{0,2,1:T(8,128)(2,1)} %bitcast.51, bf16[512,2048]{1,0:T(8,128)(2,1)} %all-gather.3.cloned.1.call-done, f32[2048]{0:T(1024)S(1)} %convert_element_type.28, f32[512]{0:T(512)S(1)} %add_rsqrt_fusion), kind=kOutput, calls=%fused_computation.7 | convolution fusion | flops 3225419776 | bytes 11544576 | tf_op jit(solution)/shard_map/td,dhe->hte/dot_general | solution.py:87
  53.9 0.0 copy-done.1
  53.9 0.0 copy-done.6
  53.9 0.8 convolution_bitcast_fusion
  54.7 3.2 %add_bitcast_fusion = f32[4,512,384]{2,1,0:T(8,128)} fusion(f32[512,4,384]{2,0,1:T(8,128)S(1)} %fusion.3, f32[512,128,1]{1,0,2:T(8,128)S(1)} %convolution_bitcast_fusion, bf16[128,4,384]{0,2,1:T(8,128)(2,1)S(1)} %bitcast.57), kind=kOutput, calls=%fused_computation.5 | convolution fusion | flops 1208745984 | bytes 6946816 | tf_op jit(solution)/shard_map/tr,rhe->hte/dot_general | solution.py:90
  57.9 0.0 copy-start.4
  57.9 0.0 reduce-scatter.3.cloned.1.call-update
  57.9 0.0 all-gather.5.cloned.1.call-start
  58.0 14.1 %reduce-scatter.3.cloned.1.call-done = f32[2,512,384]{2,1,0:T(8,128)} async-done(((f32[4,512,384]{2,1,0:T(8,128)}), f32[2,512,384]{2,1,0:T(8,128)}) %reduce-scatter.3.cloned.1.call-update) | async-done | bytes 1572880 | tf_op jit(solution)/shard_map/reduce_scatter | solution.py:96
  72.0 1.5 convert_element_type.30
  73.5 0.3 copy.15
  73.9 1.0 copy.23
  74.9 0.0 all-gather.5.cloned.1.call-update
  74.9 0.0 reduce-scatter.5.cloned.1.call-start
  74.9 0.0 copy-done.4
  75.0 0.1 dynamic_slice.10
  75.0 0.1 copy.18.qseg_ref
  75.2 0.1 dynamic_slice.11
  75.3 0.2 copy.24
  75.5 71.9 %all-gather.5.cloned.1.call-done = bf16[8192,512]{1,0:T(8,128)(2,1)} async-done(((bf16[512,512]{1,0:T(8,128)(2,1)}), bf16[8192,512]{1,0:T(8,128)(2,1)}) %all-gather.5.cloned.1.call-update) | async-done | bytes 8388624 | tf_op jit(solution)/shard_map/all_gather | solution.py:124
  147.4 2.8 %constant_dynamic-slice_fusion.k_ref.v_ref = bf16[5120,512]{1,0:T(8,128)(2,1)S(1)} fusion(bf16[8192,512]{1,0:T(8,128)(2,1)} %all-gather.5.cloned.1.call-done, s32[]{:T(128)S(6)} %select_n.7), kind=kLoop, calls=%fused_computation.25 | loop fusion | bytes 10485764 | tf_op jit(solution)/shard_map/dynamic_slice | solution.py:125
  150.2 17.9 %shard_map.95 = bf16[2,512,128]{2,1,0:T(8,128)(2,1)S(1)} custom-call(s32[1]{0:T(128)} %bitcast.offset_ref, bf16[2,512,128]{2,1,0:T(8,128)(2,1)S(1)} %bitcast.48, bf16[5120,512]{1,0:T(8,128)(2,1)S(1)} %constant_dynamic-slice_fusion.k_ref.v_ref, bf16[5120,512]{1,0:T(8,128)(2,1)S(1)} %constant_dynamic-slice_fusion.k_ref.v_ref, s32[512,1]{1,0:T(8,128)S(1)} %copy.18.qseg_ref, ...), custom_call_target="tpu_custom_call" | custom-call | flops 2684354560 | bytes 5767168 | tf_op jit(solution)/shard_map/pallas_call | solution.py:39
  168.1 0.0 copy-start.3
  168.1 0.1 copy.19
  168.2 0.0 copy-done
  168.3 2.1 convolution_convert_fusion
  170.3 0.0 reduce-scatter.5.cloned.1.call-update
  170.4 0.0 copy-done.3
  170.4 1.2 reduce-window.6
  171.5 0.2 slice_reduce_fusion
  171.8 0.1 fusion.12
  171.9 0.7 fusion.6
  172.7 21.7 %all_to_all.5 = bf16[16,64,512]{2,1,0:T(8,128)(2,1)S(1)} all-to-all(bf16[16,64,512]{2,1,0:T(8,128)(2,1)S(1)} %bitcast.58), channel_id=1, replica_groups=mesh['tok'=16,'row'=4,'col'=2] {'tok'}, dimensions={0} | all-to-all | bytes 2097152 | tf_op jit(solution)/shard_map/all_to_all | solution.py:128
  194.4 1.1 reshape.70
  195.5 8.8 %reduce-scatter.5.cloned.1.call-done = bf16[64,2048]{1,0:T(8,128)(2,1)} async-done(((bf16[512,2048]{1,0:T(8,128)(2,1)}), bf16[64,2048]{1,0:T(8,128)(2,1)}) %reduce-scatter.5.cloned.1.call-update) | async-done | bytes 262160 | tf_op jit(solution)/shard_map/reduce_scatter | solution.py:130
  (8 shorter events, 0.1 us)
Async XLA Ops:
  7.2 161.1 %copy-start = (bf16[256,2048]{1,0:T(8,128)(2,1)S(1)}, bf16[256,2048]{1,0:T(8,128)(2,1)}, u32[]{:S(2)}) copy-start(bf16[256,2048]{1,0:T(8,128)(2,1)} %param.13) | copy-start | bytes 3145732
  7.2 35.8 %all-gather.3.cloned.1.call-start = ((), (), s32[]{:S(2)}) async-start(), calls=%async_computation.3 | async-start | bytes 2621440 | tf_op jit(solution)/shard_map/all_gather | solution.py:69
  7.9 10.8 %copy-start.5 = (bf16[2048]{0:T(1024)(128)(2,1)S(1)}, bf16[2048]{0:T(1024)(128)(2,1)}, u32[]{:S(2)}) copy-start(bf16[2048]{0:T(1024)(128)(2,1)} %param.9) | copy-start | bytes 12292
  7.9 10.8 %copy-start.2 = (bf16[128,4,3,128]{3,1,2,0:T(4,128)(2,1)S(1)}, bf16[128,4,3,128]{3,1,2,0:T(4,128)(2,1)}, u32[]{:S(2)}) copy-start(bf16[128,4,3,128]{3,1,2,0:T(4,128)(2,1)} %param.12) | copy-start | bytes 1179652
  7.9 64.1 %reduce-scatter.3.cloned.1.call-start = ((), (), s32[]{:S(2)}) async-start(), calls=%async_computation.4 | async-start | bytes 4718592 | tf_op jit(solution)/shard_map/reduce_scatter | solution.py:96
  47.5 6.4 %copy-start.1 = (bf16[512,2048]{1,0:T(8,128)(2,1)S(1)}, bf16[512,2048]{1,0:T(8,128)(2,1)}, u32[]{:S(2)}) copy-start(bf16[512,2048]{1,0:T(8,128)(2,1)} %all-gather.3.cloned.1.call-done) | copy-start | bytes 6291460
  47.5 6.4 %copy-start.6 = (bf16[2048,128]{1,0:T(8,128)(2,1)S(1)}, bf16[2048,128]{1,0:T(8,128)(2,1)}, u32[]{:S(2)}) copy-start(bf16[2048,128]{1,0:T(8,128)(2,1)} %param.11) | copy-start | bytes 1572868
  57.9 17.1 %copy-start.4 = (s32[8192]{0:T(1024)S(1)}, s32[8192]{0:T(1024)}, u32[]{:S(2)}) copy-start(s32[8192]{0:T(1024)} %param.14) | copy-start | bytes 98308
  57.9 89.4 %all-gather.5.cloned.1.call-start = ((), (), s32[]{:S(2)}) async-start(), calls=%async_computation.5 | async-start | bytes 8912896 | tf_op jit(solution)/shard_map/all_gather | solution.py:124
  74.9 129.5 %reduce-scatter.5.cloned.1.call-start = ((), (), s32[]{:S(2)}) async-start(), calls=%async_computation.6 | async-start | bytes 2359296 | tf_op jit(solution)/shard_map/reduce_scatter | solution.py:130
  168.1 2.3 %copy-start.3 = (s32[512,1]{0,1:T(1,128)S(1)}, s32[512,1]{0,1:T(1,128)}, u32[]{:S(2)}) copy-start(s32[512,1]{0,1:T(1,128)} %param.15) | copy-start | bytes 6148
Sparse Core Ops, SparseCore 0:
  9.7 33.2 all-gather.2
  58.0 13.9 reduce-scatter.2
  75.0 72.2 all-gather.4
  170.5 33.8 reduce-scatter.4

commit v7 on v6

--- a/solution.py
+++ b/solution.py
@@ -12,48 +12,84 @@
 HEAD_SIZE = 128
 ADAPTER_RANK = 128
 MAXLEN = 4352
+CHUNK = 512
 
-def attend_kernel(offset_ref, q_ref, k_ref, v_ref, qseg_ref, kseg_ref, o_ref, *, scale, rows):
+
+def attend_kernel(off_ref, lo_ref, q_ref, k_ref, v_ref, low_ref, o_ref, *, scale, rows):
     tile = pl.program_id(1)
     q = q_ref[0]
-    k = k_ref[...]
-    v = v_ref[...]
-    count = k.shape[0]
-    score = lax.dot_general(q, k, (((1,), (1,)), ((), ())), preferred_element_type=jnp.float32) * scale
-    key_pos = lax.broadcasted_iota(jnp.int32, (rows, count), 1)
-    query_pos = offset_ref[0] + tile * rows + lax.broadcasted_iota(jnp.int32, (rows, count), 0)
-    allowed = (qseg_ref[...] == kseg_ref[...]) & (key_pos <= query_pos)
-    masked = jnp.where(allowed, score, -1e30)
-    top = jnp.max(masked, axis=1, keepdims=True)
-    weights = jnp.where(allowed, jnp.exp(score - top), 0.0).astype(jnp.bfloat16)
-    total = jnp.sum(weights.astype(jnp.float32), axis=1, keepdims=True)
-    summed = jnp.dot(weights, v, preferred_element_type=jnp.float32)
+    base = off_ref[0] + tile * rows
+    query_pos = base + lax.broadcasted_iota(jnp.int32, (rows, 1), 0)
+    low = low_ref[...]
+    last_chunk = (base + rows - 1) // CHUNK
+    first_chunk = jnp.clip(lo_ref[tile] // CHUNK, 0, last_chunk)
+
+    def scores(chunk):
+        start = pl.multiple_of(chunk * CHUNK, CHUNK)
+        keys = k_ref[pl.ds(start, CHUNK), :]
+        score = lax.dot_general(
+            q, keys, (((1,), (1,)), ((), ())), preferred_element_type=jnp.float32
+        ) * scale
+        key_pos = start + lax.broadcasted_iota(jnp.int32, (rows, CHUNK), 1)
+        allowed = (key_pos >= low) & (key_pos <= query_pos)
+        return jnp.where(allowed, score, -1e30), start
+
+    def top_step(chunk, top):
+        masked, _ = scores(chunk)
+        return jnp.maximum(top, jnp.max(masked, axis=1, keepdims=True))
+
+    top = lax.fori_loop(
+        first_chunk, last_chunk + 1, top_step, jnp.full((rows, 1), -1e30, jnp.float32)
+    )
+
+    def sum_step(chunk, carry):
+        total, summed = carry
+        masked, start = scores(chunk)
+        weights = jnp.exp(masked - top).astype(jnp.bfloat16)
+        total = total + jnp.sum(weights.astype(jnp.float32), axis=1, keepdims=True)
+        values = v_ref[pl.ds(start, CHUNK), :]
+        summed = summed + jnp.dot(weights, values, preferred_element_type=jnp.float32)
+        return total, summed
+
+    total, summed = lax.fori_loop(
+        first_chunk,
+        last_chunk + 1,
+        sum_step,
+        (jnp.zeros((rows, 1), jnp.float32), jnp.zeros((rows, HEAD_SIZE), jnp.float32)),
+    )
     o_ref[0] = (summed / total).astype(o_ref.dtype)
 
-def attend(query, window_kv, own_seg, key_seg, offset, scale, rows=128):
+
+def attend(query, window_kv, low, offset, scale, rows=128):
     heads, tokens, _ = query.shape
     count = window_kv.shape[0]
-    grid = (heads, tokens // rows)
+    tiles = tokens // rows
     kernel = functools.partial(attend_kernel, scale=scale, rows=rows)
-    flops = 4 * heads * tokens * count * HEAD_SIZE
+    flops = 6 * heads * tokens * count * HEAD_SIZE
+    tile_low = low.reshape(tiles, rows)[:, 0]
     return pl.pallas_call(
         kernel,
         out_shape=jax.ShapeDtypeStruct((heads, tokens, HEAD_SIZE), jnp.bfloat16),
         grid_spec=pltpu.PrefetchScalarGridSpec(
-            num_scalar_prefetch=1,
-            grid=grid,
+            num_scalar_prefetch=2,
+            grid=(heads, tiles),
             in_specs=[
-                pl.BlockSpec((1, rows, HEAD_SIZE), lambda h, i, off: (h, i, 0)),
-                pl.BlockSpec((count, HEAD_SIZE), lambda h, i, off: (0, 2 * h)),
-                pl.BlockSpec((count, HEAD_SIZE), lambda h, i, off: (0, 2 * h + 1)),
-                pl.BlockSpec((rows, 1), lambda h, i, off: (i, 0)),
-                pl.BlockSpec((1, count), lambda h, i, off: (0, 0)),
+                pl.BlockSpec((1, rows, HEAD_SIZE), lambda h, i, off, lo: (h, i, 0)),
+                pl.BlockSpec((count, HEAD_SIZE), lambda h, i, off, lo: (0, 2 * h)),
+                pl.BlockSpec((count, HEAD_SIZE), lambda h, i, off, lo: (0, 2 * h + 1)),
+                pl.BlockSpec((rows, 1), lambda h, i, off, lo: (i, 0)),
             ],
-            out_specs=pl.BlockSpec((1, rows, HEAD_SIZE), lambda h, i, off: (h, i, 0)),
+            out_specs=pl.BlockSpec((1, rows, HEAD_SIZE), lambda h, i, off, lo: (h, i, 0)),
         ),
-        compiler_params=pltpu.CompilerParams(dimension_semantics=("arbitrary", "arbitrary"), vmem_limit_bytes=48 * 1024 * 1024),
-        cost_estimate=pl.CostEstimate(flops=flops, transcendentals=heads * tokens * count, bytes_accessed=2 * count * 512 + 4 * heads * tokens * HEAD_SIZE),
-    )(offset.reshape(1).astype(jnp.int32), query, window_kv, window_kv, own_seg.reshape(tokens, 1), key_seg.reshape(1, count))
+        compiler_params=pltpu.CompilerParams(
+            dimension_semantics=("arbitrary", "arbitrary"), vmem_limit_bytes=48 * 1024 * 1024
+        ),
+        cost_estimate=pl.CostEstimate(
+            flops=flops,
+            transcendentals=heads * tokens * count,
+            bytes_accessed=2 * count * 512 + 4 * heads * tokens * HEAD_SIZE,
+        ),
+    )(offset.reshape(1).astype(jnp.int32), tile_low, query, window_kv, window_kv, low.reshape(tokens, 1))
 
 
 def shards_body(
@@ -106,7 +142,6 @@
     back = min(count_tok - 1, -(-(MAXLEN - 1) // tok_dev))
     window = (back + 1) * tok_dev
     first = jnp.clip(me - back, 0, count_tok - 1 - back) * tok_dev
-    key_seg = lax.dynamic_slice_in_dim(prompt_segment_index, first, window, 0)
     capacity = max(2, 2 * tok_dev // count_tok)
     owner = cache_owner_index[:, 0]
     onehot = (owner[:, None] == jnp.arange(count_tok, dtype=jnp.int32)[None, :]).astype(jnp.int32)
@@ -123,7 +158,10 @@
     ).astype(jnp.bfloat16).reshape(count_tok, capacity, heads_dev * 2 * HEAD_SIZE)
     gathered_all = lax.all_gather(kv_flat, "tok", axis=0, tiled=True)
     window_kv = lax.dynamic_slice_in_dim(gathered_all, first, window, 0)
-    attended = attend(query, window_kv, own_seg, key_seg, own_start - first, scale)
+    seg_start = jnp.searchsorted(
+        prompt_segment_index, own_seg, side="left", method="scan_unrolled"
+    ).astype(jnp.int32)
+    attended = attend(query, window_kv, seg_start - first, own_start - first, scale)
     outgoing, _ = lax.optimization_barrier((outgoing, attended))
     received = lax.all_to_all(outgoing, "tok", split_axis=0, concat_axis=0, tiled=True)
     attended = jnp.transpose(attended, (1, 0, 2)).reshape(tok_dev, heads_dev * HEAD_SIZE)
@@ -137,6 +175,7 @@
     )
     kv_cache = received.reshape(count_tok * capacity, heads_dev, 2, HEAD_SIZE)
     return (block_output, kv_cache)
+
 
 def solution(mesh):
     placed = (

time: 211 us -> 236 us (1.12)
  waiting for transfers between devices: 119 us -> 74.4 us
  local copies, waits for them, and re-layouts: 17.2 us -> 61.1 us
  blocking collectives: 24.2 us -> 59.7 us
  Pallas kernels: 17.9 us -> 7.28 us
    all_gather x1, waiting for transfers between devices: 71.9 us -> 27.1 us  [shards_body(): gathered_all = lax.all_gather(kv_flat, 'tok', axis=0, tiled=True)]
    gather x0 -> x14, local copies, waits for them, and re-layouts: none -> 44 us  [shards_body(): jnp.searchsorted(prompt_segment_index, own_seg, side='left', method='scan...]
    all_to_all x1, blocking collectives: 21.7 us -> 57.2 us  [shards_body(): lax.all_to_all(outgoing, 'tok', split_axis=0, concat_axis=0, tiled=True)]
    pallas_call x1, Pallas kernels: 17.9 us -> 7.28 us  [attend(): pl.pallas_call(kernel, out_shape=jax.ShapeDtypeStruct((heads, tokens, HEA...]
  transfers between devices with their start and end apart: 4 -> 4, of which waited for: 4 -> 4; matrix products, arithmetic and copies ran while one was open for 7% -> 25% of each run, Pallas kernels for 0% -> 0%
where the time goes in v7:
time: 236 us; the launch traced here: 235 us
  waiting for transfers between devices  74.4 us (32%)
  local copies, waits for them, and re-layouts  61.1 us (26%)
  blocking collectives  59.7 us (25%)
  between operations  14.2 us (6%)
  matrix products  13.2 us (6%)
  Pallas kernels  7.28 us (3%)
  other arithmetic  5.23 us (2%)
    all_to_all x1, blocking collectives, shards_body(): lax.all_to_all(outgoing, 'tok', split_axis=0, concat_axis=0, tiled=True)  57.2 us
    gather x14, local copies, waits for them, and re-layouts, shards_body(): jnp.searchsorted(prompt_segment_index, own_seg, side='left', method='scan...  44 us
    all_gather x1, waiting for transfers between devices, shards_body(): gathered_all = lax.all_gather(kv_flat, 'tok', axis=0, tiled=True)  27.1 us
    all_gather x1, waiting for transfers between devices, shards_body(): gathered = lax.all_gather(block_input_rows, 'row', axis=0, tiled=True)  24 us
    reduce_scatter x1, waiting for transfers between devices, shards_body(): lax.psum_scatter(main + adapter_down_output, 'col', scatter_dimension=0,...  14.1 us
    unnamed x17, local copies, waits for them, and re-layouts  11.2 us
    reduce_scatter x1, waiting for transfers between devices, shards_body(): lax.psum_scatter(jnp.dot(attended, output_projection_weight, preferred_el...  8.58 us
    pallas_call x1, Pallas kernels, attend(): pl.pallas_call(kernel, out_shape=jax.ShapeDtypeStruct((heads, tokens, HEA...  7.28 us
  transfers between devices with their start and end apart: 4, of which 4 were waited for; matrix products, arithmetic and copies ran while one was open for 25% of the time, Pallas kernels for 0%

profile of v7, /device:TPU:0, one launch (start us, length us, event | category | flops | bytes accessed | tf_op | source)
XLA Modules:
  0.0 235.5 jit_solution(3134954058536645074)
XLA Ops:
  7.2 0.0 copy-start
  7.2 0.0 all-gather.3.cloned.1.call-start
  7.2 0.7 all-gather.3.cloned.1.call-update
  7.9 0.0 copy-start.5
  7.9 0.0 copy-start.3
  7.9 0.0 reduce-scatter.3.cloned.1.call-start
  8.0 10.7 %copy.21 = bf16[2048,4,3,128]{0,3,2,1:T(8,128)(2,1)} copy(bf16[2048,4,3,128]{3,1,2,0:T(4,128)(2,1)} %param.10) | data formatting | bytes 12582912 | tf_op args[2]
  18.7 0.0 copy-done.5
  18.7 0.0 copy-done.3
  18.7 0.3 copy.23
  19.0 24.0 %all-gather.3.cloned.1.call-done = bf16[512,2048]{1,0:T(8,128)(2,1)} async-done(((bf16[128,2048]{1,0:T(8,128)(2,1)}), bf16[512,2048]{1,0:T(8,128)(2,1)}) %all-gather.3.cloned.1.call-update) | async-done | bytes 2097168 | tf_op jit(solution)/shard_map/all_gather | solution.py:105
  43.0 2.1 fusion
  45.0 2.5 %psum.7 = f32[512]{0:T(512)S(1)} all-reduce(f32[512]{0:T(512)S(1)} %fusion), channel_id=1, replica_groups=mesh['tok'=16,'row'=4,'col'=2] {'col'}, use_global_device_ids=true, to_apply=%region_1.0 | all-reduce | flops 512 | bytes 4096 | tf_op jit(solution)/shard_map/psum | solution.py:108
  47.5 0.0 copy-start.2
  47.5 0.0 copy-start.6
  47.5 6.4 %fusion.3 = f32[512,4,384]{2,0,1:T(8,128)S(1)} fusion(bf16[2048,4,384]{0,2,1:T(8,128)(2,1)} %bitcast.50, bf16[512,2048]{1,0:T(8,128)(2,1)} %all-gather.3.cloned.1.call-done, f32[2048]{0:T(1024)S(1)} %convert_element_type.92, f32[512]{0:T(512)S(1)} %add_rsqrt_fusion), kind=kOutput, calls=%fused_computation.21 | convolution fusion | flops 3225419776 | bytes 11544576 | tf_op jit(solution)/shard_map/td,dhe->hte/dot_general | solution.py:123
  53.9 0.0 copy-done.2
  53.9 0.0 copy-done.6
  54.0 0.8 convolution_bitcast_fusion
  54.7 3.2 %add_bitcast_fusion = f32[4,512,384]{2,1,0:T(8,128)} fusion(f32[512,4,384]{2,0,1:T(8,128)S(1)} %fusion.3, f32[512,128,1]{1,0,2:T(8,128)S(1)} %convolution_bitcast_fusion, bf16[128,4,384]{0,2,1:T(8,128)(2,1)S(1)} %bitcast.56), kind=kOutput, calls=%fused_computation.19 | convolution fusion | flops 1208745984 | bytes 6946816 | tf_op jit(solution)/shard_map/tr,rhe->hte/dot_general | solution.py:126
  57.9 0.0 copy-start.1
  57.9 0.0 reduce-scatter.3.cloned.1.call-update
  57.9 0.0 all-gather.5.cloned.1.call-start
  58.0 14.1 %reduce-scatter.3.cloned.1.call-done = f32[2,512,384]{2,1,0:T(8,128)} async-done(((f32[4,512,384]{2,1,0:T(8,128)}), f32[2,512,384]{2,1,0:T(8,128)}) %reduce-scatter.3.cloned.1.call-update) | async-done | bytes 1572880 | tf_op jit(solution)/shard_map/reduce_scatter | solution.py:132
  72.0 1.5 convert_element_type.94
  73.5 0.3 copy.25
  73.9 1.0 copy.33
  74.9 0.0 all-gather.5.cloned.1.call-update
  74.9 0.2 reduce-scatter.5.cloned.1.call-start
  75.2 0.0 copy-done.1
  75.2 3.1 %gather_fusion = s32[512]{0:T(512)S(1)} fusion(s32[8192]{0:T(1024)S(1)} %copy-done.1, u32[1024]{0:T(1024)S(1)} %pad_clamp_fusion.13), kind=kCustom, calls=%fused_computation | custom fusion | bytes 6144 | tf_op jit(solution)/shard_map/jit(searchsorted)/jit(_searchsorted_scan_impl)/vmap(jit(_searchsorted_scan_impl))/eval_jaxpr/gather | solution.py:161
  78.3 0.1 select_add_fusion
  78.4 3.1 %gather_fusion.1 = s32[512]{0:T(512)S(1)} fusion(s32[8192]{0:T(1024)S(1)} %copy-done.1, u32[1024]{0:T(1024)S(1)} %pad_clamp_fusion.12), kind=kCustom, calls=%fused_computation.1 | custom fusion | bytes 6144 | tf_op jit(solution)/shard_map/jit(searchsorted)/jit(_searchsorted_scan_impl)/vmap(jit(_searchsorted_scan_impl))/eval_jaxpr/gather | solution.py:161
  81.6 3.1 %gather_fusion.2 = s32[512]{0:T(512)S(1)} fusion(s32[8192]{0:T(1024)S(1)} %copy-done.1, u32[1024]{0:T(1024)S(1)} %pad_clamp_fusion.11), kind=kCustom, calls=%fused_computation.2 | custom fusion | bytes 6144 | tf_op jit(solution)/shard_map/jit(searchsorted)/jit(_searchsorted_scan_impl)/vmap(jit(_searchsorted_scan_impl))/eval_jaxpr/gather | solution.py:161
  84.8 3.1 %gather_fusion.3 = s32[512]{0:T(512)S(1)} fusion(s32[8192]{0:T(1024)S(1)} %copy-done.1, u32[1024]{0:T(1024)S(1)} %pad_clamp_fusion.10), kind=kCustom, calls=%fused_computation.3 | custom fusion | bytes 6144 | tf_op jit(solution)/shard_map/jit(searchsorted)/jit(_searchsorted_scan_impl)/vmap(jit(_searchsorted_scan_impl))/eval_jaxpr/gather | solution.py:161
  87.9 3.1 %gather_fusion.4 = s32[512]{0:T(512)S(1)} fusion(s32[8192]{0:T(1024)S(1)} %copy-done.1, u32[1024]{0:T(1024)S(1)} %pad_clamp_fusion.9), kind=kCustom, calls=%fused_computation.4 | custom fusion | bytes 6144 | tf_op jit(solution)/shard_map/jit(searchsorted)/jit(_searchsorted_scan_impl)/vmap(jit(_searchsorted_scan_impl))/eval_jaxpr/gather | solution.py:161
  91.1 3.1 %gather_fusion.5 = s32[512]{0:T(512)S(1)} fusion(s32[8192]{0:T(1024)S(1)} %copy-done.1, u32[1024]{0:T(1024)S(1)} %pad_clamp_fusion.8), kind=kCustom, calls=%fused_computation.5 | custom fusion | bytes 6144 | tf_op jit(solution)/shard_map/jit(searchsorted)/jit(_searchsorted_scan_impl)/vmap(jit(_searchsorted_scan_impl))/eval_jaxpr/gather | solution.py:161
  94.3 3.1 %gather_fusion.6 = s32[512]{0:T(512)S(1)} fusion(s32[8192]{0:T(1024)S(1)} %copy-done.1, u32[1024]{0:T(1024)S(1)} %pad_clamp_fusion.7), kind=kCustom, calls=%fused_computation.6 | custom fusion | bytes 6144 | tf_op jit(solution)/shard_map/jit(searchsorted)/jit(_searchsorted_scan_impl)/vmap(jit(_searchsorted_scan_impl))/eval_jaxpr/gather | solution.py:161
  97.5 3.1 %gather_fusion.7 = s32[512]{0:T(512)S(1)} fusion(s32[8192]{0:T(1024)S(1)} %copy-done.1, u32[1024]{0:T(1024)S(1)} %pad_clamp_fusion.6), kind=kCustom, calls=%fused_computation.7 | custom fusion | bytes 6144 | tf_op jit(solution)/shard_map/jit(searchsorted)/jit(_searchsorted_scan_impl)/vmap(jit(_searchsorted_scan_impl))/eval_jaxpr/gather | solution.py:161
  100.7 3.1 %gather_fusion.8 = s32[512]{0:T(512)S(1)} fusion(s32[8192]{0:T(1024)S(1)} %copy-done.1, u32[1024]{0:T(1024)S(1)} %pad_clamp_fusion.5), kind=kCustom, calls=%fused_computation.8 | custom fusion | bytes 6144 | tf_op jit(solution)/shard_map/jit(searchsorted)/jit(_searchsorted_scan_impl)/vmap(jit(_searchsorted_scan_impl))/eval_jaxpr/gather | solution.py:161
  103.9 3.1 %gather_fusion.9 = s32[512]{0:T(512)S(1)} fusion(s32[8192]{0:T(1024)S(1)} %copy-done.1, u32[1024]{0:T(1024)S(1)} %pad_clamp_fusion.4), kind=kCustom, calls=%fused_computation.9 | custom fusion | bytes 6144 | tf_op jit(solution)/shard_map/jit(searchsorted)/jit(_searchsorted_scan_impl)/vmap(jit(_searchsorted_scan_impl))/eval_jaxpr/gather | solution.py:161
  107.0 3.1 %gather_fusion.10 = s32[512]{0:T(512)S(1)} fusion(s32[8192]{0:T(1024)S(1)} %copy-done.1, u32[1024]{0:T(1024)S(1)} %pad_clamp_fusion.3), kind=kCustom, calls=%fused_computation.10 | custom fusion | bytes 6144 | tf_op jit(solution)/shard_map/jit(searchsorted)/jit(_searchsorted_scan_impl)/vmap(jit(_searchsorted_scan_impl))/eval_jaxpr/gather | solution.py:161
  110.2 3.1 %gather_fusion.11 = s32[512]{0:T(512)S(1)} fusion(s32[8192]{0:T(1024)S(1)} %copy-done.1, u32[1024]{0:T(1024)S(1)} %pad_clamp_fusion.2), kind=kCustom, calls=%fused_computation.11 | custom fusion | bytes 6144 | tf_op jit(solution)/shard_map/jit(searchsorted)/jit(_searchsorted_scan_impl)/vmap(jit(_searchsorted_scan_impl))/eval_jaxpr/gather | solution.py:161
  113.4 3.1 %gather_fusion.12 = s32[512]{0:T(512)S(1)} fusion(s32[8192]{0:T(1024)S(1)} %copy-done.1, u32[1024]{0:T(1024)S(1)} %pad_clamp_fusion.1), kind=kCustom, calls=%fused_computation.12 | custom fusion | bytes 6144 | tf_op jit(solution)/shard_map/jit(searchsorted)/jit(_searchsorted_scan_impl)/vmap(jit(_searchsorted_scan_impl))/eval_jaxpr/gather | solution.py:161
  116.6 3.1 %gather_fusion.13 = s32[512]{0:T(512)S(1)} fusion(s32[8192]{0:T(1024)S(1)} %copy-done.1, u32[1024]{0:T(1024)S(1)} %pad_clamp_fusion), kind=kCustom, calls=%fused_computation.13 | custom fusion | bytes 6144 | tf_op jit(solution)/shard_map/jit(searchsorted)/jit(_searchsorted_scan_impl)/vmap(jit(_searchsorted_scan_impl))/eval_jaxpr/gather | solution.py:161
  119.8 0.1 copy.28.low_ref
  119.9 0.1 slice_reduce_fusion.1.lo_ref
  120.0 0.2 copy.34
  120.2 27.1 %all-gather.5.cloned.1.call-done = bf16[8192,512]{1,0:T(8,128)(2,1)} async-done(((bf16[512,512]{1,0:T(8,128)(2,1)}), bf16[8192,512]{1,0:T(8,128)(2,1)}) %all-gather.5.cloned.1.call-update) | async-done | bytes 8388624 | tf_op jit(solution)/shard_map/all_gather | solution.py:159
  147.3 2.8 %constant_dynamic-slice_fusion.k_ref.v_ref = bf16[5120,512]{1,0:T(8,128)(2,1)S(1)} fusion(bf16[8192,512]{1,0:T(8,128)(2,1)} %all-gather.5.cloned.1.call-done, s32[]{:T(128)S(6)} %select_n.196), kind=kLoop, calls=%fused_computation.74 | loop fusion | bytes 10485764 | tf_op jit(solution)/shard_map/dynamic_slice | solution.py:160
  150.2 7.3 %shard_map.95 = bf16[2,512,128]{2,1,0:T(8,128)(2,1)S(1)} custom-call(s32[1]{0:T(128)} %bitcast.off_ref, s32[4]{0:T(128)S(1)} %slice_reduce_fusion.1.lo_ref, bf16[2,512,128]{2,1,0:T(8,128)(2,1)S(1)} %bitcast.48, bf16[5120,512]{1,0:T(8,128)(2,1)S(1)} %constant_dynamic-slice_fusion.k_ref.v_ref, bf16[5120,512]{1,0:T(8,128)(2,1)S(1)} %constant_dynamic-slice_fusion.k_ref.v_ref, ...), custom_call_target="tpu_custom_call" | custom-call | flops 4026531840 | bytes 5767168 | tf_op jit(solution)/shard_map/pallas_call | solution.py:70
  157.5 0.0 copy-start.4
  157.5 0.1 copy.29
  157.6 0.0 copy-done
  157.6 2.1 convolution_convert_fusion
  159.7 0.0 reduce-scatter.5.cloned.1.call-update
  159.7 0.0 copy-done.4
  159.8 1.2 reduce-window.6
  160.9 0.2 slice_reduce_fusion
  161.2 0.1 fusion.12
  161.3 0.8 fusion.6
  162.1 57.2 %all_to_all.5 = bf16[16,64,512]{2,1,0:T(8,128)(2,1)S(1)} all-to-all(bf16[16,64,512]{2,1,0:T(8,128)(2,1)S(1)} %bitcast.57), channel_id=1, replica_groups=mesh['tok'=16,'row'=4,'col'=2] {'tok'}, dimensions={0} | all-to-all | bytes 2097152 | tf_op jit(solution)/shard_map/all_to_all | solution.py:166
  219.3 1.1 reshape.70
  220.4 8.6 %reduce-scatter.5.cloned.1.call-done = bf16[64,2048]{1,0:T(8,128)(2,1)} async-done(((bf16[512,2048]{1,0:T(8,128)(2,1)}), bf16[64,2048]{1,0:T(8,128)(2,1)}) %reduce-scatter.5.cloned.1.call-update) | async-done | bytes 262160 | tf_op jit(solution)/shard_map/reduce_scatter | solution.py:168
  (36 shorter events, 0.4 us)
Async XLA Ops:
  7.2 150.5 %copy-start = (bf16[256,2048]{1,0:T(8,128)(2,1)S(1)}, bf16[256,2048]{1,0:T(8,128)(2,1)}, u32[]{:S(2)}) copy-start(bf16[256,2048]{1,0:T(8,128)(2,1)} %param.13) | copy-start | bytes 3145732
  7.2 35.8 %all-gather.3.cloned.1.call-start = ((), (), s32[]{:S(2)}) async-start(), calls=%async_computation.3 | async-start | bytes 2621440 | tf_op jit(solution)/shard_map/all_gather | solution.py:105
  7.9 10.8 %copy-start.5 = (bf16[2048]{0:T(1024)(128)(2,1)S(1)}, bf16[2048]{0:T(1024)(128)(2,1)}, u32[]{:S(2)}) copy-start(bf16[2048]{0:T(1024)(128)(2,1)} %param.9) | copy-start | bytes 12292
  7.9 10.7 %copy-start.3 = (bf16[128,4,3,128]{3,1,2,0:T(4,128)(2,1)S(1)}, bf16[128,4,3,128]{3,1,2,0:T(4,128)(2,1)}, u32[]{:S(2)}) copy-start(bf16[128,4,3,128]{3,1,2,0:T(4,128)(2,1)} %param.12) | copy-start | bytes 1179652
  7.9 64.1 %reduce-scatter.3.cloned.1.call-start = ((), (), s32[]{:S(2)}) async-start(), calls=%async_computation.4 | async-start | bytes 4718592 | tf_op jit(solution)/shard_map/reduce_scatter | solution.py:132
  47.5 6.4 %copy-start.2 = (bf16[512,2048]{1,0:T(8,128)(2,1)S(1)}, bf16[512,2048]{1,0:T(8,128)(2,1)}, u32[]{:S(2)}) copy-start(bf16[512,2048]{1,0:T(8,128)(2,1)} %all-gather.3.cloned.1.call-done) | copy-start | bytes 6291460
  47.5 6.4 %copy-start.6 = (bf16[2048,128]{1,0:T(8,128)(2,1)S(1)}, bf16[2048,128]{1,0:T(8,128)(2,1)}, u32[]{:S(2)}) copy-start(bf16[2048,128]{1,0:T(8,128)(2,1)} %param.11) | copy-start | bytes 1572868
  57.9 17.3 %copy-start.1 = (s32[8192]{0:T(1024)S(1)}, s32[8192]{0:T(1024)}, u32[]{:S(2)}) copy-start(s32[8192]{0:T(1024)} %param.14) | copy-start | bytes 98308
  57.9 89.4 %all-gather.5.cloned.1.call-start = ((), (), s32[]{:S(2)}) async-start(), calls=%async_computation.5 | async-start | bytes 8912896 | tf_op jit(solution)/shard_map/all_gather | solution.py:159
  74.9 154.1 %reduce-scatter.5.cloned.1.call-start = ((), (), s32[]{:S(2)}) async-start(), calls=%async_computation.6 | async-start | bytes 2359296 | tf_op jit(solution)/shard_map/reduce_scatter | solution.py:168
  157.5 2.3 copy-start.4
Sparse Core Ops, SparseCore 0:
  9.7 33.2 all-gather.2
  58.0 13.9 reduce-scatter.2
  75.0 72.2 all-gather.4
  159.9 69.0 reduce-scatter.4

commit v8 on v6

--- a/solution.py
+++ b/solution.py
@@ -13,24 +13,28 @@
 ADAPTER_RANK = 128
 MAXLEN = 4352
 
-def attend_kernel(offset_ref, q_ref, k_ref, v_ref, qseg_ref, kseg_ref, o_ref, *, scale, rows):
+
+def attend_kernel(offset_ref, q_ref, k_ref, v_ref, low_ref, o_ref, *, scale, rows):
     tile = pl.program_id(1)
     q = q_ref[0]
     k = k_ref[...]
     v = v_ref[...]
     count = k.shape[0]
-    score = lax.dot_general(q, k, (((1,), (1,)), ((), ())), preferred_element_type=jnp.float32) * scale
+    score = lax.dot_general(
+        q, k, (((1,), (1,)), ((), ())), preferred_element_type=jnp.float32
+    ) * scale
     key_pos = lax.broadcasted_iota(jnp.int32, (rows, count), 1)
-    query_pos = offset_ref[0] + tile * rows + lax.broadcasted_iota(jnp.int32, (rows, count), 0)
-    allowed = (qseg_ref[...] == kseg_ref[...]) & (key_pos <= query_pos)
+    query_pos = offset_ref[0] + tile * rows + lax.broadcasted_iota(jnp.int32, (rows, 1), 0)
+    allowed = (key_pos >= low_ref[...]) & (key_pos <= query_pos)
     masked = jnp.where(allowed, score, -1e30)
     top = jnp.max(masked, axis=1, keepdims=True)
-    weights = jnp.where(allowed, jnp.exp(score - top), 0.0).astype(jnp.bfloat16)
+    weights = jnp.exp(masked - top).astype(jnp.bfloat16)
     total = jnp.sum(weights.astype(jnp.float32), axis=1, keepdims=True)
     summed = jnp.dot(weights, v, preferred_element_type=jnp.float32)
     o_ref[0] = (summed / total).astype(o_ref.dtype)
 
-def attend(query, window_kv, own_seg, key_seg, offset, scale, rows=128):
+
+def attend(query, window_kv, low, offset, scale, rows=256):
     heads, tokens, _ = query.shape
     count = window_kv.shape[0]
     grid = (heads, tokens // rows)
@@ -47,13 +51,18 @@
                 pl.BlockSpec((count, HEAD_SIZE), lambda h, i, off: (0, 2 * h)),
                 pl.BlockSpec((count, HEAD_SIZE), lambda h, i, off: (0, 2 * h + 1)),
                 pl.BlockSpec((rows, 1), lambda h, i, off: (i, 0)),
-                pl.BlockSpec((1, count), lambda h, i, off: (0, 0)),
             ],
             out_specs=pl.BlockSpec((1, rows, HEAD_SIZE), lambda h, i, off: (h, i, 0)),
         ),
-        compiler_params=pltpu.CompilerParams(dimension_semantics=("arbitrary", "arbitrary"), vmem_limit_bytes=48 * 1024 * 1024),
-        cost_estimate=pl.CostEstimate(flops=flops, transcendentals=heads * tokens * count, bytes_accessed=2 * count * 512 + 4 * heads * tokens * HEAD_SIZE),
-    )(offset.reshape(1).astype(jnp.int32), query, window_kv, window_kv, own_seg.reshape(tokens, 1), key_seg.reshape(1, count))
+        compiler_params=pltpu.CompilerParams(
+            dimension_semantics=("arbitrary", "arbitrary"), vmem_limit_bytes=56 * 1024 * 1024
+        ),
+        cost_estimate=pl.CostEstimate(
+            flops=flops,
+            transcendentals=heads * tokens * count,
+            bytes_accessed=2 * count * 512 + 4 * heads * tokens * HEAD_SIZE,
+        ),
+    )(offset.reshape(1).astype(jnp.int32), query, window_kv, window_kv, low.reshape(tokens, 1))
 
 
 def shards_body(
@@ -106,7 +115,6 @@
     back = min(count_tok - 1, -(-(MAXLEN - 1) // tok_dev))
     window = (back + 1) * tok_dev
     first = jnp.clip(me - back, 0, count_tok - 1 - back) * tok_dev
-    key_seg = lax.dynamic_slice_in_dim(prompt_segment_index, first, window, 0)
     capacity = max(2, 2 * tok_dev // count_tok)
     owner = cache_owner_index[:, 0]
     onehot = (owner[:, None] == jnp.arange(count_tok, dtype=jnp.int32)[None, :]).astype(jnp.int32)
@@ -123,7 +131,10 @@
     ).astype(jnp.bfloat16).reshape(count_tok, capacity, heads_dev * 2 * HEAD_SIZE)
     gathered_all = lax.all_gather(kv_flat, "tok", axis=0, tiled=True)
     window_kv = lax.dynamic_slice_in_dim(gathered_all, first, window, 0)
-    attended = attend(query, window_kv, own_seg, key_seg, own_start - first, scale)
+    seg_start = jnp.sum(
+        (prompt_segment_index[None, :] < own_seg[:, None]).astype(jnp.int32), axis=1
+    )
+    attended = attend(query, window_kv, seg_start - first, own_start - first, scale)
     outgoing, _ = lax.optimization_barrier((outgoing, attended))
     received = lax.all_to_all(outgoing, "tok", split_axis=0, concat_axis=0, tiled=True)
     attended = jnp.transpose(attended, (1, 0, 2)).reshape(tok_dev, heads_dev * HEAD_SIZE)
@@ -137,6 +148,7 @@
     )
     kv_cache = received.reshape(count_tok * capacity, heads_dev, 2, HEAD_SIZE)
     return (block_output, kv_cache)
+
 
 def solution(mesh):
     placed = (

time: 211 us -> 213 us (level)
  local copies, waits for them, and re-layouts: 17.2 us -> 21.8 us
  waiting for transfers between devices: 119 us -> 116 us
    all_gather x1, waiting for transfers between devices: 71.9 us -> 68.4 us  [shards_body(): gathered_all = lax.all_gather(kv_flat, 'tok', axis=0, tiled=True)]
    dynamic_slice x1, local copies, waits for them, and re-layouts: 2.82 us -> 5.21 us  [shards_body(): window_kv = lax.dynamic_slice_in_dim(gathered_all, first, window, 0)]
  transfers between devices with their start and end apart: 4 -> 4, of which waited for: 4 -> 4; matrix products, arithmetic and copies ran while one was open for 7% -> 9% of each run, Pallas kernels for 0% -> 0%
where the time goes in v8:
time: 213 us
  waiting for transfers between devices  116 us (54%)
  blocking collectives  24.5 us (12%)
  local copies, waits for them, and re-layouts  21.8 us (10%)
  Pallas kernels  16.2 us (8%)
  between operations  13.9 us (7%)
  matrix products  13.2 us (6%)
  other arithmetic  6.91 us (3%)
    all_gather x1, waiting for transfers between devices, shards_body(): gathered_all = lax.all_gather(kv_flat, 'tok', axis=0, tiled=True)  68.4 us
    all_gather x1, waiting for transfers between devices, shards_body(): gathered = lax.all_gather(block_input_rows, 'row', axis=0, tiled=True)  23.9 us
    all_to_all x1, blocking collectives, shards_body(): lax.all_to_all(outgoing, 'tok', split_axis=0, concat_axis=0, tiled=True)  22 us
    pallas_call x1, Pallas kernels, attend(): pl.pallas_call(kernel, out_shape=jax.ShapeDtypeStruct((heads, tokens, HEA...  16.2 us
    reduce_scatter x1, waiting for transfers between devices, shards_body(): lax.psum_scatter(main + adapter_down_output, 'col', scatter_dimension=0,...  14.1 us
    unnamed x17, local copies, waits for them, and re-layouts  11.9 us
    reduce_scatter x1, waiting for transfers between devices, shards_body(): lax.psum_scatter(jnp.dot(attended, output_projection_weight, preferred_el...  8.57 us
    dot_general x1, matrix products, shards_body(): jnp.einsum('td,dhe->hte', normalized_input, flat_weight, preferred_elemen...  6.4 us
  transfers between devices with their start and end apart: 4, of which 4 were waited for; matrix products, arithmetic and copies ran while one was open for 9% of the time, Pallas kernels for 0%

profile of v8, /device:TPU:0, one launch (start us, length us, event | category | flops | bytes accessed | tf_op | source)
XLA Modules:
  0.0 212.5 jit_solution(616562237785585646)
XLA Ops:
  7.2 0.0 copy-start
  7.2 0.0 all-gather.3.cloned.1.call-start
  7.2 0.7 all-gather.3.cloned.1.call-update
  7.9 0.0 copy-start.4
  7.9 0.0 copy-start.2
  7.9 0.0 reduce-scatter.3.cloned.1.call-start
  8.0 10.7 %copy.21 = bf16[2048,4,3,128]{0,3,2,1:T(8,128)(2,1)} copy(bf16[2048,4,3,128]{3,1,2,0:T(4,128)(2,1)} %param.10) | data formatting | bytes 12582912 | tf_op args[2]
  18.7 0.0 copy-done.4
  18.7 0.0 copy-done.2
  18.7 0.3 copy.23
  19.0 23.9 %all-gather.3.cloned.1.call-done = bf16[512,2048]{1,0:T(8,128)(2,1)} async-done(((bf16[128,2048]{1,0:T(8,128)(2,1)}), bf16[512,2048]{1,0:T(8,128)(2,1)}) %all-gather.3.cloned.1.call-update) | async-done | bytes 2097168 | tf_op jit(solution)/shard_map/all_gather | solution.py:78
  43.0 2.1 fusion
  45.0 2.5 %psum.7 = f32[512]{0:T(512)S(1)} all-reduce(f32[512]{0:T(512)S(1)} %fusion), channel_id=1, replica_groups=mesh['tok'=16,'row'=4,'col'=2] {'col'}, use_global_device_ids=true, to_apply=%region_1.0 | all-reduce | flops 512 | bytes 4096 | tf_op jit(solution)/shard_map/psum | solution.py:81
  47.5 0.0 copy-start.1
  47.5 0.0 copy-start.6
  47.5 6.4 %fusion.3 = f32[512,4,384]{2,0,1:T(8,128)S(1)} fusion(bf16[2048,4,384]{0,2,1:T(8,128)(2,1)} %bitcast.47, bf16[512,2048]{1,0:T(8,128)(2,1)} %all-gather.3.cloned.1.call-done, f32[2048]{0:T(1024)S(1)} %convert_element_type.31, f32[512]{0:T(512)S(1)} %add_rsqrt_fusion), kind=kOutput, calls=%fused_computation.8 | convolution fusion | flops 3225419776 | bytes 11544576 | tf_op jit(solution)/shard_map/td,dhe->hte/dot_general | solution.py:96
  53.9 0.0 copy-done.1
  53.9 0.0 copy-done.6
  54.0 0.8 convolution_bitcast_fusion
  54.7 3.2 %add_bitcast_fusion = f32[4,512,384]{2,1,0:T(8,128)} fusion(f32[512,4,384]{2,0,1:T(8,128)S(1)} %fusion.3, f32[512,128,1]{1,0,2:T(8,128)S(1)} %convolution_bitcast_fusion, bf16[128,4,384]{0,2,1:T(8,128)(2,1)S(1)} %bitcast.53), kind=kOutput, calls=%fused_computation.6 | convolution fusion | flops 1208745984 | bytes 6946816 | tf_op jit(solution)/shard_map/tr,rhe->hte/dot_general | solution.py:99
  57.9 0.0 copy-start.5
  57.9 0.0 reduce-scatter.3.cloned.1.call-update
  57.9 0.0 all-gather.5.cloned.1.call-start
  58.0 14.1 %reduce-scatter.3.cloned.1.call-done = f32[2,512,384]{2,1,0:T(8,128)} async-done(((f32[4,512,384]{2,1,0:T(8,128)}), f32[2,512,384]{2,1,0:T(8,128)}) %reduce-scatter.3.cloned.1.call-update) | async-done | bytes 1572880 | tf_op jit(solution)/shard_map/reduce_scatter | solution.py:105
  72.0 1.5 convert_element_type.33
  73.5 0.3 copy.25
  73.9 1.0 copy.33
  74.9 0.0 all-gather.5.cloned.1.call-update
  74.9 0.2 reduce-scatter.5.cloned.1.call-start
  75.1 0.0 copy-done.5
  75.1 0.1 dynamic_slice.7
  75.2 2.0 convert_reduce_fusion
  77.3 0.9 copy.28.low_ref
  78.1 0.8 copy.34
  79.0 68.4 %all-gather.5.cloned.1.call-done = bf16[8192,512]{1,0:T(8,128)(2,1)} async-done(((bf16[512,512]{1,0:T(8,128)(2,1)}), bf16[8192,512]{1,0:T(8,128)(2,1)}) %all-gather.5.cloned.1.call-update) | async-done | bytes 8388624 | tf_op jit(solution)/shard_map/all_gather | solution.py:132
  147.4 5.2 %constant_dynamic-slice_fusion.k_ref.v_ref = bf16[5120,512]{1,0:T(8,128)(2,1)} fusion(bf16[8192,512]{1,0:T(8,128)(2,1)} %all-gather.5.cloned.1.call-done, s32[]{:T(128)S(6)} %select_n.6), kind=kLoop, calls=%fused_computation.27 | loop fusion | bytes 10485764 | tf_op jit(solution)/shard_map/dynamic_slice | solution.py:133
  152.6 16.2 %shard_map.95 = bf16[2,512,128]{2,1,0:T(8,128)(2,1)} custom-call(s32[1]{0:T(128)} %bitcast.offset_ref, bf16[2,512,128]{2,1,0:T(8,128)(2,1)} %bitcast.54, bf16[5120,512]{1,0:T(8,128)(2,1)} %constant_dynamic-slice_fusion.k_ref.v_ref, bf16[5120,512]{1,0:T(8,128)(2,1)} %constant_dynamic-slice_fusion.k_ref.v_ref, s32[512,1]{1,0:T(8,128)} %copy.28.low_ref), custom_call_target="tpu_custom_call" | custom-call | flops 2684354560 | bytes 5767168 | tf_op jit(solution)/shard_map/pallas_call | solution.py:43
  168.8 0.0 copy-start.3
  168.8 1.1 copy.29
  169.9 0.0 copy-done
  169.9 2.1 convolution_convert_fusion
  172.0 0.0 reduce-scatter.5.cloned.1.call-update
  172.0 0.0 copy-done.3
  172.1 1.2 reduce-window.6
  173.2 0.2 slice_reduce_fusion
  173.5 0.1 fusion.12
  173.6 0.8 fusion.6
  174.3 22.0 %all_to_all.5 = bf16[16,64,512]{2,1,0:T(8,128)(2,1)S(1)} all-to-all(bf16[16,64,512]{2,1,0:T(8,128)(2,1)S(1)} %bitcast.56), channel_id=1, replica_groups=mesh['tok'=16,'row'=4,'col'=2] {'tok'}, dimensions={0} | all-to-all | bytes 2097152 | tf_op jit(solution)/shard_map/all_to_all | solution.py:139
  196.3 1.1 reshape.74
  197.4 8.6 %reduce-scatter.5.cloned.1.call-done = bf16[64,2048]{1,0:T(8,128)(2,1)} async-done(((bf16[512,2048]{1,0:T(8,128)(2,1)}), bf16[64,2048]{1,0:T(8,128)(2,1)}) %reduce-scatter.5.cloned.1.call-update) | async-done | bytes 262160 | tf_op jit(solution)/shard_map/reduce_scatter | solution.py:141
  (9 shorter events, 0.1 us)
Async XLA Ops:
  7.2 162.8 %copy-start = (bf16[256,2048]{1,0:T(8,128)(2,1)S(1)}, bf16[256,2048]{1,0:T(8,128)(2,1)}, u32[]{:S(2)}) copy-start(bf16[256,2048]{1,0:T(8,128)(2,1)} %param.13) | copy-start | bytes 3145732
  7.2 35.8 %all-gather.3.cloned.1.call-start = ((), (), s32[]{:S(2)}) async-start(), calls=%async_computation.3 | async-start | bytes 2621440 | tf_op jit(solution)/shard_map/all_gather | solution.py:78
  7.9 10.8 %copy-start.4 = (bf16[2048]{0:T(1024)(128)(2,1)S(1)}, bf16[2048]{0:T(1024)(128)(2,1)}, u32[]{:S(2)}) copy-start(bf16[2048]{0:T(1024)(128)(2,1)} %param.9) | copy-start | bytes 12292
  7.9 10.8 %copy-start.2 = (bf16[128,4,3,128]{3,1,2,0:T(4,128)(2,1)S(1)}, bf16[128,4,3,128]{3,1,2,0:T(4,128)(2,1)}, u32[]{:S(2)}) copy-start(bf16[128,4,3,128]{3,1,2,0:T(4,128)(2,1)} %param.12) | copy-start | bytes 1179652
  7.9 64.1 %reduce-scatter.3.cloned.1.call-start = ((), (), s32[]{:S(2)}) async-start(), calls=%async_computation.4 | async-start | bytes 4718592 | tf_op jit(solution)/shard_map/reduce_scatter | solution.py:105
  47.5 6.4 %copy-start.1 = (bf16[512,2048]{1,0:T(8,128)(2,1)S(1)}, bf16[512,2048]{1,0:T(8,128)(2,1)}, u32[]{:S(2)}) copy-start(bf16[512,2048]{1,0:T(8,128)(2,1)} %all-gather.3.cloned.1.call-done) | copy-start | bytes 6291460
  47.5 6.4 %copy-start.6 = (bf16[2048,128]{1,0:T(8,128)(2,1)S(1)}, bf16[2048,128]{1,0:T(8,128)(2,1)}, u32[]{:S(2)}) copy-start(bf16[2048,128]{1,0:T(8,128)(2,1)} %param.11) | copy-start | bytes 1572868
  57.9 17.2 %copy-start.5 = (s32[8192]{0:T(1024)S(1)}, s32[8192]{0:T(1024)}, u32[]{:S(2)}) copy-start(s32[8192]{0:T(1024)} %param.14) | copy-start | bytes 98308
  57.9 89.4 %all-gather.5.cloned.1.call-start = ((), (), s32[]{:S(2)}) async-start(), calls=%async_computation.5 | async-start | bytes 8912896 | tf_op jit(solution)/shard_map/all_gather | solution.py:132
  74.9 131.1 %reduce-scatter.5.cloned.1.call-start = ((), (), s32[]{:S(2)}) async-start(), calls=%async_computation.6 | async-start | bytes 2359296 | tf_op jit(solution)/shard_map/reduce_scatter | solution.py:141
  168.8 3.2 %copy-start.3 = (s32[512,1]{0,1:T(1,128)S(1)}, s32[512,1]{0,1:T(1,128)}, u32[]{:S(2)}) copy-start(s32[512,1]{0,1:T(1,128)} %param.15) | copy-start | bytes 6148
Sparse Core Ops, SparseCore 0:
  9.7 33.2 all-gather.2
  58.0 13.9 reduce-scatter.2
  75.0 72.2 all-gather.4
  172.2 33.8 reduce-scatter.4
